TPU v7x, 256 devices: a whole 4x4x8 slice. The times are simulated.
256 devices in a mesh: kv: 8 (over y, core), blk: 32 (over x, z).
Axes of the slice: x: 4, y: 4, z: 8, core: 2. Of those that a mesh axis runs over, the one named last changes fastest.
Arguments:
- queries: bfloat16 [256, 8192], P('blk', 'kv'), may hold values from -40 to 40
- draft_token_keys: bfloat16 [256, 1024], P('blk', 'kv'), may hold values from -15 to 15
- draft_token_values: bfloat16 [256, 1024], P('blk', 'kv'), may hold values from -6 to 6
- cached_key_vectors: bfloat16 [4, 4096, 1024], P(None, 'blk', 'kv'), may hold values from -40 to 40
- cached_value_vectors: bfloat16 [4, 4096, 1024], P(None, 'blk', 'kv'), may hold values from -6 to 6
- out_weight: bfloat16 [8192, 8192], P('kv', 'blk'), may hold values from -0.5 to 0.5
- lengths: int32 [4], replicated, may hold values from 256 to 4088, as said below
- parents: int32 [4, 64], replicated, may hold values from 0 to 62, as said below
- accepted_nodes: int32 [4, 8], replicated, may hold values from 0 to 62, as said below
- accepted_count: int32 [4], replicated, may hold values from 1 to 8, as said below
Outputs:
- projected: bfloat16 [256, 8192], P('kv', 'blk')
- new_cache_keys: bfloat16 [4, 4096, 1024], P(None, 'blk', 'kv')
- new_cache_values: bfloat16 [4, 4096, 1024], P(None, 'blk', 'kv')
Inputs may be any that keep to these rules, and one draw needn't show every extreme that they name: `lengths`: some request has exactly 4088, some exactly 256. parents[r, 0] = 0 and parents[r, i] < i for i >= 1. accepted_nodes[r, 0] = 0 and accepted_nodes[r, k] is a child of accepted_nodes[r, k - 1] in request r's tree; only the first accepted_count[r] entries are used. `accepted_count`: some request has exactly 8, some exactly 1.
All inputs are finite; a program needn't handle non-finite values.
Results may differ from a plain program's by a relative error of at most 0.0055.
Values may be sent and summed in bfloat16 or wider, within the bound.
No kernel may reach another device: no remote copies, remote signals or barrier semaphores. Data moves between devices by JAX's collectives and lax.ppermute only.
A program may use at most 64 MiB of HBM per device.

v0:
```python
import math

import jax
import jax.numpy as jnp
from jax import lax
from jax.sharding import PartitionSpec as P

HEAD_SIZE = 128
TREE_TOKENS = 64
ACC = 8


NEG_FLOOR = -1e30


def ancestors(parent_rows):
    node_ids = jnp.arange(TREE_TOKENS, dtype=jnp.int32)
    parent_link = (
        (parent_rows[:, :, None] == node_ids[None, None, :]) & (node_ids[None, :, None] >= 1)
    ).astype(jnp.float32)
    reachable = jnp.eye(TREE_TOKENS, dtype=jnp.float32)[None] + parent_link
    for doubling in range((TREE_TOKENS - 1).bit_length()):
        reachable = jnp.minimum(
            reachable
            + jnp.einsum("rij,rjk->rik", reachable, reachable, precision=lax.Precision.HIGHEST),
            1.0,
        )
    return reachable


def partial_softmax(query_vectors, key_rows, value_rows, usable, score_scale):
    scores = (
        jnp.einsum(
            "rtkgh,rbpkh->brkgtp", query_vectors, key_rows, preferred_element_type=jnp.float32
        )
        * score_scale
    )
    scores = jnp.where(usable, scores, NEG_FLOOR)
    peak_score = jnp.max(scores, axis=-1)
    weights = jnp.where(usable, jnp.exp(scores - peak_score[..., None]), 0.0)
    weight_sum = jnp.sum(weights, axis=-1)
    weighted = jnp.einsum(
        "brkgtp,rbpkh->brtkgh",
        weights.astype(jnp.bfloat16),
        value_rows,
        preferred_element_type=jnp.float32,
    )
    block_count, req_count, kv_count, query_group_width, row_count = peak_score.shape
    weighted = weighted.reshape(
        block_count, req_count * row_count, kv_count * query_group_width * value_rows.shape[-1]
    )
    peak_score = peak_score.transpose(0, 1, 4, 2, 3).reshape(
        block_count, req_count * row_count, kv_count * query_group_width
    )
    weight_sum = weight_sum.transpose(0, 1, 4, 2, 3).reshape(
        block_count, req_count * row_count, kv_count * query_group_width
    )
    return (weighted, peak_score, weight_sum)


def merge_parts(cache_part, draft_part, head_dim):
    cache_out, cache_peak, cache_sum = cache_part
    draft_out, draft_peak, draft_sum = draft_part
    cache_out = cache_out.astype(jnp.float32)
    overall = jnp.maximum(jnp.max(cache_peak, axis=0), draft_peak[0])
    cache_factor = jnp.exp(cache_peak - overall[None])
    draft_factor = jnp.exp(draft_peak[0] - overall)
    denominator = jnp.sum(cache_factor * cache_sum, axis=0) + draft_factor * draft_sum[0]
    block_count, row_count, head_count = cache_peak.shape
    numerator = jnp.sum(
        cache_factor[..., None] * cache_out.reshape(block_count, row_count, head_count, head_dim),
        axis=0,
    )
    numerator = numerator + draft_factor[..., None] * draft_out[0].reshape(
        row_count, head_count, head_dim
    )
    return (
        (numerator / denominator[..., None])
        .reshape(row_count, head_count * head_dim)
        .astype(jnp.bfloat16)
    )


def place_rows(sources, slot_index, written, cache_rows):
    slot_ids = jnp.arange(sources.shape[1], dtype=jnp.int32)
    selector = ((slot_index[:, :, None] == slot_ids[None, None, :]) & written[:, :, None]).astype(
        jnp.bfloat16
    )
    placed = jnp.einsum(
        "rps,rsc->rpc", selector, sources, preferred_element_type=jnp.float32
    ).astype(jnp.bfloat16)
    return jnp.where(written[:, :, None], placed, cache_rows)


def on_device(
    queries,
    draft_token_keys,
    draft_token_values,
    cached_key_vectors,
    cached_value_vectors,
    out_weight,
    lengths,
    parents,
    accepted_nodes,
    accepted_count,
):
    block_count = lax.axis_size("blk")
    my_block = lax.axis_index("blk")
    rows_dev, width_q = queries.shape
    requests = lengths.shape[0]
    cache_width = cached_key_vectors.shape[2]
    kv_local = cache_width // HEAD_SIZE
    query_group_width = width_q // (kv_local * HEAD_SIZE)
    block_len = cached_key_vectors.shape[1]
    score_scale = 1.0 / math.sqrt(HEAD_SIZE)
    leading_row = my_block * rows_dev
    my_request = leading_row // TREE_TOKENS
    node_start = leading_row - my_request * TREE_TOKENS
    local_queries = queries.reshape(1, rows_dev, kv_local, query_group_width, HEAD_SIZE)
    gathered_keys, gathered_values = (
        lax.all_gather(draft_token_keys, "blk", axis=0, tiled=True),
        lax.all_gather(draft_token_values, "blk", axis=0, tiled=True),
    )
    tree_keys = lax.dynamic_slice_in_dim(
        gathered_keys, my_request * TREE_TOKENS, TREE_TOKENS, 0
    ).reshape(1, 1, TREE_TOKENS, kv_local, HEAD_SIZE)
    tree_values = lax.dynamic_slice_in_dim(
        gathered_values, my_request * TREE_TOKENS, TREE_TOKENS, 0
    ).reshape(1, 1, TREE_TOKENS, kv_local, HEAD_SIZE)
    reachable = ancestors(lax.dynamic_slice_in_dim(parents, my_request, 1, 0))
    own_reach = lax.dynamic_slice_in_dim(reachable, node_start, rows_dev, 1)
    draft_usable = (own_reach > 0.5)[None, :, None, None, :, :]
    draft_part = partial_softmax(local_queries, tree_keys, tree_values, draft_usable, score_scale)
    every_query = lax.all_gather(queries, "blk", axis=0, tiled=True)
    all_queries = every_query.reshape(requests, TREE_TOKENS, kv_local, query_group_width, HEAD_SIZE)
    positions = my_block * block_len + jnp.arange(block_len, dtype=jnp.int32)
    usable = (positions[None, :] < lengths[:, None])[None, :, None, None, None, :]
    local_out, local_peak, local_sum = partial_softmax(
        all_queries,
        cached_key_vectors.reshape(requests, 1, block_len, kv_local, HEAD_SIZE),
        cached_value_vectors.reshape(requests, 1, block_len, kv_local, HEAD_SIZE),
        usable,
        score_scale,
    )
    moved_out = lax.all_to_all(
        local_out[0].astype(jnp.bfloat16), "blk", split_axis=0, concat_axis=0, tiled=True
    )
    moved_peak, moved_sum = (
        lax.all_to_all(local_peak[0], "blk", split_axis=0, concat_axis=0, tiled=True),
        lax.all_to_all(local_sum[0], "blk", split_axis=0, concat_axis=0, tiled=True),
    )
    cache_part = (
        moved_out.reshape(block_count, rows_dev, -1),
        moved_peak.reshape(block_count, rows_dev, -1),
        moved_sum.reshape(block_count, rows_dev, -1),
    )
    attention = merge_parts(cache_part, draft_part, HEAD_SIZE)
    every_row = lax.all_gather(attention, "blk", axis=0, tiled=True)
    projected = lax.psum_scatter(
        jnp.dot(every_row, out_weight, preferred_element_type=jnp.float32),
        "kv",
        scatter_dimension=0,
        tiled=True,
    ).astype(jnp.bfloat16)
    positions_here = my_block * block_len + jnp.arange(block_len, dtype=jnp.int32)
    offset = positions_here[None, :] - lengths[:, None]
    written = (offset >= 0) & (offset < accepted_count[:, None])
    slot_match = offset[:, :, None] == jnp.arange(ACC, dtype=jnp.int32)[None, None, :]
    node_ids = jnp.sum(jnp.where(slot_match, accepted_nodes[:, None, :], 0), axis=-1)
    new_cache_keys = place_rows(
        gathered_keys.reshape(requests, TREE_TOKENS, cache_width),
        node_ids,
        written,
        cached_key_vectors,
    )
    new_cache_values = place_rows(
        gathered_values.reshape(requests, TREE_TOKENS, cache_width),
        node_ids,
        written,
        cached_value_vectors,
    )
    return (projected, new_cache_keys, new_cache_values)


def solution(mesh):
    return jax.shard_map(
        on_device,
        mesh=mesh,
        in_specs=(
            P("blk", "kv"),
            P("blk", "kv"),
            P("blk", "kv"),
            P(None, "blk", "kv"),
            P(None, "blk", "kv"),
            P("kv", "blk"),
            P(),
            P(),
            P(),
            P(),
        ),
        out_specs=(P("kv", "blk"), P(None, "blk", "kv"), P(None, "blk", "kv")),
        check_vma=False,
    )
```

profile of v0, /device:TPU:1, one launch (start us, length us, event | category | flops | bytes accessed | tf_op | source)
XLA Modules:
  0.0 281.8 jit_solution(6626827668490179836)
XLA Ops:
  7.2 41.5 %all_gather.12 = bf16[256,1024]{1,0:T(8,128)(2,1)S(1)} all-gather(bf16[8,1024]{1,0:T(8,128)(2,1)} %param.10), channel_id=1, replica_groups=mesh['kv'=8,'blk'=32] {'blk'}, dimensions={0}, use_global_device_ids=true | all-gather | bytes 540672 | tf_op jit(solution)/shard_map/all_gather | solution.py:134
  48.9 0.5 copy-done.6
  49.5 0.2 copy-done.8
  49.7 0.5 fusion.53
  50.3 0.7 copy.63
  51.1 5.7 %all-to-all-start = ((f32[32,8,8]{1,2,0:T(8,128)}), f32[32,8,8]{1,2,0:T(8,128)S(1)}, u32[]{:S(2)}, u32[]{:S(2)}) async-start(f32[32,8,8]{1,2,0:T(8,128)} %copy.63), calls=%async_computation | async-start | bytes 262144 | tf_op jit(solution)/shard_map/all_to_all | solution.py:149
  56.8 0.7 fusion.51
  57.5 0.2 fusion.35
  57.7 0.2 fusion.14
  58.2 0.2 fusion.8
  58.7 0.6 fusion.18
  59.4 0.2 copy-done.1
  59.6 0.5 fusion.3
  60.3 0.7 copy.73
  61.0 0.3 copy.69
  61.3 1.0 convert_element_type.101
  62.4 3.6 %all-to-all-done = f32[32,8,8]{1,2,0:T(8,128)S(1)} async-done(((f32[32,8,8]{1,2,0:T(8,128)}), f32[32,8,8]{1,2,0:T(8,128)S(1)}, u32[]{:S(2)}, u32[]{:S(2)}) %all-to-all-start) | async-done | bytes 8224 | tf_op jit(solution)/shard_map/all_to_all | solution.py:149
  66.0 5.7 %all-to-all-start.2 = ((f32[32,8,8]{1,2,0:T(8,128)}), f32[32,8,8]{1,2,0:T(8,128)S(1)}, u32[]{:S(2)}, u32[]{:S(2)}) async-start(f32[32,8,8]{1,2,0:T(8,128)} %copy.73), calls=%async_computation.2 | async-start | bytes 262144 | tf_op jit(solution)/shard_map/all_to_all | solution.py:150
  71.7 38.3 %all_gather.13 = bf16[256,128]{1,0:T(8,128)(2,1)S(1)} all-gather(bf16[8,128]{1,0:T(8,128)(2,1)S(1)} %copy-done.3), channel_id=1, replica_groups=mesh['kv'=8,'blk'=32] {'blk'}, dimensions={0}, use_global_device_ids=true | all-gather | bytes 67584 | tf_op jit(solution)/shard_map/all_gather | solution.py:121
  110.0 6.1 %all-to-all-start.1 = ((bf16[32,8,1024]{2,1,0:T(8,128)(2,1)}), bf16[32,8,1024]{2,1,0:T(8,128)(2,1)S(1)}, u32[]{:S(2)}, u32[]{:S(2)}) async-start(bf16[32,8,1024]{2,1,0:T(8,128)(2,1)} %convert_element_type.101), calls=%async_computation.1 | async-start | bytes 1048576 | tf_op jit(solution)/shard_map/all_to_all | solution.py:145
  116.2 0.2 fusion.54
  116.4 0.2 fusion.37
  116.7 0.6 copy-done.4
  117.4 40.3 %all_gather.14 = bf16[256,128]{1,0:T(8,128)(2,1)S(1)} all-gather(bf16[8,128]{1,0:T(8,128)(2,1)S(1)} %copy-done.4), channel_id=1, replica_groups=mesh['kv'=8,'blk'=32] {'blk'}, dimensions={0}, use_global_device_ids=true | all-gather | bytes 67584 | tf_op jit(solution)/shard_map/all_gather | solution.py:122
  157.9 0.3 fusion.17
  158.3 36.0 %all_gather.15 = bf16[256,1024]{1,0:T(8,128)(2,1)S(1)} all-gather(bf16[8,1024]{1,0:T(8,128)(2,1)S(1)} %fusion.15), channel_id=1, replica_groups=mesh['kv'=8,'blk'=32] {'blk'}, dimensions={0}, use_global_device_ids=true | all-gather | bytes 540672 | tf_op jit(solution)/shard_map/all_gather | solution.py:158
  194.4 1.0 fusion.56
  195.4 0.7 copy-done.5
  196.1 0.9 fusion.4
  197.1 0.9 fusion.5
  198.0 75.7 %reduce-scatter.2.cloned.1.call-done = f32[32,256]{1,0:T(8,128)} async-done(((f32[256,256]{1,0:T(8,128)}), f32[32,256]{1,0:T(8,128)}) %reduce-scatter.2.cloned.1.call-update) | async-done | bytes 32784 | tf_op jit(solution)/shard_map/reduce_scatter | solution.py:159
  273.6 1.4 convert_element_type.105
  (39 shorter events, 1.7 us)
Async XLA Ops:
  7.2 187.2 %copy-start = (bf16[1024,256]{1,0:T(8,128)(2,1)S(1)}, bf16[1024,256]{1,0:T(8,128)(2,1)}, u32[]{:S(2)}) copy-start(bf16[1024,256]{1,0:T(8,128)(2,1)} %param.15) | copy-start | bytes 1572868
  48.7 0.7 copy-start.6
  48.7 0.7 copy-start.7
  48.7 0.9 copy-start.8
  51.1 14.9 %all-to-all-start = ((f32[32,8,8]{1,2,0:T(8,128)}), f32[32,8,8]{1,2,0:T(8,128)S(1)}, u32[]{:S(2)}, u32[]{:S(2)}) async-start(f32[32,8,8]{1,2,0:T(8,128)} %copy.63), calls=%async_computation | async-start | bytes 262144 | tf_op jit(solution)/shard_map/all_to_all | solution.py:149
  58.7 0.9 copy-start.1
  62.4 9.4 %copy-start.3 = (bf16[8,128]{1,0:T(8,128)(2,1)S(1)}, bf16[8,128]{1,0:T(8,128)(2,1)}, u32[]{:S(2)}) copy-start(bf16[8,128]{1,0:T(8,128)(2,1)} %param.11) | copy-start | bytes 6148
  66.0 44.1 %all-to-all-start.2 = ((f32[32,8,8]{1,2,0:T(8,128)}), f32[32,8,8]{1,2,0:T(8,128)S(1)}, u32[]{:S(2)}, u32[]{:S(2)}) async-start(f32[32,8,8]{1,2,0:T(8,128)} %copy.73), calls=%async_computation.2 | async-start | bytes 262144 | tf_op jit(solution)/shard_map/all_to_all | solution.py:150
  110.0 6.2 %copy-start.2 = (bf16[8,1024]{1,0:T(8,128)(2,1)S(1)}, bf16[8,1024]{1,0:T(8,128)(2,1)}, u32[]{:S(2)}) copy-start(bf16[8,1024]{1,0:T(8,128)(2,1)} %param.10) | copy-start | bytes 49156
  110.0 47.8 %all-to-all-start.1 = ((bf16[32,8,1024]{2,1,0:T(8,128)(2,1)}), bf16[32,8,1024]{2,1,0:T(8,128)(2,1)S(1)}, u32[]{:S(2)}, u32[]{:S(2)}) async-start(bf16[32,8,1024]{2,1,0:T(8,128)(2,1)} %convert_element_type.101), calls=%async_computation.1 | async-start | bytes 1048576 | tf_op jit(solution)/shard_map/all_to_all | solution.py:145
  116.1 157.5 %reduce-scatter.2.cloned.1.call-start = ((), (), s32[]{:S(2)}) async-start(), calls=%async_computation.4 | async-start | bytes 294912 | tf_op jit(solution)/shard_map/reduce_scatter | solution.py:159
  116.7 0.7 copy-start.4
  195.4 0.7 copy-start.5
Sparse Core Ops, SparseCore 0:
  195.5 78.0 reduce-scatter.1
where the time goes:
time: 284 us; the launch traced here: 282 us
  blocking collectives  156 us (55%)
  waiting for transfers between devices  79.3 us (28%)
  starting transfers between devices  17.6 us (6%)
  between operations  14.3 us (5%)
  local copies, waits for them, and re-layouts  6.25 us (2%)
  matrix products  5.14 us (2%)
  other arithmetic  3.09 us (1%)
    reduce_scatter x1, waiting for transfers between devices, on_device(): lax.psum_scatter(jnp.dot(every_row, out_weight, preferred_element_type=jn...  75.7 us
    all_gather x1, blocking collectives, on_device(): every_query = lax.all_gather(queries, 'blk', axis=0, tiled=True)  41.5 us
    all_gather x1, blocking collectives, on_device(): lax.all_gather(draft_token_values, 'blk', axis=0, tiled=True)  40.3 us
    all_gather x1, blocking collectives, on_device(): lax.all_gather(draft_token_keys, 'blk', axis=0, tiled=True)  38.3 us
    all_gather x1, blocking collectives, on_device(): every_row = lax.all_gather(attention, 'blk', axis=0, tiled=True)  36 us
    all_to_all x1, starting transfers between devices, on_device(): lax.all_to_all(local_out[0].astype(jnp.bfloat16), 'blk', split_axis=0, co...  6.1 us
    all_to_all x1, starting transfers between devices, on_device(): lax.all_to_all(local_sum[0], 'blk', split_axis=0, concat_axis=0, tiled=True)  5.74 us
    all_to_all x1, starting transfers between devices, on_device(): lax.all_to_all(local_peak[0], 'blk', split_axis=0, concat_axis=0, tiled=T...  5.68 us
  transfers between devices with their start and end apart: 4, of which 2 were waited for; matrix products, arithmetic and copies ran while one was open for 3% of the time, Pallas kernels for 0%

commit v1 on v0

--- a/solution.py
+++ b/solution.py
@@ -92,6 +92,13 @@
     return jnp.where(written[:, :, None], placed, cache_rows)
 
 
+def gather_rows(block, axis_name):
+    count = lax.axis_size(axis_name)
+    spread = jnp.broadcast_to(block[None], (count,) + block.shape)
+    moved = lax.all_to_all(spread, axis_name, split_axis=0, concat_axis=0, tiled=True)
+    return moved.reshape((count * block.shape[0],) + block.shape[1:])
+
+
 def on_device(
     queries,
     draft_token_keys,
@@ -105,6 +112,7 @@
     accepted_count,
 ):
     block_count = lax.axis_size("blk")
+    kv_count = lax.axis_size("kv")
     my_block = lax.axis_index("blk")
     rows_dev, width_q = queries.shape
     requests = lengths.shape[0]
@@ -117,10 +125,12 @@
     my_request = leading_row // TREE_TOKENS
     node_start = leading_row - my_request * TREE_TOKENS
     local_queries = queries.reshape(1, rows_dev, kv_local, query_group_width, HEAD_SIZE)
-    gathered_keys, gathered_values = (
-        lax.all_gather(draft_token_keys, "blk", axis=0, tiled=True),
-        lax.all_gather(draft_token_values, "blk", axis=0, tiled=True),
-    )
+    packed = gather_rows(
+        jnp.concatenate([queries, draft_token_keys, draft_token_values], axis=1), "blk"
+    )
+    every_query = packed[:, :width_q]
+    gathered_keys = packed[:, width_q : width_q + cache_width]
+    gathered_values = packed[:, width_q + cache_width :]
     tree_keys = lax.dynamic_slice_in_dim(
         gathered_keys, my_request * TREE_TOKENS, TREE_TOKENS, 0
     ).reshape(1, 1, TREE_TOKENS, kv_local, HEAD_SIZE)
@@ -131,7 +141,6 @@
     own_reach = lax.dynamic_slice_in_dim(reachable, node_start, rows_dev, 1)
     draft_usable = (own_reach > 0.5)[None, :, None, None, :, :]
     draft_part = partial_softmax(local_queries, tree_keys, tree_values, draft_usable, score_scale)
-    every_query = lax.all_gather(queries, "blk", axis=0, tiled=True)
     all_queries = every_query.reshape(requests, TREE_TOKENS, kv_local, query_group_width, HEAD_SIZE)
     positions = my_block * block_len + jnp.arange(block_len, dtype=jnp.int32)
     usable = (positions[None, :] < lengths[:, None])[None, :, None, None, None, :]
@@ -145,23 +154,31 @@
     moved_out = lax.all_to_all(
         local_out[0].astype(jnp.bfloat16), "blk", split_axis=0, concat_axis=0, tiled=True
     )
-    moved_peak, moved_sum = (
-        lax.all_to_all(local_peak[0], "blk", split_axis=0, concat_axis=0, tiled=True),
-        lax.all_to_all(local_sum[0], "blk", split_axis=0, concat_axis=0, tiled=True),
-    )
+    head_count = local_peak.shape[-1]
+    moved_stats = lax.all_to_all(
+        jnp.concatenate([local_peak[0], local_sum[0]], axis=1),
+        "blk",
+        split_axis=0,
+        concat_axis=0,
+        tiled=True,
+    ).reshape(block_count, rows_dev, 2 * head_count)
     cache_part = (
         moved_out.reshape(block_count, rows_dev, -1),
-        moved_peak.reshape(block_count, rows_dev, -1),
-        moved_sum.reshape(block_count, rows_dev, -1),
+        moved_stats[..., :head_count],
+        moved_stats[..., head_count:],
     )
     attention = merge_parts(cache_part, draft_part, HEAD_SIZE)
-    every_row = lax.all_gather(attention, "blk", axis=0, tiled=True)
-    projected = lax.psum_scatter(
-        jnp.dot(every_row, out_weight, preferred_element_type=jnp.float32),
+    every_row = gather_rows(attention, "blk")
+    partial = jnp.dot(every_row, out_weight, preferred_element_type=jnp.float32)
+    out_rows = partial.shape[0] // kv_count
+    arrived = lax.all_to_all(
+        partial.reshape(kv_count, out_rows, partial.shape[1]),
         "kv",
-        scatter_dimension=0,
+        split_axis=0,
+        concat_axis=0,
         tiled=True,
-    ).astype(jnp.bfloat16)
+    )
+    projected = jnp.sum(arrived, axis=0).astype(jnp.bfloat16)
     positions_here = my_block * block_len + jnp.arange(block_len, dtype=jnp.int32)
     offset = positions_here[None, :] - lengths[:, None]
     written = (offset >= 0) & (offset < accepted_count[:, None])

time: 284 us -> 107 us (0.38)
  blocking collectives: 156 us -> 0 us
  waiting for transfers between devices: 79.3 us -> 47.2 us
  starting transfers between devices: 17.6 us -> 41.4 us
  between operations: 14.3 us -> 0.96 us
    all_gather x4 -> x0, blocking collectives: 156 us -> none  [the longest x1 41.5 us: on_device(): every_query = lax.all_gather(queries, 'blk', axis=0, tiled=True)]
    reduce_scatter x1 -> x0, waiting for transfers between devices: 75.7 us -> none  [on_device(): lax.psum_scatter(jnp.dot(every_row, out_weight, preferred_element_type=jn...]
    all_to_all x2 -> x4, waiting for transfers between devices: 3.62 us -> 37 us  [the longest x2 24.5 us: gather_rows(): lax.all_to_all(spread, axis_name, split_axis=0, concat_axis=0, tiled=True)]
    all_to_all x2 -> x4, starting transfers between devices: 11.4 us -> 37.5 us  [the longest x2 19.6 us: gather_rows(): lax.all_to_all(spread, axis_name, split_axis=0, concat_axis=0, tiled=True)]
    all_to_all x1, waiting for transfers between devices: 0.01 us -> 10.2 us  [on_device(): lax.all_to_all(local_out[0].astype(jnp.bfloat16), 'blk', split_axis=0, co...]
  transfers between devices with their start and end apart: 4 -> 5, of which waited for: 2 -> 5; matrix products, arithmetic and copies ran while one was open for 3% -> 7% of each run, Pallas kernels for 0% -> 0%
where the time goes in v1:
time: 107 us; the launch traced here: 106 us
  waiting for transfers between devices  47.2 us (44%)
  starting transfers between devices  41.4 us (39%)
  local copies, waits for them, and re-layouts  7.84 us (7%)
  matrix products  4.98 us (5%)
  other arithmetic  3.98 us (4%)
    all_to_all x2, waiting for transfers between devices, gather_rows(): lax.all_to_all(spread, axis_name, split_axis=0, concat_axis=0, tiled=True)  24.5 us
    all_to_all x2, starting transfers between devices, gather_rows(): lax.all_to_all(spread, axis_name, split_axis=0, concat_axis=0, tiled=True)  19.6 us
    all_to_all x1, starting transfers between devices, on_device(): lax.all_to_all(partial.reshape(kv_count, out_rows, partial.shape[1]), 'kv...  10.2 us
    all_to_all x1, waiting for transfers between devices, on_device(): lax.all_to_all(local_out[0].astype(jnp.bfloat16), 'blk', split_axis=0, co...  10.2 us
    all_to_all x1, starting transfers between devices, on_device(): lax.all_to_all(jnp.concatenate([local_peak[0], local_sum[0]], axis=1), 'b...  7.72 us
    all_to_all x1, waiting for transfers between devices, on_device(): lax.all_to_all(jnp.concatenate([local_peak[0], local_sum[0]], axis=1), 'b...  6.92 us
    all_to_all x1, waiting for transfers between devices, on_device(): lax.all_to_all(partial.reshape(kv_count, out_rows, partial.shape[1]), 'kv...  5.56 us
    all_to_all x1, starting transfers between devices, on_device(): lax.all_to_all(local_out[0].astype(jnp.bfloat16), 'blk', split_axis=0, co...  3.89 us
  transfers between devices with their start and end apart: 5, of which 5 were waited for; matrix products, arithmetic and copies ran while one was open for 7% of the time, Pallas kernels for 0%

profile of v1, /device:TPU:1, one launch (start us, length us, event | category | flops | bytes accessed | tf_op | source)
XLA Modules:
  0.0 106.3 jit_solution(13886491952676601671)
XLA Ops:
  0.6 0.8 pad_maximum_fusion.1
  1.5 0.9 broadcast_in_dim.102
  2.3 11.9 %all-to-all-start = ((bf16[32,8,1280]{2,1,0:T(8,128)(2,1)}), bf16[32,8,1280]{2,1,0:T(8,128)(2,1)S(1)}, u32[]{:S(2)}, u32[]{:S(2)}) async-start(bf16[32,8,1280]{2,1,0:T(8,128)(2,1)} %broadcast_in_dim.102), calls=%async_computation | async-start | bytes 1310720 | tf_op jit(solution)/shard_map/all_to_all | solution.py:98
  14.2 0.7 fusion.52
  14.9 0.2 fusion.35
  16.2 0.6 copy-done.5
  16.9 14.3 %all-to-all-done = bf16[32,8,1280]{2,1,0:T(8,128)(2,1)S(1)} async-done(((bf16[32,8,1280]{2,1,0:T(8,128)(2,1)}), bf16[32,8,1280]{2,1,0:T(8,128)(2,1)S(1)}, u32[]{:S(2)}, u32[]{:S(2)}) %all-to-all-start) | async-done | bytes 655392 | tf_op jit(solution)/shard_map/all_to_all | solution.py:98
  31.4 0.8 copy-done.2
  32.2 0.5 fusion.55
  32.8 0.6 fusion.19
  33.6 0.7 reshape.476
  34.3 7.7 %all-to-all-start.1 = ((f32[32,1,128]{2,1,0:T(1,128)}), f32[32,1,128]{2,1,0:T(1,128)S(1)}, u32[]{:S(2)}, u32[]{:S(2)}) async-start(f32[32,1,128]{2,1,0:T(1,128)} %reshape.476), calls=%async_computation.1 | async-start | bytes 32768 | tf_op jit(solution)/shard_map/all_to_all | solution.py:158
  42.0 0.3 fusion.3
  42.3 0.3 copy.47
  42.7 1.0 convert_element_type.105
  43.7 6.9 %all-to-all-done.1 = f32[32,1,128]{2,1,0:T(1,128)S(1)} async-done(((f32[32,1,128]{2,1,0:T(1,128)}), f32[32,1,128]{2,1,0:T(1,128)S(1)}, u32[]{:S(2)}, u32[]{:S(2)}) %all-to-all-start.1) | async-done | bytes 16416 | tf_op jit(solution)/shard_map/all_to_all | solution.py:158
  50.6 3.9 %all-to-all-start.2 = ((bf16[32,8,1024]{2,1,0:T(8,128)(2,1)}), bf16[32,8,1024]{2,1,0:T(8,128)(2,1)S(1)}, u32[]{:S(2)}, u32[]{:S(2)}) async-start(bf16[32,8,1024]{2,1,0:T(8,128)(2,1)} %convert_element_type.105), calls=%async_computation.2 | async-start | bytes 1048576 | tf_op jit(solution)/shard_map/all_to_all | solution.py:154
  54.5 0.2 fusion.56
  55.2 0.5 broadcast.199
  55.7 0.7 reduce.5
  56.9 10.2 %all-to-all-done.2 = bf16[32,8,1024]{2,1,0:T(8,128)(2,1)S(1)} async-done(((bf16[32,8,1024]{2,1,0:T(8,128)(2,1)}), bf16[32,8,1024]{2,1,0:T(8,128)(2,1)S(1)}, u32[]{:S(2)}, u32[]{:S(2)}) %all-to-all-start.2) | async-done | bytes 524320 | tf_op jit(solution)/shard_map/all_to_all | solution.py:154
  67.1 0.3 fusion.17
  67.5 0.9 broadcast_in_dim.109
  68.4 7.7 %all-to-all-start.3 = ((bf16[32,8,1024]{2,1,0:T(8,128)(2,1)}), bf16[32,8,1024]{2,1,0:T(8,128)(2,1)S(1)}, u32[]{:S(2)}, u32[]{:S(2)}) async-start(bf16[32,8,1024]{2,1,0:T(8,128)(2,1)} %broadcast_in_dim.109), calls=%async_computation.3 | async-start | bytes 1048576 | tf_op jit(solution)/shard_map/all_to_all | solution.py:98
  76.2 0.6 copy-done.4
  76.9 0.9 fusion.4
  77.8 10.2 %all-to-all-done.3 = bf16[32,8,1024]{2,1,0:T(8,128)(2,1)S(1)} async-done(((bf16[32,8,1024]{2,1,0:T(8,128)(2,1)}), bf16[32,8,1024]{2,1,0:T(8,128)(2,1)S(1)}, u32[]{:S(2)}, u32[]{:S(2)}) %all-to-all-start.3) | async-done | bytes 524320 | tf_op jit(solution)/shard_map/all_to_all | solution.py:98
  88.0 1.0 fusion.22
  89.0 10.2 %all-to-all-start.4 = ((f32[8,32,256]{2,1,0:T(8,128)}), f32[8,32,256]{2,1,0:T(8,128)S(1)}, u32[]{:S(2)}, u32[]{:S(2)}) async-start(f32[8,32,256]{2,1,0:T(8,128)} %fusion.22), calls=%async_computation.4 | async-start | bytes 524288 | tf_op jit(solution)/shard_map/all_to_all | solution.py:174
  99.3 0.9 fusion.5
  100.2 5.6 %all-to-all-done.4 = f32[8,32,256]{2,1,0:T(8,128)S(1)} async-done(((f32[8,32,256]{2,1,0:T(8,128)}), f32[8,32,256]{2,1,0:T(8,128)S(1)}, u32[]{:S(2)}, u32[]{:S(2)}) %all-to-all-start.4) | async-done | bytes 262176 | tf_op jit(solution)/shard_map/all_to_all | solution.py:174
  105.7 0.6 reduce_sum.64
  (41 shorter events, 2.6 us)
Async XLA Ops:
  0.6 87.4 %copy-start = (bf16[1024,256]{1,0:T(8,128)(2,1)S(1)}, bf16[1024,256]{1,0:T(8,128)(2,1)}, u32[]{:S(2)}) copy-start(bf16[1024,256]{1,0:T(8,128)(2,1)} %param.15) | copy-start | bytes 1572868
  2.3 28.9 %all-to-all-start = ((bf16[32,8,1280]{2,1,0:T(8,128)(2,1)}), bf16[32,8,1280]{2,1,0:T(8,128)(2,1)S(1)}, u32[]{:S(2)}, u32[]{:S(2)}) async-start(bf16[32,8,1280]{2,1,0:T(8,128)(2,1)} %broadcast_in_dim.102), calls=%async_computation | async-start | bytes 1310720 | tf_op jit(solution)/shard_map/all_to_all | solution.py:98
  16.2 0.7 copy-start.5
  16.2 0.7 copy-start.6
  31.3 0.9 copy-start.2
  33.5 8.5 %copy-start.1 = (bf16[4,128,128]{2,1,0:T(8,128)(2,1)S(1)}, bf16[4,128,128]{2,1,0:T(8,128)(2,1)}, u32[]{:S(2)}) copy-start(bf16[4,128,128]{2,1,0:T(8,128)(2,1)} %param.14) | copy-start | bytes 393220
  34.3 16.3 %all-to-all-start.1 = ((f32[32,1,128]{2,1,0:T(1,128)}), f32[32,1,128]{2,1,0:T(1,128)S(1)}, u32[]{:S(2)}, u32[]{:S(2)}) async-start(f32[32,1,128]{2,1,0:T(1,128)} %reshape.476), calls=%async_computation.1 | async-start | bytes 32768 | tf_op jit(solution)/shard_map/all_to_all | solution.py:158
  43.7 10.8 %copy-start.3 = (bf16[8,1024]{1,0:T(8,128)(2,1)S(1)}, bf16[8,1024]{1,0:T(8,128)(2,1)}, u32[]{:S(2)}) copy-start(bf16[8,1024]{1,0:T(8,128)(2,1)} %param.10) | copy-start | bytes 49156
  50.6 16.5 %all-to-all-start.2 = ((bf16[32,8,1024]{2,1,0:T(8,128)(2,1)}), bf16[32,8,1024]{2,1,0:T(8,128)(2,1)S(1)}, u32[]{:S(2)}, u32[]{:S(2)}) async-start(bf16[32,8,1024]{2,1,0:T(8,128)(2,1)} %convert_element_type.105), calls=%async_computation.2 | async-start | bytes 1048576 | tf_op jit(solution)/shard_map/all_to_all | solution.py:154
  68.4 19.6 %all-to-all-start.3 = ((bf16[32,8,1024]{2,1,0:T(8,128)(2,1)}), bf16[32,8,1024]{2,1,0:T(8,128)(2,1)S(1)}, u32[]{:S(2)}, u32[]{:S(2)}) async-start(bf16[32,8,1024]{2,1,0:T(8,128)(2,1)} %broadcast_in_dim.109), calls=%async_computation.3 | async-start | bytes 1048576 | tf_op jit(solution)/shard_map/all_to_all | solution.py:98
  76.1 0.7 copy-start.4
  89.0 16.7 %all-to-all-start.4 = ((f32[8,32,256]{2,1,0:T(8,128)}), f32[8,32,256]{2,1,0:T(8,128)S(1)}, u32[]{:S(2)}, u32[]{:S(2)}) async-start(f32[8,32,256]{2,1,0:T(8,128)} %fusion.22), calls=%async_computation.4 | async-start | bytes 524288 | tf_op jit(solution)/shard_map/all_to_all | solution.py:174

commit v2 on v1

--- a/solution.py
+++ b/solution.py
@@ -151,19 +151,29 @@
         usable,
         score_scale,
     )
-    moved_out = lax.all_to_all(
-        local_out[0].astype(jnp.bfloat16), "blk", split_axis=0, concat_axis=0, tiled=True
-    )
     head_count = local_peak.shape[-1]
-    moved_stats = lax.all_to_all(
-        jnp.concatenate([local_peak[0], local_sum[0]], axis=1),
-        "blk",
-        split_axis=0,
-        concat_axis=0,
-        tiled=True,
-    ).reshape(block_count, rows_dev, 2 * head_count)
+    stats = jnp.concatenate([local_peak[0], local_sum[0]], axis=1)
+    hi = lax.reduce_precision(stats, exponent_bits=8, mantissa_bits=7)
+    rest = stats - hi
+    mid = lax.reduce_precision(rest, exponent_bits=8, mantissa_bits=7)
+    lo = rest - mid
+    width_out = local_out.shape[-1]
+    packed_out = jnp.concatenate(
+        [local_out[0].astype(jnp.bfloat16)]
+        + [part.astype(jnp.bfloat16) for part in (hi, mid, lo)],
+        axis=1,
+    )
+    moved = lax.all_to_all(packed_out, "blk", split_axis=0, concat_axis=0, tiled=True)
+    moved = moved.reshape(block_count, rows_dev, -1)
+    parts = [
+        moved[..., width_out + j * 2 * head_count : width_out + (j + 1) * 2 * head_count].astype(
+            jnp.float32
+        )
+        for j in range(3)
+    ]
+    moved_stats = (parts[0] + parts[1]) + parts[2]
     cache_part = (
-        moved_out.reshape(block_count, rows_dev, -1),
+        moved[..., :width_out],
         moved_stats[..., :head_count],
         moved_stats[..., head_count:],
     )

time: 107 us -> 101 us (0.944)
  starting transfers between devices: 41.4 us -> 36.2 us
  waiting for transfers between devices: 47.2 us -> 45.9 us
    all_to_all x2 -> x1, starting transfers between devices: 11.6 us -> 7.72 us  [on_device(): lax.all_to_all(packed_out, 'blk', split_axis=0, concat_axis=0, tiled=True)]
    all_to_all x2 -> x1, waiting for transfers between devices: 17.1 us -> 13.8 us  [on_device(): lax.all_to_all(packed_out, 'blk', split_axis=0, concat_axis=0, tiled=True)]
    all_to_all x2, waiting for transfers between devices: 24.5 us -> 26.6 us  [gather_rows(): lax.all_to_all(spread, axis_name, split_axis=0, concat_axis=0, tiled=True)]
    concatenate x0 -> x3, local copies, waits for them, and re-layouts: none -> 1.19 us  [the longest x1 0.98 us: on_device(): jnp.concatenate([local_out[0].astype(jnp.bfloat16)] + [part.astype(jnp.bf...]
    all_to_all x1, starting transfers between devices: 10.2 us -> 9.09 us  [on_device(): lax.all_to_all(partial.reshape(kv_count, out_rows, partial.shape[1]), 'kv...]
    unnamed x18 -> x16, local copies, waits for them, and re-layouts: 3.02 us -> 3.45 us
  transfers between devices with their start and end apart: 5 -> 4, of which waited for: 5 -> 4; matrix products, arithmetic and copies ran while one was open for 7% -> 5% of each run, Pallas kernels for 0% -> 0%
where the time goes in v2:
time: 101 us; the launch traced here: 99.9 us
  waiting for transfers between devices  45.9 us (45%)
  starting transfers between devices  36.2 us (36%)
  local copies, waits for them, and re-layouts  8.5 us (8%)
  matrix products  4.96 us (5%)
  other arithmetic  3.35 us (3%)
    all_to_all x2, waiting for transfers between devices, gather_rows(): lax.all_to_all(spread, axis_name, split_axis=0, concat_axis=0, tiled=True)  26.6 us
    all_to_all x2, starting transfers between devices, gather_rows(): lax.all_to_all(spread, axis_name, split_axis=0, concat_axis=0, tiled=True)  19.4 us
    all_to_all x1, waiting for transfers between devices, on_device(): lax.all_to_all(packed_out, 'blk', split_axis=0, concat_axis=0, tiled=True)  13.8 us
    all_to_all x1, starting transfers between devices, on_device(): lax.all_to_all(partial.reshape(kv_count, out_rows, partial.shape[1]), 'kv...  9.09 us
    all_to_all x1, starting transfers between devices, on_device(): lax.all_to_all(packed_out, 'blk', split_axis=0, concat_axis=0, tiled=True)  7.72 us
    all_to_all x1, waiting for transfers between devices, on_device(): lax.all_to_all(partial.reshape(kv_count, out_rows, partial.shape[1]), 'kv...  5.56 us
    unnamed x16, local copies, waits for them, and re-layouts  3.45 us
  transfers between devices with their start and end apart: 4, of which 4 were waited for; matrix products, arithmetic and copies ran while one was open for 5% of the time, Pallas kernels for 0%

profile of v2, /device:TPU:1, one launch (start us, length us, event | category | flops | bytes accessed | tf_op | source)
XLA Modules:
  0.0 99.9 jit_solution(17257791120549548467)
XLA Ops:
  0.6 0.8 pad_maximum_fusion.1
  1.5 0.9 broadcast_in_dim.103
  2.3 11.9 %all-to-all-start = ((bf16[32,8,1280]{2,1,0:T(8,128)(2,1)}), bf16[32,8,1280]{2,1,0:T(8,128)(2,1)S(1)}, u32[]{:S(2)}, u32[]{:S(2)}) async-start(bf16[32,8,1280]{2,1,0:T(8,128)(2,1)} %broadcast_in_dim.103), calls=%async_computation | async-start | bytes 1310720 | tf_op jit(solution)/shard_map/all_to_all | solution.py:98
  14.2 0.6 copy-done.5
  15.0 0.7 fusion.53
  15.7 0.2 fusion.36
  15.9 0.2 fusion.14
  16.6 14.7 %all-to-all-done = bf16[32,8,1280]{2,1,0:T(8,128)(2,1)S(1)} async-done(((bf16[32,8,1280]{2,1,0:T(8,128)(2,1)}), bf16[32,8,1280]{2,1,0:T(8,128)(2,1)S(1)}, u32[]{:S(2)}, u32[]{:S(2)}) %all-to-all-start) | async-done | bytes 655392 | tf_op jit(solution)/shard_map/all_to_all | solution.py:98
  31.4 0.8 copy-done.2
  32.2 0.5 fusion.56
  32.8 0.6 fusion.18
  34.0 0.6 copy-done.1
  34.6 0.3 fusion.3
  34.9 0.3 copy.86
  35.2 0.2 convert_element_type.120
  35.5 1.0 concatenate.21
  36.4 7.7 %all-to-all-start.1 = ((bf16[32,8,1072]{2,1,0:T(8,128)(2,1)}), bf16[32,8,1072]{2,1,0:T(8,128)(2,1)S(1)}, u32[]{:S(2)}, u32[]{:S(2)}) async-start(bf16[32,8,1072]{2,1,0:T(8,128)(2,1)} %concatenate.21), calls=%async_computation.1 | async-start | bytes 1179648 | tf_op jit(solution)/shard_map/all_to_all | solution.py:166
  44.6 0.7 copy-done.3
  45.3 0.2 fusion.57
  45.6 0.2 fusion.38
  45.9 13.8 %all-to-all-done.1 = bf16[32,8,1072]{2,1,0:T(8,128)(2,1)S(1)} async-done(((bf16[32,8,1072]{2,1,0:T(8,128)(2,1)}), bf16[32,8,1072]{2,1,0:T(8,128)(2,1)S(1)}, u32[]{:S(2)}, u32[]{:S(2)}) %all-to-all-start.1) | async-done | bytes 548896 | tf_op jit(solution)/shard_map/all_to_all | solution.py:166
  60.3 0.3 fusion.17
  60.7 0.9 broadcast_in_dim.109
  61.6 7.6 %all-to-all-start.2 = ((bf16[32,8,1024]{2,1,0:T(8,128)(2,1)}), bf16[32,8,1024]{2,1,0:T(8,128)(2,1)S(1)}, u32[]{:S(2)}, u32[]{:S(2)}) async-start(bf16[32,8,1024]{2,1,0:T(8,128)(2,1)} %broadcast_in_dim.109), calls=%async_computation.2 | async-start | bytes 1048576 | tf_op jit(solution)/shard_map/all_to_all | solution.py:98
  69.2 0.6 copy-done.4
  69.9 0.9 fusion.4
  70.8 11.9 %all-to-all-done.2 = bf16[32,8,1024]{2,1,0:T(8,128)(2,1)S(1)} async-done(((bf16[32,8,1024]{2,1,0:T(8,128)(2,1)}), bf16[32,8,1024]{2,1,0:T(8,128)(2,1)S(1)}, u32[]{:S(2)}, u32[]{:S(2)}) %all-to-all-start.2) | async-done | bytes 524320 | tf_op jit(solution)/shard_map/all_to_all | solution.py:98
  82.7 1.0 fusion.22
  83.7 9.1 %all-to-all-start.3 = ((f32[8,32,256]{2,1,0:T(8,128)}), f32[8,32,256]{2,1,0:T(8,128)S(1)}, u32[]{:S(2)}, u32[]{:S(2)}) async-start(f32[8,32,256]{2,1,0:T(8,128)} %fusion.22), calls=%async_computation.3 | async-start | bytes 524288 | tf_op jit(solution)/shard_map/all_to_all | solution.py:184
  92.8 0.9 fusion.5
  93.7 5.6 %all-to-all-done.3 = f32[8,32,256]{2,1,0:T(8,128)S(1)} async-done(((f32[8,32,256]{2,1,0:T(8,128)}), f32[8,32,256]{2,1,0:T(8,128)S(1)}, u32[]{:S(2)}, u32[]{:S(2)}) %all-to-all-start.3) | async-done | bytes 262176 | tf_op jit(solution)/shard_map/all_to_all | solution.py:184
  99.3 0.6 reduce_sum.64
  (42 shorter events, 2.8 us)
Async XLA Ops:
  0.6 82.1 %copy-start = (bf16[1024,256]{1,0:T(8,128)(2,1)S(1)}, bf16[1024,256]{1,0:T(8,128)(2,1)}, u32[]{:S(2)}) copy-start(bf16[1024,256]{1,0:T(8,128)(2,1)} %param.15) | copy-start | bytes 1572868
  2.3 28.9 %all-to-all-start = ((bf16[32,8,1280]{2,1,0:T(8,128)(2,1)}), bf16[32,8,1280]{2,1,0:T(8,128)(2,1)S(1)}, u32[]{:S(2)}, u32[]{:S(2)}) async-start(bf16[32,8,1280]{2,1,0:T(8,128)(2,1)} %broadcast_in_dim.103), calls=%async_computation | async-start | bytes 1310720 | tf_op jit(solution)/shard_map/all_to_all | solution.py:98
  14.2 0.7 copy-start.5
  14.2 0.7 copy-start.6
  31.3 0.9 copy-start.2
  33.7 0.9 copy-start.1
  36.4 23.3 %all-to-all-start.1 = ((bf16[32,8,1072]{2,1,0:T(8,128)(2,1)}), bf16[32,8,1072]{2,1,0:T(8,128)(2,1)S(1)}, u32[]{:S(2)}, u32[]{:S(2)}) async-start(bf16[32,8,1072]{2,1,0:T(8,128)(2,1)} %concatenate.21), calls=%async_computation.1 | async-start | bytes 1179648 | tf_op jit(solution)/shard_map/all_to_all | solution.py:166
  44.5 0.7 copy-start.3
  61.6 21.1 %all-to-all-start.2 = ((bf16[32,8,1024]{2,1,0:T(8,128)(2,1)}), bf16[32,8,1024]{2,1,0:T(8,128)(2,1)S(1)}, u32[]{:S(2)}, u32[]{:S(2)}) async-start(bf16[32,8,1024]{2,1,0:T(8,128)(2,1)} %broadcast_in_dim.109), calls=%async_computation.2 | async-start | bytes 1048576 | tf_op jit(solution)/shard_map/all_to_all | solution.py:98
  69.2 0.7 copy-start.4
  83.7 15.6 %all-to-all-start.3 = ((f32[8,32,256]{2,1,0:T(8,128)}), f32[8,32,256]{2,1,0:T(8,128)S(1)}, u32[]{:S(2)}, u32[]{:S(2)}) async-start(f32[8,32,256]{2,1,0:T(8,128)} %fusion.22), calls=%async_computation.3 | async-start | bytes 524288 | tf_op jit(solution)/shard_map/all_to_all | solution.py:184

commit v3 on v2

--- a/solution.py
+++ b/solution.py
@@ -4,6 +4,8 @@
 import jax.numpy as jnp
 from jax import lax
 from jax.sharding import PartitionSpec as P
+from jax.experimental import pallas as pl
+from jax.experimental.pallas import tpu as pltpu
 
 HEAD_SIZE = 128
 TREE_TOKENS = 64
@@ -90,6 +92,68 @@
         "rps,rsc->rpc", selector, sources, preferred_element_type=jnp.float32
     ).astype(jnp.bfloat16)
     return jnp.where(written[:, :, None], placed, cache_rows)
+
+
+def split_three(x):
+    hi = x.astype(jnp.bfloat16)
+    rest = x - hi.astype(jnp.float32)
+    mid = rest.astype(jnp.bfloat16)
+    lo = (rest - mid.astype(jnp.float32)).astype(jnp.bfloat16)
+    return hi, mid, lo
+
+
+def block_attention_kernel(limit_ref, q_ref, k_ref, v_ref, out_ref, stats_ref):
+    requests, block_len, _ = k_ref.shape
+    rows = q_ref.shape[0] // requests
+    heads = q_ref.shape[1] // HEAD_SIZE
+    score_scale = 1.0 / math.sqrt(HEAD_SIZE)
+    for r in range(requests):
+        keys = k_ref[r]
+        values = v_ref[r]
+        valid = lax.broadcasted_iota(jnp.int32, (rows, block_len), 1) < limit_ref[r]
+        for h in range(heads):
+            q = q_ref[r * rows : (r + 1) * rows, h * HEAD_SIZE : (h + 1) * HEAD_SIZE]
+            scores = (
+                lax.dot_general(
+                    q, keys, (((1,), (1,)), ((), ())), preferred_element_type=jnp.float32
+                )
+                * score_scale
+            )
+            scores = jnp.where(valid, scores, NEG_FLOOR)
+            peak = jnp.max(scores, axis=1, keepdims=True)
+            weights = jnp.where(valid, jnp.exp(scores - peak), 0.0)
+            total = jnp.sum(weights, axis=1, keepdims=True)
+            out = jnp.dot(
+                weights.astype(jnp.bfloat16), values, preferred_element_type=jnp.float32
+            )
+            out_ref[r * rows : (r + 1) * rows, h * HEAD_SIZE : (h + 1) * HEAD_SIZE] = out.astype(
+                out_ref.dtype
+            )
+            stats_ref[r * rows : (r + 1) * rows, h : h + 1] = peak
+            stats_ref[r * rows : (r + 1) * rows, heads + h : heads + h + 1] = total
+    width = heads * HEAD_SIZE
+    stats = stats_ref[...]
+    for j, part in enumerate(split_three(stats)):
+        out_ref[:, width + j * 2 * heads : width + (j + 1) * 2 * heads] = part
+
+
+def block_attention(limit, every_query, keys, values):
+    rows, width = every_query.shape
+    heads = width // HEAD_SIZE
+    requests, block_len, _ = keys.shape
+    vmem = pl.BlockSpec(memory_space=pltpu.VMEM)
+    return pl.pallas_call(
+        block_attention_kernel,
+        out_shape=jax.ShapeDtypeStruct((rows, width + 6 * heads), jnp.bfloat16),
+        in_specs=[pl.BlockSpec(memory_space=pltpu.SMEM), vmem, vmem, vmem],
+        out_specs=vmem,
+        scratch_shapes=[pltpu.VMEM((rows, 2 * heads), jnp.float32)],
+        cost_estimate=pl.CostEstimate(
+            flops=4 * rows * heads * block_len * HEAD_SIZE,
+            transcendentals=rows * heads * block_len,
+            bytes_accessed=2 * (rows * width + 2 * requests * block_len * HEAD_SIZE + rows * (width + 6 * heads)),
+        ),
+    )(limit, every_query, keys, values)
 
 
 def gather_rows(block, axis_name):
@@ -141,28 +205,12 @@
     own_reach = lax.dynamic_slice_in_dim(reachable, node_start, rows_dev, 1)
     draft_usable = (own_reach > 0.5)[None, :, None, None, :, :]
     draft_part = partial_softmax(local_queries, tree_keys, tree_values, draft_usable, score_scale)
-    all_queries = every_query.reshape(requests, TREE_TOKENS, kv_local, query_group_width, HEAD_SIZE)
-    positions = my_block * block_len + jnp.arange(block_len, dtype=jnp.int32)
-    usable = (positions[None, :] < lengths[:, None])[None, :, None, None, None, :]
-    local_out, local_peak, local_sum = partial_softmax(
-        all_queries,
-        cached_key_vectors.reshape(requests, 1, block_len, kv_local, HEAD_SIZE),
-        cached_value_vectors.reshape(requests, 1, block_len, kv_local, HEAD_SIZE),
-        usable,
-        score_scale,
-    )
-    head_count = local_peak.shape[-1]
-    stats = jnp.concatenate([local_peak[0], local_sum[0]], axis=1)
-    hi = lax.reduce_precision(stats, exponent_bits=8, mantissa_bits=7)
-    rest = stats - hi
-    mid = lax.reduce_precision(rest, exponent_bits=8, mantissa_bits=7)
-    lo = rest - mid
-    width_out = local_out.shape[-1]
-    packed_out = jnp.concatenate(
-        [local_out[0].astype(jnp.bfloat16)]
-        + [part.astype(jnp.bfloat16) for part in (hi, mid, lo)],
-        axis=1,
-    )
+    limit = lengths - my_block * block_len
+    packed_out = block_attention(
+        limit, every_query, cached_key_vectors, cached_value_vectors
+    )
+    head_count = width_q // HEAD_SIZE
+    width_out = width_q
     moved = lax.all_to_all(packed_out, "blk", split_axis=0, concat_axis=0, tiled=True)
     moved = moved.reshape(block_count, rows_dev, -1)
     parts = [

time: 101 us -> 106 us (1.050)
  Pallas kernels: 0 us -> 9.69 us
  local copies, waits for them, and re-layouts: 8.5 us -> 6.31 us
    pallas_call x0 -> x1, Pallas kernels: none -> 9.69 us  [block_attention(): pl.pallas_call(block_attention_kernel, out_shape=jax.ShapeDtypeStruct((ro...]
    concatenate x3 -> x0, local copies, waits for them, and re-layouts: 1.19 us -> none  [the longest x1 0.98 us: on_device(): jnp.concatenate([local_out[0].astype(jnp.bfloat16)] + [part.astype(jnp.bf...]
    unnamed x16 -> x14, local copies, waits for them, and re-layouts: 3.45 us -> 2.52 us
where the time goes in v3:
time: 106 us
  waiting for transfers between devices  44.9 us (42%)
  starting transfers between devices  36.5 us (34%)
  Pallas kernels  9.69 us (9%)
  local copies, waits for them, and re-layouts  6.31 us (6%)
  matrix products  4.14 us (4%)
  other arithmetic  3.18 us (3%)
    all_to_all x2, waiting for transfers between devices, gather_rows(): lax.all_to_all(spread, axis_name, split_axis=0, concat_axis=0, tiled=True)  25.5 us
    all_to_all x2, starting transfers between devices, gather_rows(): lax.all_to_all(spread, axis_name, split_axis=0, concat_axis=0, tiled=True)  19.6 us
    all_to_all x1, waiting for transfers between devices, on_device(): lax.all_to_all(packed_out, 'blk', split_axis=0, concat_axis=0, tiled=True)  13.8 us
    pallas_call x1, Pallas kernels, block_attention(): pl.pallas_call(block_attention_kernel, out_shape=jax.ShapeDtypeStruct((ro...  9.69 us
    all_to_all x1, starting transfers between devices, on_device(): lax.all_to_all(partial.reshape(kv_count, out_rows, partial.shape[1]), 'kv...  9.22 us
    all_to_all x1, starting transfers between devices, on_device(): lax.all_to_all(packed_out, 'blk', split_axis=0, concat_axis=0, tiled=True)  7.72 us
    all_to_all x1, waiting for transfers between devices, on_device(): lax.all_to_all(partial.reshape(kv_count, out_rows, partial.shape[1]), 'kv...  5.55 us
    unnamed x14, local copies, waits for them, and re-layouts  2.52 us
  transfers between devices with their start and end apart: 4, of which 4 were waited for; matrix products, arithmetic and copies ran while one was open for 5% of the time, Pallas kernels for 0%

profile of v3, /device:TPU:1, one launch (start us, length us, event | category | flops | bytes accessed | tf_op | source)
XLA Modules:
  0.0 105.5 jit_solution(13801095103329121498)
XLA Ops:
  0.6 0.8 pad_maximum_fusion
  1.5 0.9 broadcast_in_dim.42
  2.3 11.9 %all-to-all-start = ((bf16[32,8,1280]{2,1,0:T(8,128)(2,1)}), bf16[32,8,1280]{2,1,0:T(8,128)(2,1)S(1)}, u32[]{:S(2)}, u32[]{:S(2)}) async-start(bf16[32,8,1280]{2,1,0:T(8,128)(2,1)} %broadcast_in_dim.42), calls=%async_computation | async-start | bytes 1310720 | tf_op jit(solution)/shard_map/all_to_all | solution.py:162
  14.2 0.6 copy-done.5
  14.9 0.5 broadcast_subtract_fusion.1.limit_ref
  15.4 0.7 fusion.41
  16.1 0.2 fusion.24
  16.3 0.2 fusion.10
  16.4 0.2 fusion.2
  16.6 0.2 fusion.3
  16.8 0.2 fusion.4
  17.0 14.3 %all-to-all-done = bf16[32,8,1280]{2,1,0:T(8,128)(2,1)S(1)} async-done(((bf16[32,8,1280]{2,1,0:T(8,128)(2,1)}), bf16[32,8,1280]{2,1,0:T(8,128)(2,1)S(1)}, u32[]{:S(2)}, u32[]{:S(2)}) %all-to-all-start) | async-done | bytes 655392 | tf_op jit(solution)/shard_map/all_to_all | solution.py:162
  31.3 0.8 slice.36.q_ref
  32.1 9.7 %shard_map.121 = bf16[256,1072]{1,0:T(8,128)(2,1)} custom-call(s32[4]{0:T(128)} %broadcast_subtract_fusion.1.limit_ref, bf16[256,1024]{1,0:T(8,128)(2,1)} %slice.36.q_ref, bf16[4,128,128]{2,1,0:T(8,128)(2,1)} %k_ref.1, bf16[4,128,128]{2,1,0:T(8,128)(2,1)} %v_ref.1), custom_call_target="tpu_custom_call" | custom-call | flops 134217728 | bytes 1335296 | tf_op jit(solution)/shard_map/pallas_call | solution.py:145
  41.8 7.7 %all-to-all-start.1 = ((bf16[32,8,1072]{2,1,0:T(8,128)(2,1)}), bf16[32,8,1072]{2,1,0:T(8,128)(2,1)S(1)}, u32[]{:S(2)}, u32[]{:S(2)}) async-start(bf16[32,8,1072]{2,1,0:T(8,128)(2,1)} %bitcast.85), calls=%async_computation.1 | async-start | bytes 1179648 | tf_op jit(solution)/shard_map/all_to_all | solution.py:214
  49.5 0.2 fusion.5
  49.9 0.7 copy-done.3
  50.6 0.2 fusion.44
  50.9 0.2 fusion.26
  51.3 13.8 %all-to-all-done.1 = bf16[32,8,1072]{2,1,0:T(8,128)(2,1)S(1)} async-done(((bf16[32,8,1072]{2,1,0:T(8,128)(2,1)}), bf16[32,8,1072]{2,1,0:T(8,128)(2,1)S(1)}, u32[]{:S(2)}, u32[]{:S(2)}) %all-to-all-start.1) | async-done | bytes 548896 | tf_op jit(solution)/shard_map/all_to_all | solution.py:214
  65.6 0.3 fusion.13
  66.1 0.9 broadcast_in_dim.46
  66.9 7.7 %all-to-all-start.2 = ((bf16[32,8,1024]{2,1,0:T(8,128)(2,1)}), bf16[32,8,1024]{2,1,0:T(8,128)(2,1)S(1)}, u32[]{:S(2)}, u32[]{:S(2)}) async-start(bf16[32,8,1024]{2,1,0:T(8,128)(2,1)} %broadcast_in_dim.46), calls=%async_computation.2 | async-start | bytes 1048576 | tf_op jit(solution)/shard_map/all_to_all | solution.py:162
  74.7 0.6 copy-done.4
  75.4 0.6 copy-done.6
  76.1 0.9 fusion
  77.0 11.2 %all-to-all-done.2 = bf16[32,8,1024]{2,1,0:T(8,128)(2,1)S(1)} async-done(((bf16[32,8,1024]{2,1,0:T(8,128)(2,1)}), bf16[32,8,1024]{2,1,0:T(8,128)(2,1)S(1)}, u32[]{:S(2)}, u32[]{:S(2)}) %all-to-all-start.2) | async-done | bytes 524320 | tf_op jit(solution)/shard_map/all_to_all | solution.py:162
  88.2 1.0 fusion.14
  89.2 9.2 %all-to-all-start.3 = ((f32[8,32,256]{2,1,0:T(8,128)}), f32[8,32,256]{2,1,0:T(8,128)S(1)}, u32[]{:S(2)}, u32[]{:S(2)}) async-start(f32[8,32,256]{2,1,0:T(8,128)} %fusion.14), calls=%async_computation.3 | async-start | bytes 524288 | tf_op jit(solution)/shard_map/all_to_all | solution.py:232
  98.4 0.9 fusion.1
  99.4 5.6 %all-to-all-done.3 = f32[8,32,256]{2,1,0:T(8,128)S(1)} async-done(((f32[8,32,256]{2,1,0:T(8,128)}), f32[8,32,256]{2,1,0:T(8,128)S(1)}, u32[]{:S(2)}, u32[]{:S(2)}) %all-to-all-start.3) | async-done | bytes 262176 | tf_op jit(solution)/shard_map/all_to_all | solution.py:232
  104.9 0.6 reduce_sum.51
  (31 shorter events, 1.4 us)
Async XLA Ops:
  0.6 87.6 %copy-start = (bf16[1024,256]{1,0:T(8,128)(2,1)S(1)}, bf16[1024,256]{1,0:T(8,128)(2,1)}, u32[]{:S(2)}) copy-start(bf16[1024,256]{1,0:T(8,128)(2,1)} %param.15) | copy-start | bytes 1572868
  2.3 28.9 %all-to-all-start = ((bf16[32,8,1280]{2,1,0:T(8,128)(2,1)}), bf16[32,8,1280]{2,1,0:T(8,128)(2,1)S(1)}, u32[]{:S(2)}, u32[]{:S(2)}) async-start(bf16[32,8,1280]{2,1,0:T(8,128)(2,1)} %broadcast_in_dim.42), calls=%async_computation | async-start | bytes 1310720 | tf_op jit(solution)/shard_map/all_to_all | solution.py:162
  14.2 0.7 copy-start.5
  41.8 23.3 %all-to-all-start.1 = ((bf16[32,8,1072]{2,1,0:T(8,128)(2,1)}), bf16[32,8,1072]{2,1,0:T(8,128)(2,1)S(1)}, u32[]{:S(2)}, u32[]{:S(2)}) async-start(bf16[32,8,1072]{2,1,0:T(8,128)(2,1)} %bitcast.85), calls=%async_computation.1 | async-start | bytes 1179648 | tf_op jit(solution)/shard_map/all_to_all | solution.py:214
  49.9 0.7 copy-start.3
  66.9 9.1 %copy-start.1 = (bf16[4,128,128]{2,1,0:T(8,128)(2,1)S(1)}, bf16[4,128,128]{2,1,0:T(8,128)(2,1)}, u32[]{:S(2)}) copy-start(bf16[4,128,128]{2,1,0:T(8,128)(2,1)} %k_ref.1) | copy-start | bytes 393220
  66.9 21.3 %all-to-all-start.2 = ((bf16[32,8,1024]{2,1,0:T(8,128)(2,1)}), bf16[32,8,1024]{2,1,0:T(8,128)(2,1)S(1)}, u32[]{:S(2)}, u32[]{:S(2)}) async-start(bf16[32,8,1024]{2,1,0:T(8,128)(2,1)} %broadcast_in_dim.46), calls=%async_computation.2 | async-start | bytes 1048576 | tf_op jit(solution)/shard_map/all_to_all | solution.py:162
  74.6 0.7 copy-start.4
  75.3 0.7 copy-start.6
  89.2 9.2 %copy-start.2 = (bf16[4,128,128]{2,1,0:T(8,128)(2,1)S(1)}, bf16[4,128,128]{2,1,0:T(8,128)(2,1)}, u32[]{:S(2)}) copy-start(bf16[4,128,128]{2,1,0:T(8,128)(2,1)} %v_ref.1) | copy-start | bytes 393220
  89.2 15.7 %all-to-all-start.3 = ((f32[8,32,256]{2,1,0:T(8,128)}), f32[8,32,256]{2,1,0:T(8,128)S(1)}, u32[]{:S(2)}, u32[]{:S(2)}) async-start(f32[8,32,256]{2,1,0:T(8,128)} %fusion.14), calls=%async_computation.3 | async-start | bytes 524288 | tf_op jit(solution)/shard_map/all_to_all | solution.py:232

commit v4 on v3

--- a/solution.py
+++ b/solution.py
@@ -104,41 +104,44 @@
 
 def block_attention_kernel(limit_ref, q_ref, k_ref, v_ref, out_ref, stats_ref):
     requests, block_len, _ = k_ref.shape
-    rows = q_ref.shape[0] // requests
-    heads = q_ref.shape[1] // HEAD_SIZE
+    rows = out_ref.shape[0] // requests
+    heads = stats_ref.shape[1] // 2
     score_scale = 1.0 / math.sqrt(HEAD_SIZE)
     for r in range(requests):
-        keys = k_ref[r]
-        values = v_ref[r]
-        valid = lax.broadcasted_iota(jnp.int32, (rows, block_len), 1) < limit_ref[r]
+        q = jnp.concatenate(
+            [
+                q_ref[r * rows : (r + 1) * rows, h * HEAD_SIZE : (h + 1) * HEAD_SIZE]
+                for h in range(heads)
+            ],
+            axis=0,
+        )
+        scores = (
+            lax.dot_general(
+                q, k_ref[r], (((1,), (1,)), ((), ())), preferred_element_type=jnp.float32
+            )
+            * score_scale
+        )
+        valid = lax.broadcasted_iota(jnp.int32, scores.shape, 1) < limit_ref[r]
+        scores = jnp.where(valid, scores, NEG_FLOOR)
+        peak = jnp.max(scores, axis=1, keepdims=True)
+        weights = jnp.where(valid, jnp.exp(scores - peak), 0.0)
+        total = jnp.sum(weights, axis=1, keepdims=True)
+        out = jnp.dot(
+            weights.astype(jnp.bfloat16), v_ref[r], preferred_element_type=jnp.float32
+        ).astype(out_ref.dtype)
         for h in range(heads):
-            q = q_ref[r * rows : (r + 1) * rows, h * HEAD_SIZE : (h + 1) * HEAD_SIZE]
-            scores = (
-                lax.dot_general(
-                    q, keys, (((1,), (1,)), ((), ())), preferred_element_type=jnp.float32
-                )
-                * score_scale
-            )
-            scores = jnp.where(valid, scores, NEG_FLOOR)
-            peak = jnp.max(scores, axis=1, keepdims=True)
-            weights = jnp.where(valid, jnp.exp(scores - peak), 0.0)
-            total = jnp.sum(weights, axis=1, keepdims=True)
-            out = jnp.dot(
-                weights.astype(jnp.bfloat16), values, preferred_element_type=jnp.float32
-            )
-            out_ref[r * rows : (r + 1) * rows, h * HEAD_SIZE : (h + 1) * HEAD_SIZE] = out.astype(
-                out_ref.dtype
-            )
-            stats_ref[r * rows : (r + 1) * rows, h : h + 1] = peak
-            stats_ref[r * rows : (r + 1) * rows, heads + h : heads + h + 1] = total
+            here = slice(h * rows, (h + 1) * rows)
+            out_ref[r * rows : (r + 1) * rows, h * HEAD_SIZE : (h + 1) * HEAD_SIZE] = out[here]
+            stats_ref[r * rows : (r + 1) * rows, h : h + 1] = peak[here]
+            stats_ref[r * rows : (r + 1) * rows, heads + h : heads + h + 1] = total[here]
     width = heads * HEAD_SIZE
     stats = stats_ref[...]
     for j, part in enumerate(split_three(stats)):
         out_ref[:, width + j * 2 * heads : width + (j + 1) * 2 * heads] = part
 
 
-def block_attention(limit, every_query, keys, values):
-    rows, width = every_query.shape
+def block_attention(limit, every_query, keys, values, width):
+    rows = every_query.shape[0]
     heads = width // HEAD_SIZE
     requests, block_len, _ = keys.shape
     vmem = pl.BlockSpec(memory_space=pltpu.VMEM)
@@ -207,7 +210,7 @@
     draft_part = partial_softmax(local_queries, tree_keys, tree_values, draft_usable, score_scale)
     limit = lengths - my_block * block_len
     packed_out = block_attention(
-        limit, every_query, cached_key_vectors, cached_value_vectors
+        limit, packed, cached_key_vectors, cached_value_vectors, width_q
     )
     head_count = width_q // HEAD_SIZE
     width_out = width_q

time: 106 us -> 99.6 us (0.940)
  Pallas kernels: 9.69 us -> 3.14 us
    pallas_call x1, Pallas kernels: 9.69 us -> 3.14 us  [block_attention(): pl.pallas_call(block_attention_kernel, out_shape=jax.ShapeDtypeStruct((ro...]
    unnamed x14 -> x16, local copies, waits for them, and re-layouts: 2.52 us -> 2.68 us
  transfers between devices with their start and end apart: 4 -> 4, of which waited for: 4 -> 4; matrix products, arithmetic and copies ran while one was open for 5% -> 6% of each run, Pallas kernels for 0% -> 0%
where the time goes in v4:
time: 99.6 us; the launch traced here: 99 us
  waiting for transfers between devices  44.7 us (45%)
  starting transfers between devices  36.5 us (37%)
  local copies, waits for them, and re-layouts  6.52 us (7%)
  matrix products  4.14 us (4%)
  other arithmetic  3.18 us (3%)
  Pallas kernels  3.14 us (3%)
    all_to_all x2, waiting for transfers between devices, gather_rows(): lax.all_to_all(spread, axis_name, split_axis=0, concat_axis=0, tiled=True)  25.5 us
    all_to_all x2, starting transfers between devices, gather_rows(): lax.all_to_all(spread, axis_name, split_axis=0, concat_axis=0, tiled=True)  19.6 us
    all_to_all x1, waiting for transfers between devices, on_device(): lax.all_to_all(packed_out, 'blk', split_axis=0, concat_axis=0, tiled=True)  13.6 us
    all_to_all x1, starting transfers between devices, on_device(): lax.all_to_all(partial.reshape(kv_count, out_rows, partial.shape[1]), 'kv...  9.22 us
    all_to_all x1, starting transfers between devices, on_device(): lax.all_to_all(packed_out, 'blk', split_axis=0, concat_axis=0, tiled=True)  7.72 us
    all_to_all x1, waiting for transfers between devices, on_device(): lax.all_to_all(partial.reshape(kv_count, out_rows, partial.shape[1]), 'kv...  5.55 us
    pallas_call x1, Pallas kernels, block_attention(): pl.pallas_call(block_attention_kernel, out_shape=jax.ShapeDtypeStruct((ro...  3.14 us
    unnamed x16, local copies, waits for them, and re-layouts  2.68 us
  transfers between devices with their start and end apart: 4, of which 4 were waited for; matrix products, arithmetic and copies ran while one was open for 6% of the time, Pallas kernels for 0%

profile of v4, /device:TPU:1, one launch (start us, length us, event | category | flops | bytes accessed | tf_op | source)
XLA Modules:
  0.0 99.0 jit_solution(15706787882990210746)
XLA Ops:
  0.6 0.8 pad_maximum_fusion
  1.5 0.9 broadcast_in_dim.42
  2.3 11.9 %all-to-all-start = ((bf16[32,8,1280]{2,1,0:T(8,128)(2,1)}), bf16[32,8,1280]{2,1,0:T(8,128)(2,1)S(1)}, u32[]{:S(2)}, u32[]{:S(2)}) async-start(bf16[32,8,1280]{2,1,0:T(8,128)(2,1)} %broadcast_in_dim.42), calls=%async_computation | async-start | bytes 1310720 | tf_op jit(solution)/shard_map/all_to_all | solution.py:165
  14.2 0.6 copy-done.6
  14.9 0.5 broadcast_subtract_fusion.1.limit_ref
  15.4 0.7 fusion.41
  16.1 0.2 fusion.24
  16.3 0.2 fusion.10
  16.5 0.2 fusion.2
  16.6 0.2 fusion.3
  16.8 0.2 fusion.4
  17.0 14.3 %all-to-all-done = bf16[32,8,1280]{2,1,0:T(8,128)(2,1)S(1)} async-done(((bf16[32,8,1280]{2,1,0:T(8,128)(2,1)}), bf16[32,8,1280]{2,1,0:T(8,128)(2,1)S(1)}, u32[]{:S(2)}, u32[]{:S(2)}) %all-to-all-start) | async-done | bytes 655392 | tf_op jit(solution)/shard_map/all_to_all | solution.py:165
  31.3 0.8 copy-done.1
  32.1 3.1 %shard_map.121 = bf16[256,1072]{1,0:T(8,128)(2,1)} custom-call(s32[4]{0:T(128)} %broadcast_subtract_fusion.1.limit_ref, bf16[256,1280]{1,0:T(8,128)(2,1)} %bitcast.83, bf16[4,128,128]{2,1,0:T(8,128)(2,1)} %k_ref.1, bf16[4,128,128]{2,1,0:T(8,128)(2,1)} %v_ref.1), custom_call_target="tpu_custom_call" | custom-call | flops 134217728 | bytes 1335296 | tf_op jit(solution)/shard_map/pallas_call | solution.py:148
  35.3 7.7 %all-to-all-start.1 = ((bf16[32,8,1072]{2,1,0:T(8,128)(2,1)}), bf16[32,8,1072]{2,1,0:T(8,128)(2,1)S(1)}, u32[]{:S(2)}, u32[]{:S(2)}) async-start(bf16[32,8,1072]{2,1,0:T(8,128)(2,1)} %bitcast.85), calls=%async_computation.1 | async-start | bytes 1179648 | tf_op jit(solution)/shard_map/all_to_all | solution.py:217
  43.0 0.2 fusion.5
  43.4 0.9 fusion.43
  44.3 0.2 fusion.44
  44.6 0.2 fusion.26
  44.9 13.6 %all-to-all-done.1 = bf16[32,8,1072]{2,1,0:T(8,128)(2,1)S(1)} async-done(((bf16[32,8,1072]{2,1,0:T(8,128)(2,1)}), bf16[32,8,1072]{2,1,0:T(8,128)(2,1)S(1)}, u32[]{:S(2)}, u32[]{:S(2)}) %all-to-all-start.1) | async-done | bytes 548896 | tf_op jit(solution)/shard_map/all_to_all | solution.py:217
  59.0 0.3 fusion.13
  59.5 0.9 broadcast_in_dim.46
  60.4 7.7 %all-to-all-start.2 = ((bf16[32,8,1024]{2,1,0:T(8,128)(2,1)}), bf16[32,8,1024]{2,1,0:T(8,128)(2,1)S(1)}, u32[]{:S(2)}, u32[]{:S(2)}) async-start(bf16[32,8,1024]{2,1,0:T(8,128)(2,1)} %broadcast_in_dim.46), calls=%async_computation.2 | async-start | bytes 1048576 | tf_op jit(solution)/shard_map/all_to_all | solution.py:165
  68.2 0.6 copy-done.5
  68.9 0.6 copy-done.7
  69.5 0.9 fusion
  70.4 11.2 %all-to-all-done.2 = bf16[32,8,1024]{2,1,0:T(8,128)(2,1)S(1)} async-done(((bf16[32,8,1024]{2,1,0:T(8,128)(2,1)}), bf16[32,8,1024]{2,1,0:T(8,128)(2,1)S(1)}, u32[]{:S(2)}, u32[]{:S(2)}) %all-to-all-start.2) | async-done | bytes 524320 | tf_op jit(solution)/shard_map/all_to_all | solution.py:165
  81.7 1.0 %fusion.14 = f32[8,32,256]{2,1,0:T(8,128)} fusion(bf16[8,32,1024]{2,1,0:T(8,128)(2,1)S(1)} %bitcast.86, bf16[1024,256]{1,0:T(8,128)(2,1)S(1)} %copy-done), kind=kOutput, calls=%fused_computation.24 | convolution fusion | flops 134217728 | bytes 1310720 | tf_op jit(solution)/shard_map/dot_general | solution.py:233
  82.7 9.2 %all-to-all-start.3 = ((f32[8,32,256]{2,1,0:T(8,128)}), f32[8,32,256]{2,1,0:T(8,128)S(1)}, u32[]{:S(2)}, u32[]{:S(2)}) async-start(f32[8,32,256]{2,1,0:T(8,128)} %fusion.14), calls=%async_computation.3 | async-start | bytes 524288 | tf_op jit(solution)/shard_map/all_to_all | solution.py:235
  91.9 0.9 fusion.1
  92.8 5.6 %all-to-all-done.3 = f32[8,32,256]{2,1,0:T(8,128)S(1)} async-done(((f32[8,32,256]{2,1,0:T(8,128)}), f32[8,32,256]{2,1,0:T(8,128)S(1)}, u32[]{:S(2)}, u32[]{:S(2)}) %all-to-all-start.3) | async-done | bytes 262176 | tf_op jit(solution)/shard_map/all_to_all | solution.py:235
  98.4 0.6 reduce_sum.51
  (32 shorter events, 1.4 us)
Async XLA Ops:
  0.6 81.0 %copy-start = (bf16[1024,256]{1,0:T(8,128)(2,1)S(1)}, bf16[1024,256]{1,0:T(8,128)(2,1)}, u32[]{:S(2)}) copy-start(bf16[1024,256]{1,0:T(8,128)(2,1)} %param.15) | copy-start | bytes 1572868
  2.3 28.9 %all-to-all-start = ((bf16[32,8,1280]{2,1,0:T(8,128)(2,1)}), bf16[32,8,1280]{2,1,0:T(8,128)(2,1)S(1)}, u32[]{:S(2)}, u32[]{:S(2)}) async-start(bf16[32,8,1280]{2,1,0:T(8,128)(2,1)} %broadcast_in_dim.42), calls=%async_computation | async-start | bytes 1310720 | tf_op jit(solution)/shard_map/all_to_all | solution.py:165
  14.2 0.7 copy-start.6
  31.3 0.8 copy-start.1
  35.3 23.3 %all-to-all-start.1 = ((bf16[32,8,1072]{2,1,0:T(8,128)(2,1)}), bf16[32,8,1072]{2,1,0:T(8,128)(2,1)S(1)}, u32[]{:S(2)}, u32[]{:S(2)}) async-start(bf16[32,8,1072]{2,1,0:T(8,128)(2,1)} %bitcast.85), calls=%async_computation.1 | async-start | bytes 1179648 | tf_op jit(solution)/shard_map/all_to_all | solution.py:217
  43.3 0.9 copy-start.4
  60.4 9.1 %copy-start.2 = (bf16[4,128,128]{2,1,0:T(8,128)(2,1)S(1)}, bf16[4,128,128]{2,1,0:T(8,128)(2,1)}, u32[]{:S(2)}) copy-start(bf16[4,128,128]{2,1,0:T(8,128)(2,1)} %k_ref.1) | copy-start | bytes 393220
  60.4 21.3 %all-to-all-start.2 = ((bf16[32,8,1024]{2,1,0:T(8,128)(2,1)}), bf16[32,8,1024]{2,1,0:T(8,128)(2,1)S(1)}, u32[]{:S(2)}, u32[]{:S(2)}) async-start(bf16[32,8,1024]{2,1,0:T(8,128)(2,1)} %broadcast_in_dim.46), calls=%async_computation.2 | async-start | bytes 1048576 | tf_op jit(solution)/shard_map/all_to_all | solution.py:165
  68.1 0.7 copy-start.5
  68.8 0.7 copy-start.7
  82.7 9.2 %copy-start.3 = (bf16[4,128,128]{2,1,0:T(8,128)(2,1)S(1)}, bf16[4,128,128]{2,1,0:T(8,128)(2,1)}, u32[]{:S(2)}) copy-start(bf16[4,128,128]{2,1,0:T(8,128)(2,1)} %v_ref.1) | copy-start | bytes 393220
  82.7 15.7 %all-to-all-start.3 = ((f32[8,32,256]{2,1,0:T(8,128)}), f32[8,32,256]{2,1,0:T(8,128)S(1)}, u32[]{:S(2)}, u32[]{:S(2)}) async-start(f32[8,32,256]{2,1,0:T(8,128)} %fusion.14), calls=%async_computation.3 | async-start | bytes 524288 | tf_op jit(solution)/shard_map/all_to_all | solution.py:235

commit v5 on v4

--- a/solution.py
+++ b/solution.py
@@ -3,7 +3,7 @@
 import jax
 import jax.numpy as jnp
 from jax import lax
-from jax.sharding import PartitionSpec as P
+from jax.sharding import Mesh, PartitionSpec as P
 from jax.experimental import pallas as pl
 from jax.experimental.pallas import tpu as pltpu
 
@@ -102,61 +102,71 @@
     return hi, mid, lo
 
 
-def block_attention_kernel(limit_ref, q_ref, k_ref, v_ref, out_ref, stats_ref):
-    requests, block_len, _ = k_ref.shape
-    rows = out_ref.shape[0] // requests
+def block_attention_kernel(limit_ref, q_ref, kv_ref, out_ref, stats_ref):
+    blocks, block_len, _ = kv_ref.shape
+    rows = out_ref.shape[0]
     heads = stats_ref.shape[1] // 2
     score_scale = 1.0 / math.sqrt(HEAD_SIZE)
-    for r in range(requests):
-        q = jnp.concatenate(
-            [
-                q_ref[r * rows : (r + 1) * rows, h * HEAD_SIZE : (h + 1) * HEAD_SIZE]
-                for h in range(heads)
-            ],
-            axis=0,
-        )
-        scores = (
+    q = jnp.concatenate(
+        [q_ref[:, h * HEAD_SIZE : (h + 1) * HEAD_SIZE] for h in range(heads)], axis=0
+    )
+    scores = []
+    valids = []
+    for b in range(blocks):
+        s = (
             lax.dot_general(
-                q, k_ref[r], (((1,), (1,)), ((), ())), preferred_element_type=jnp.float32
+                q,
+                kv_ref[b, :, :HEAD_SIZE],
+                (((1,), (1,)), ((), ())),
+                preferred_element_type=jnp.float32,
             )
             * score_scale
         )
-        valid = lax.broadcasted_iota(jnp.int32, scores.shape, 1) < limit_ref[r]
-        scores = jnp.where(valid, scores, NEG_FLOOR)
-        peak = jnp.max(scores, axis=1, keepdims=True)
-        weights = jnp.where(valid, jnp.exp(scores - peak), 0.0)
-        total = jnp.sum(weights, axis=1, keepdims=True)
-        out = jnp.dot(
-            weights.astype(jnp.bfloat16), v_ref[r], preferred_element_type=jnp.float32
-        ).astype(out_ref.dtype)
-        for h in range(heads):
-            here = slice(h * rows, (h + 1) * rows)
-            out_ref[r * rows : (r + 1) * rows, h * HEAD_SIZE : (h + 1) * HEAD_SIZE] = out[here]
-            stats_ref[r * rows : (r + 1) * rows, h : h + 1] = peak[here]
-            stats_ref[r * rows : (r + 1) * rows, heads + h : heads + h + 1] = total[here]
+        valid = lax.broadcasted_iota(jnp.int32, s.shape, 1) < limit_ref[b]
+        scores.append(jnp.where(valid, s, NEG_FLOOR))
+        valids.append(valid)
+    peak = jnp.max(scores[0], axis=1, keepdims=True)
+    for s in scores[1:]:
+        peak = jnp.maximum(peak, jnp.max(s, axis=1, keepdims=True))
+    total = jnp.zeros_like(peak)
+    out = jnp.zeros((q.shape[0], HEAD_SIZE), jnp.float32)
+    for b in range(blocks):
+        weights = jnp.where(valids[b], jnp.exp(scores[b] - peak), 0.0)
+        total = total + jnp.sum(weights, axis=1, keepdims=True)
+        out = out + jnp.dot(
+            weights.astype(jnp.bfloat16),
+            kv_ref[b, :, HEAD_SIZE:],
+            preferred_element_type=jnp.float32,
+        )
+    out = out.astype(out_ref.dtype)
+    for h in range(heads):
+        here = slice(h * rows, (h + 1) * rows)
+        out_ref[:, h * HEAD_SIZE : (h + 1) * HEAD_SIZE] = out[here]
+        stats_ref[:, h : h + 1] = peak[here]
+        stats_ref[:, heads + h : heads + h + 1] = total[here]
     width = heads * HEAD_SIZE
     stats = stats_ref[...]
     for j, part in enumerate(split_three(stats)):
         out_ref[:, width + j * 2 * heads : width + (j + 1) * 2 * heads] = part
 
 
-def block_attention(limit, every_query, keys, values, width):
-    rows = every_query.shape[0]
+def block_attention(limit, group_rows, blocks_kv, width):
+    rows = group_rows.shape[0]
     heads = width // HEAD_SIZE
-    requests, block_len, _ = keys.shape
+    blocks, block_len, _ = blocks_kv.shape
     vmem = pl.BlockSpec(memory_space=pltpu.VMEM)
     return pl.pallas_call(
         block_attention_kernel,
         out_shape=jax.ShapeDtypeStruct((rows, width + 6 * heads), jnp.bfloat16),
-        in_specs=[pl.BlockSpec(memory_space=pltpu.SMEM), vmem, vmem, vmem],
+        in_specs=[pl.BlockSpec(memory_space=pltpu.SMEM), vmem, vmem],
         out_specs=vmem,
         scratch_shapes=[pltpu.VMEM((rows, 2 * heads), jnp.float32)],
         cost_estimate=pl.CostEstimate(
-            flops=4 * rows * heads * block_len * HEAD_SIZE,
-            transcendentals=rows * heads * block_len,
-            bytes_accessed=2 * (rows * width + 2 * requests * block_len * HEAD_SIZE + rows * (width + 6 * heads)),
+            flops=4 * rows * heads * blocks * block_len * HEAD_SIZE,
+            transcendentals=rows * heads * blocks * block_len,
+            bytes_accessed=2 * (rows * width + 2 * blocks * block_len * HEAD_SIZE + rows * (width + 6 * heads)),
         ),
-    )(limit, every_query, keys, values)
+    )(limit, group_rows, blocks_kv)
 
 
 def gather_rows(block, axis_name):
@@ -178,9 +188,12 @@
     accepted_nodes,
     accepted_count,
 ):
-    block_count = lax.axis_size("blk")
+    blk = ("bx", "bz")
     kv_count = lax.axis_size("kv")
-    my_block = lax.axis_index("blk")
+    ring = lax.axis_size("bz")
+    my_block = lax.axis_index(blk)
+    my_x = lax.axis_index("bx")
+    my_z = lax.axis_index("bz")
     rows_dev, width_q = queries.shape
     requests = lengths.shape[0]
     cache_width = cached_key_vectors.shape[2]
@@ -188,34 +201,36 @@
     query_group_width = width_q // (kv_local * HEAD_SIZE)
     block_len = cached_key_vectors.shape[1]
     score_scale = 1.0 / math.sqrt(HEAD_SIZE)
-    leading_row = my_block * rows_dev
-    my_request = leading_row // TREE_TOKENS
-    node_start = leading_row - my_request * TREE_TOKENS
+    my_request = my_x
+    node_start = my_z * rows_dev
     local_queries = queries.reshape(1, rows_dev, kv_local, query_group_width, HEAD_SIZE)
-    packed = gather_rows(
-        jnp.concatenate([queries, draft_token_keys, draft_token_values], axis=1), "blk"
-    )
-    every_query = packed[:, :width_q]
-    gathered_keys = packed[:, width_q : width_q + cache_width]
-    gathered_values = packed[:, width_q + cache_width :]
-    tree_keys = lax.dynamic_slice_in_dim(
-        gathered_keys, my_request * TREE_TOKENS, TREE_TOKENS, 0
-    ).reshape(1, 1, TREE_TOKENS, kv_local, HEAD_SIZE)
-    tree_values = lax.dynamic_slice_in_dim(
-        gathered_values, my_request * TREE_TOKENS, TREE_TOKENS, 0
-    ).reshape(1, 1, TREE_TOKENS, kv_local, HEAD_SIZE)
+    own_draft = jnp.concatenate([draft_token_keys, draft_token_values], axis=1)
+    group_rows = gather_rows(jnp.concatenate([queries, own_draft], axis=1), "bz")
+    blocks_kv = lax.all_to_all(
+        jnp.concatenate([cached_key_vectors, cached_value_vectors], axis=2),
+        "bx",
+        split_axis=0,
+        concat_axis=0,
+        tiled=True,
+    )
+    tree_keys = group_rows[:, width_q : width_q + cache_width].reshape(
+        1, 1, TREE_TOKENS, kv_local, HEAD_SIZE
+    )
+    tree_values = group_rows[:, width_q + cache_width :].reshape(
+        1, 1, TREE_TOKENS, kv_local, HEAD_SIZE
+    )
     reachable = ancestors(lax.dynamic_slice_in_dim(parents, my_request, 1, 0))
     own_reach = lax.dynamic_slice_in_dim(reachable, node_start, rows_dev, 1)
     draft_usable = (own_reach > 0.5)[None, :, None, None, :, :]
     draft_part = partial_softmax(local_queries, tree_keys, tree_values, draft_usable, score_scale)
-    limit = lengths - my_block * block_len
-    packed_out = block_attention(
-        limit, packed, cached_key_vectors, cached_value_vectors, width_q
-    )
+    source_blocks = jnp.arange(blocks_kv.shape[0], dtype=jnp.int32) * ring + my_z
+    limit = lengths[my_request] - source_blocks * block_len
+    packed_out = block_attention(limit, group_rows, blocks_kv, width_q)
     head_count = width_q // HEAD_SIZE
     width_out = width_q
-    moved = lax.all_to_all(packed_out, "blk", split_axis=0, concat_axis=0, tiled=True)
-    moved = moved.reshape(block_count, rows_dev, -1)
+    moved = lax.all_to_all(
+        packed_out.reshape(ring, rows_dev, -1), "bz", split_axis=0, concat_axis=0, tiled=True
+    )
     parts = [
         moved[..., width_out + j * 2 * head_count : width_out + (j + 1) * 2 * head_count].astype(
             jnp.float32
@@ -229,8 +244,10 @@
         moved_stats[..., head_count:],
     )
     attention = merge_parts(cache_part, draft_part, HEAD_SIZE)
-    every_row = gather_rows(attention, "blk")
-    partial = jnp.dot(every_row, out_weight, preferred_element_type=jnp.float32)
+    every_row = gather_rows(jnp.concatenate([attention, own_draft], axis=1), blk)
+    gathered_keys = every_row[:, width_q : width_q + cache_width]
+    gathered_values = every_row[:, width_q + cache_width :]
+    partial = jnp.dot(every_row[:, :width_q], out_weight, preferred_element_type=jnp.float32)
     out_rows = partial.shape[0] // kv_count
     arrived = lax.all_to_all(
         partial.reshape(kv_count, out_rows, partial.shape[1]),
@@ -261,21 +278,26 @@
 
 
 def solution(mesh):
+    kv_size, blk_size = mesh.devices.shape
+    requests = 4
+    ring = blk_size // requests
+    grid_mesh = Mesh(mesh.devices.reshape(kv_size, requests, ring), ("kv", "bx", "bz"))
+    blk = ("bx", "bz")
     return jax.shard_map(
         on_device,
-        mesh=mesh,
+        mesh=grid_mesh,
         in_specs=(
-            P("blk", "kv"),
-            P("blk", "kv"),
-            P("blk", "kv"),
-            P(None, "blk", "kv"),
-            P(None, "blk", "kv"),
-            P("kv", "blk"),
+            P(blk, "kv"),
+            P(blk, "kv"),
+            P(blk, "kv"),
+            P(None, blk, "kv"),
+            P(None, blk, "kv"),
+            P("kv", blk),
             P(),
             P(),
             P(),
             P(),
         ),
-        out_specs=(P("kv", "blk"), P(None, "blk", "kv"), P(None, "blk", "kv")),
+        out_specs=(P("kv", blk), P(None, blk, "kv"), P(None, blk, "kv")),
         check_vma=False,
     )

time: 99.6 us -> 85.6 us (0.86)
  waiting for transfers between devices: 44.7 us -> 33.7 us
  starting transfers between devices: 36.5 us -> 31.8 us
  matrix products: 4.14 us -> 5.57 us
  other arithmetic: 3.18 us -> 4.52 us
    all_to_all x2, starting transfers between devices: 19.6 us -> 12.1 us  [gather_rows(): lax.all_to_all(spread, axis_name, split_axis=0, concat_axis=0, tiled=True)]
    all_to_all x1 -> x2, waiting for transfers between devices: 13.6 us -> 8.25 us  [the longest x1 6.73 us: on_device(): lax.all_to_all(packed_out.reshape(ring, rows_dev, -1), 'bz', split_axis=0...]
    all_to_all x2, waiting for transfers between devices: 25.5 us -> 20.8 us  [gather_rows(): lax.all_to_all(spread, axis_name, split_axis=0, concat_axis=0, tiled=True)]
    all_to_all x1, starting transfers between devices: 9.22 us -> 11.5 us  [on_device(): lax.all_to_all(partial.reshape(kv_count, out_rows, partial.shape[1]), 'kv...]
    all_to_all x1 -> x2, starting transfers between devices: 7.72 us -> 8.21 us  [the longest x1 4.83 us: on_device(): lax.all_to_all(jnp.concatenate([cached_key_vectors, cached_value_vectors]...]
    unnamed x16 -> x22, local copies, waits for them, and re-layouts: 2.68 us -> 2.3 us
  transfers between devices with their start and end apart: 4 -> 5, of which waited for: 4 -> 5; matrix products, arithmetic and copies ran while one was open for 6% -> 8% of each run, Pallas kernels for 0% -> 0%
where the time goes in v5:
time: 85.6 us; the launch traced here: 84.7 us
  waiting for transfers between devices  33.7 us (39%)
  starting transfers between devices  31.8 us (37%)
  local copies, waits for them, and re-layouts  5.67 us (7%)
  matrix products  5.57 us (7%)
  other arithmetic  4.52 us (5%)
  Pallas kernels  2.62 us (3%)
    all_to_all x2, waiting for transfers between devices, gather_rows(): lax.all_to_all(spread, axis_name, split_axis=0, concat_axis=0, tiled=True)  20.8 us
    all_to_all x2, starting transfers between devices, gather_rows(): lax.all_to_all(spread, axis_name, split_axis=0, concat_axis=0, tiled=True)  12.1 us
    all_to_all x1, starting transfers between devices, on_device(): lax.all_to_all(partial.reshape(kv_count, out_rows, partial.shape[1]), 'kv...  11.5 us
    all_to_all x1, waiting for transfers between devices, on_device(): lax.all_to_all(packed_out.reshape(ring, rows_dev, -1), 'bz', split_axis=0...  6.73 us
    all_to_all x1, starting transfers between devices, on_device(): lax.all_to_all(jnp.concatenate([cached_key_vectors, cached_value_vectors]...  4.83 us
    all_to_all x1, waiting for transfers between devices, on_device(): lax.all_to_all(partial.reshape(kv_count, out_rows, partial.shape[1]), 'kv...  4.64 us
    all_to_all x1, starting transfers between devices, on_device(): lax.all_to_all(packed_out.reshape(ring, rows_dev, -1), 'bz', split_axis=0...  3.38 us
    pallas_call x1, Pallas kernels, block_attention(): pl.pallas_call(block_attention_kernel, out_shape=jax.ShapeDtypeStruct((ro...  2.62 us
  transfers between devices with their start and end apart: 5, of which 5 were waited for; matrix products, arithmetic and copies ran while one was open for 8% of the time, Pallas kernels for 0%

profile of v5, /device:TPU:1, one launch (start us, length us, event | category | flops | bytes accessed | tf_op | source)
XLA Modules:
  0.0 84.7 jit_solution(18358181989243718893)
XLA Ops:
  0.6 1.8 %pad_maximum_fusion = bf16[4,128,256]{2,1,0:T(8,128)(2,1)} fusion(bf16[4,128,128]{2,1,0:T(8,128)(2,1)} %param.14, bf16[4,128,128]{2,1,0:T(8,128)(2,1)} %param.13), kind=kLoop, calls=%fused_computation.24 | loop fusion | flops 524288 | bytes 524288 | tf_op jit(solution)/shard_map/concatenate | solution.py:210
  2.4 4.8 %all-to-all-start.1 = ((bf16[4,128,256]{2,1,0:T(8,128)(2,1)}), bf16[4,128,256]{2,1,0:T(8,128)(2,1)S(1)}, u32[]{:S(2)}, u32[]{:S(2)}) async-start(bf16[4,128,256]{2,1,0:T(8,128)(2,1)} %pad_maximum_fusion), calls=%async_computation.1 | async-start | bytes 524288 | tf_op jit(solution)/shard_map/all_to_all | solution.py:209
  7.2 0.7 fusion.35
  7.9 0.2 fusion.23
  8.1 0.2 fusion.10
  8.3 0.2 fusion.2
  8.6 0.2 fusion.4
  9.0 0.4 copy-done.9
  9.5 0.6 dynamic_slice.7
  10.1 1.2 %multiply_subtract_fusion.limit_ref = s32[4]{0:T(128)} fusion(s32[]{:T(128)S(6)} %axis_index.33, s32[]{:T(128)} %bitcast), kind=kLoop, calls=%fused_computation.72 | loop fusion | flops 16 | bytes 24 | tf_op jit(solution)/shard_map/sub | solution.py:227
  11.2 1.5 %all-to-all-done.1.kv_ref = bf16[4,128,256]{2,1,0:T(8,128)(2,1)S(1)} async-done(((bf16[4,128,256]{2,1,0:T(8,128)(2,1)}), bf16[4,128,256]{2,1,0:T(8,128)(2,1)S(1)}, u32[]{:S(2)}, u32[]{:S(2)}) %all-to-all-start.1) | async-done | bytes 262176 | tf_op jit(solution)/shard_map/all_to_all | solution.py:209
  12.8 0.7 broadcast_in_dim.42
  13.5 8.2 %all-to-all-start = ((bf16[8,8,1280]{2,1,0:T(8,128)(2,1)}), bf16[8,8,1280]{2,1,0:T(8,128)(2,1)S(1)}, u32[]{:S(2)}, u32[]{:S(2)}) async-start(bf16[8,8,1280]{2,1,0:T(8,128)(2,1)} %broadcast_in_dim.42), calls=%async_computation | async-start | bytes 327680 | tf_op jit(solution)/shard_map/all_to_all | solution.py:175
  21.9 8.2 %all-to-all-done = bf16[8,8,1280]{2,1,0:T(8,128)(2,1)S(1)} async-done(((bf16[8,8,1280]{2,1,0:T(8,128)(2,1)}), bf16[8,8,1280]{2,1,0:T(8,128)(2,1)S(1)}, u32[]{:S(2)}, u32[]{:S(2)}) %all-to-all-start) | async-done | bytes 163872 | tf_op jit(solution)/shard_map/all_to_all | solution.py:175
  30.1 0.7 copy-done.2
  30.7 2.6 %shard_map.121 = bf16[64,1072]{1,0:T(8,128)(2,1)} custom-call(s32[4]{0:T(128)} %multiply_subtract_fusion.limit_ref, bf16[64,1280]{1,0:T(8,128)(2,1)} %bitcast.84, bf16[4,128,256]{2,1,0:T(8,128)(2,1)} %copy-done.1), custom_call_target="tpu_custom_call" | custom-call | flops 134217728 | bytes 530432 | tf_op jit(solution)/shard_map/pallas_call | solution.py:158
  33.3 3.4 %all-to-all-start.2 = ((bf16[8,8,1072]{2,1,0:T(8,128)(2,1)}), bf16[8,8,1072]{2,1,0:T(8,128)(2,1)S(1)}, u32[]{:S(2)}, u32[]{:S(2)}) async-start(bf16[8,8,1072]{2,1,0:T(8,128)(2,1)} %bitcast.87), calls=%async_computation.2 | async-start | bytes 294912 | tf_op jit(solution)/shard_map/all_to_all | solution.py:231
  36.7 0.9 %fusion.38 = (f32[8,8]{0,1:T(8,128)S(1)}, f32[1,1,1,8,8,64]{5,3,4,0,2,1:T(8,128)S(1)}) fusion(bf16[8,8,128]{2,0,1:T(8,128)(2,1)S(1)} %bitcast.88, bf16[64,1280]{1,0:T(8,128)(2,1)} %bitcast.85, pred[8,64]{1,0:T(8,128)(4,1)S(1)} %fusion.32), kind=kOutput, calls=%fused_computation.74 | convolution fusion | flops 1060800 | bytes 49920 | tf_op jit(solution)/shard_map/rtkgh,rbpkh->brkgtp/dot_general | solution.py:35
  37.7 0.2 fusion.26
  38.1 6.7 %all-to-all-done.2 = bf16[8,8,1072]{2,1,0:T(8,128)(2,1)S(1)} async-done(((bf16[8,8,1072]{2,1,0:T(8,128)(2,1)}), bf16[8,8,1072]{2,1,0:T(8,128)(2,1)S(1)}, u32[]{:S(2)}, u32[]{:S(2)}) %all-to-all-start.2) | async-done | bytes 137248 | tf_op jit(solution)/shard_map/all_to_all | solution.py:231
  45.4 0.8 fusion.11
  46.3 0.9 %broadcast_in_dim.46 = bf16[32,8,1280]{2,1,0:T(8,128)(2,1)} broadcast(bf16[8,1280]{1,0:T(8,128)(2,1)S(1)} %pad_maximum_fusion.1), dimensions={1,2} | broadcast | bytes 675840 | tf_op jit(solution)/shard_map/broadcast_in_dim | solution.py:174
  47.1 3.9 %all-to-all-start.3 = ((bf16[32,8,1280]{2,1,0:T(8,128)(2,1)}), bf16[32,8,1280]{2,1,0:T(8,128)(2,1)S(1)}, u32[]{:S(2)}, u32[]{:S(2)}) async-start(bf16[32,8,1280]{2,1,0:T(8,128)(2,1)} %broadcast_in_dim.46), calls=%async_computation.3 | async-start | bytes 1310720 | tf_op jit(solution)/shard_map/all_to_all | solution.py:175
  51.2 0.6 copy-done.8
  51.8 0.6 copy-done.10
  52.5 12.7 %all-to-all-done.3 = bf16[32,8,1280]{2,1,0:T(8,128)(2,1)S(1)} async-done(((bf16[32,8,1280]{2,1,0:T(8,128)(2,1)}), bf16[32,8,1280]{2,1,0:T(8,128)(2,1)S(1)}, u32[]{:S(2)}, u32[]{:S(2)}) %all-to-all-start.3) | async-done | bytes 655392 | tf_op jit(solution)/shard_map/all_to_all | solution.py:175
  65.2 1.0 %fusion.13 = f32[256,256]{1,0:T(8,128)} fusion(bf16[1024,256]{1,0:T(8,128)(2,1)S(1)} %copy-done, bf16[256,1280]{1,0:T(8,128)(2,1)S(1)} %bitcast.83), kind=kOutput, calls=%fused_computation.22 | convolution fusion | flops 134217728 | bytes 1310720 | tf_op jit(solution)/shard_map/dot_general | solution.py:250
  66.2 11.5 %all-to-all-start.4 = ((f32[8,32,256]{2,1,0:T(8,128)}), f32[8,32,256]{2,1,0:T(8,128)S(1)}, u32[]{:S(2)}, u32[]{:S(2)}) async-start(f32[8,32,256]{2,1,0:T(8,128)} %bitcast.24), calls=%async_computation.4 | async-start | bytes 524288 | tf_op jit(solution)/shard_map/all_to_all | solution.py:252
  77.7 0.9 %fusion = bf16[4,128,128]{2,1,0:T(8,128)(2,1)} fusion(bf16[4,128,128]{2,1,0:T(8,128)(2,1)S(1)} %copy-done.3, bf16[4,64,128]{2,1,0:T(8,128)(2,1)S(1)} %bitcast.90, pred[4,128]{1,0:T(4,128)(4,1)S(1)} %compare_and_fusion, s32[4,128]{1,0:T(4,128)S(1)} %select_reduce_fusion), kind=kOutput, calls=%fused_computation.2 | convolution fusion | flops 8585216 | bytes 330240 | tf_op jit(solution)/shard_map/rps,rsc->rpc/dot_general | solution.py:91
  78.6 0.9 %fusion.1 = bf16[4,128,128]{2,1,0:T(8,128)(2,1)} fusion(bf16[4,128,128]{2,1,0:T(8,128)(2,1)S(1)} %copy-done.4, bf16[4,64,128]{2,1,0:T(8,128)(2,1)S(1)} %bitcast.89, pred[4,128]{1,0:T(4,128)(4,1)S(1)} %compare_and_fusion, s32[4,128]{1,0:T(4,128)S(1)} %select_reduce_fusion), kind=kOutput, calls=%fused_computation.3 | convolution fusion | flops 8585216 | bytes 330240 | tf_op jit(solution)/shard_map/rps,rsc->rpc/dot_general | solution.py:91
  79.5 4.6 %all-to-all-done.4 = f32[8,32,256]{2,1,0:T(8,128)S(1)} async-done(((f32[8,32,256]{2,1,0:T(8,128)}), f32[8,32,256]{2,1,0:T(8,128)S(1)}, u32[]{:S(2)}, u32[]{:S(2)}) %all-to-all-start.4) | async-done | bytes 262176 | tf_op jit(solution)/shard_map/all_to_all | solution.py:252
  84.1 0.6 reduce_sum.51
  (43 shorter events, 1.6 us)
Async XLA Ops:
  0.6 64.5 %copy-start = (bf16[1024,256]{1,0:T(8,128)(2,1)S(1)}, bf16[1024,256]{1,0:T(8,128)(2,1)}, u32[]{:S(2)}) copy-start(bf16[1024,256]{1,0:T(8,128)(2,1)} %param.15) | copy-start | bytes 1572868
  2.4 10.4 %all-to-all-start.1 = ((bf16[4,128,256]{2,1,0:T(8,128)(2,1)}), bf16[4,128,256]{2,1,0:T(8,128)(2,1)S(1)}, u32[]{:S(2)}, u32[]{:S(2)}) async-start(bf16[4,128,256]{2,1,0:T(8,128)(2,1)} %pad_maximum_fusion), calls=%async_computation.1 | async-start | bytes 524288 | tf_op jit(solution)/shard_map/all_to_all | solution.py:209
  8.8 0.7 copy-start.9
  8.8 2.4 %copy-start.6 = (bf16[8,128]{1,0:T(8,128)(2,1)S(1)}, bf16[8,128]{1,0:T(8,128)(2,1)}, u32[]{:S(2)}) copy-start(bf16[8,128]{1,0:T(8,128)(2,1)} %param.12) | copy-start | bytes 6148
  8.8 2.4 %copy-start.7 = (bf16[8,128]{1,0:T(8,128)(2,1)S(1)}, bf16[8,128]{1,0:T(8,128)(2,1)}, u32[]{:S(2)}) copy-start(bf16[8,128]{1,0:T(8,128)(2,1)} %param.11) | copy-start | bytes 6148
  9.0 2.2 %copy-start.5 = (bf16[8,1024]{1,0:T(8,128)(2,1)S(1)}, bf16[8,1024]{1,0:T(8,128)(2,1)}, u32[]{:S(2)}) copy-start(bf16[8,1024]{1,0:T(8,128)(2,1)} %param.10) | copy-start | bytes 49156
  12.8 9.1 %copy-start.1 = (bf16[4,128,256]{2,1,0:T(8,128)(2,1)}, bf16[4,128,256]{2,1,0:T(8,128)(2,1)S(1)}, u32[]{:S(2)}) copy-start(bf16[4,128,256]{2,1,0:T(8,128)(2,1)S(1)} %all-to-all-done.1.kv_ref) | copy-start | bytes 786436
  13.5 16.6 %all-to-all-start = ((bf16[8,8,1280]{2,1,0:T(8,128)(2,1)}), bf16[8,8,1280]{2,1,0:T(8,128)(2,1)S(1)}, u32[]{:S(2)}, u32[]{:S(2)}) async-start(bf16[8,8,1280]{2,1,0:T(8,128)(2,1)} %broadcast_in_dim.42), calls=%async_computation | async-start | bytes 327680 | tf_op jit(solution)/shard_map/all_to_all | solution.py:175
  30.1 0.7 copy-start.2
  33.3 11.5 %all-to-all-start.2 = ((bf16[8,8,1072]{2,1,0:T(8,128)(2,1)}), bf16[8,8,1072]{2,1,0:T(8,128)(2,1)S(1)}, u32[]{:S(2)}, u32[]{:S(2)}) async-start(bf16[8,8,1072]{2,1,0:T(8,128)(2,1)} %bitcast.87), calls=%async_computation.2 | async-start | bytes 294912 | tf_op jit(solution)/shard_map/all_to_all | solution.py:231
  47.1 18.0 %all-to-all-start.3 = ((bf16[32,8,1280]{2,1,0:T(8,128)(2,1)}), bf16[32,8,1280]{2,1,0:T(8,128)(2,1)S(1)}, u32[]{:S(2)}, u32[]{:S(2)}) async-start(bf16[32,8,1280]{2,1,0:T(8,128)(2,1)} %broadcast_in_dim.46), calls=%async_computation.3 | async-start | bytes 1310720 | tf_op jit(solution)/shard_map/all_to_all | solution.py:175
  51.1 0.7 copy-start.8
  51.7 0.7 copy-start.10
  66.2 11.5 %copy-start.3 = (bf16[4,128,128]{2,1,0:T(8,128)(2,1)S(1)}, bf16[4,128,128]{2,1,0:T(8,128)(2,1)}, u32[]{:S(2)}) copy-start(bf16[4,128,128]{2,1,0:T(8,128)(2,1)} %param.13) | copy-start | bytes 393220
  66.2 18.0 %all-to-all-start.4 = ((f32[8,32,256]{2,1,0:T(8,128)}), f32[8,32,256]{2,1,0:T(8,128)S(1)}, u32[]{:S(2)}, u32[]{:S(2)}) async-start(f32[8,32,256]{2,1,0:T(8,128)} %bitcast.24), calls=%async_computation.4 | async-start | bytes 524288 | tf_op jit(solution)/shard_map/all_to_all | solution.py:252
  77.7 0.9 %copy-start.4 = (bf16[4,128,128]{2,1,0:T(8,128)(2,1)S(1)}, bf16[4,128,128]{2,1,0:T(8,128)(2,1)}, u32[]{:S(2)}) copy-start(bf16[4,128,128]{2,1,0:T(8,128)(2,1)} %param.14) | copy-start | bytes 393220

commit v6 on v5

--- a/solution.py
+++ b/solution.py
@@ -206,8 +206,10 @@
     local_queries = queries.reshape(1, rows_dev, kv_local, query_group_width, HEAD_SIZE)
     own_draft = jnp.concatenate([draft_token_keys, draft_token_values], axis=1)
     group_rows = gather_rows(jnp.concatenate([queries, own_draft], axis=1), "bz")
+    cache_pair = jnp.concatenate([cached_key_vectors, cached_value_vectors], axis=2)
+    group_rows, cache_pair = lax.optimization_barrier((group_rows, cache_pair))
     blocks_kv = lax.all_to_all(
-        jnp.concatenate([cached_key_vectors, cached_value_vectors], axis=2),
+        cache_pair,
         "bx",
         split_axis=0,
         concat_axis=0,

time: 85.6 us -> 85 us (level)
  waiting for transfers between devices: 33.7 us -> 32.4 us
  local copies, waits for them, and re-layouts: 5.67 us -> 6.55 us
    all_to_all x2, waiting for transfers between devices: 20.8 us -> 16.8 us  [gather_rows(): lax.all_to_all(spread, axis_name, split_axis=0, concat_axis=0, tiled=True)]
    all_to_all x1, waiting for transfers between devices: 1.53 us -> 4.36 us  [on_device(): lax.all_to_all(cache_pair, 'bx', split_axis=0, concat_axis=0, tiled=True)]
    concatenate x1, other arithmetic: 1.76 us -> 0.73 us  [on_device(): jnp.concatenate([cached_key_vectors, cached_value_vectors], axis=2)]
    unnamed x22, local copies, waits for them, and re-layouts: 2.3 us -> 3.21 us
  transfers between devices with their start and end apart: 5 -> 5, of which waited for: 5 -> 5; matrix products, arithmetic and copies ran while one was open for 8% -> 9% of each run, Pallas kernels for 0% -> 0%
where the time goes in v6:
time: 85 us; the launch traced here: 84.2 us
  waiting for transfers between devices  32.4 us (38%)
  starting transfers between devices  31.9 us (38%)
  local copies, waits for them, and re-layouts  6.55 us (8%)
  matrix products  5.58 us (7%)
  other arithmetic  4.29 us (5%)
  Pallas kernels  2.62 us (3%)
  between operations  0.86 us (1%)
    all_to_all x2, waiting for transfers between devices, gather_rows(): lax.all_to_all(spread, axis_name, split_axis=0, concat_axis=0, tiled=True)  16.8 us
    all_to_all x2, starting transfers between devices, gather_rows(): lax.all_to_all(spread, axis_name, split_axis=0, concat_axis=0, tiled=True)  12.9 us
    all_to_all x1, starting transfers between devices, on_device(): lax.all_to_all(partial.reshape(kv_count, out_rows, partial.shape[1]), 'kv...  11.5 us
    all_to_all x1, waiting for transfers between devices, on_device(): lax.all_to_all(packed_out.reshape(ring, rows_dev, -1), 'bz', split_axis=0...  6.62 us
    all_to_all x1, waiting for transfers between devices, on_device(): lax.all_to_all(partial.reshape(kv_count, out_rows, partial.shape[1]), 'kv...  4.64 us
    all_to_all x1, waiting for transfers between devices, on_device(): lax.all_to_all(cache_pair, 'bx', split_axis=0, concat_axis=0, tiled=True)  4.36 us
    all_to_all x1, starting transfers between devices, on_device(): lax.all_to_all(cache_pair, 'bx', split_axis=0, concat_axis=0, tiled=True)  4.01 us
    all_to_all x1, starting transfers between devices, on_device(): lax.all_to_all(packed_out.reshape(ring, rows_dev, -1), 'bz', split_axis=0...  3.51 us
  transfers between devices with their start and end apart: 5, of which 5 were waited for; matrix products, arithmetic and copies ran while one was open for 9% of the time, Pallas kernels for 0%

profile of v6, /device:TPU:1, one launch (start us, length us, event | category | flops | bytes accessed | tf_op | source)
XLA Modules:
  0.0 84.2 jit_solution(12846361813218941350)
XLA Ops:
  0.6 0.8 pad_maximum_fusion.2
  1.5 0.7 broadcast_in_dim.42
  2.1 9.0 %all-to-all-start = ((bf16[8,8,1280]{2,1,0:T(8,128)(2,1)}), bf16[8,8,1280]{2,1,0:T(8,128)(2,1)S(1)}, u32[]{:S(2)}, u32[]{:S(2)}) async-start(bf16[8,8,1280]{2,1,0:T(8,128)(2,1)} %broadcast_in_dim.42), calls=%async_computation | async-start | bytes 327680 | tf_op jit(solution)/shard_map/all_to_all | solution.py:175
  11.1 0.7 fusion.39
  11.8 0.2 fusion.23
  12.0 0.2 fusion.10
  12.9 0.6 copy-done.9
  13.6 0.6 dynamic_slice.7
  14.2 0.7 pad_maximum_fusion
  15.1 4.3 %all-to-all-done = bf16[8,8,1280]{2,1,0:T(8,128)(2,1)S(1)} async-done(((bf16[8,8,1280]{2,1,0:T(8,128)(2,1)}), bf16[8,8,1280]{2,1,0:T(8,128)(2,1)S(1)}, u32[]{:S(2)}, u32[]{:S(2)}) %all-to-all-start) | async-done | bytes 163872 | tf_op jit(solution)/shard_map/all_to_all | solution.py:175
  19.4 0.7 copy-done.2
  20.0 4.0 %all-to-all-start.1 = ((bf16[4,128,256]{2,1,0:T(8,128)(2,1)}), bf16[4,128,256]{2,1,0:T(8,128)(2,1)S(1)}, u32[]{:S(2)}, u32[]{:S(2)}) async-start(bf16[4,128,256]{2,1,0:T(8,128)(2,1)} %pad_maximum_fusion), calls=%async_computation.1 | async-start | bytes 524288 | tf_op jit(solution)/shard_map/all_to_all | solution.py:211
  24.0 1.2 %multiply_subtract_fusion.limit_ref = s32[4]{0:T(128)} fusion(s32[]{:T(128)S(6)} %axis_index.33, s32[]{:T(128)} %bitcast), kind=kLoop, calls=%fused_computation.74 | loop fusion | flops 16 | bytes 24 | tf_op jit(solution)/shard_map/sub | solution.py:229
  25.2 4.4 %all-to-all-done.1.kv_ref = bf16[4,128,256]{2,1,0:T(8,128)(2,1)S(1)} async-done(((bf16[4,128,256]{2,1,0:T(8,128)(2,1)}), bf16[4,128,256]{2,1,0:T(8,128)(2,1)S(1)}, u32[]{:S(2)}, u32[]{:S(2)}) %all-to-all-start.1) | async-done | bytes 262176 | tf_op jit(solution)/shard_map/all_to_all | solution.py:211
  29.6 0.7 copy-done.1
  30.3 2.6 %shard_map.121 = bf16[64,1072]{1,0:T(8,128)(2,1)} custom-call(s32[4]{0:T(128)} %multiply_subtract_fusion.limit_ref, bf16[64,1280]{1,0:T(8,128)(2,1)} %bitcast.84, bf16[4,128,256]{2,1,0:T(8,128)(2,1)} %copy-done.1), custom_call_target="tpu_custom_call" | custom-call | flops 134217728 | bytes 530432 | tf_op jit(solution)/shard_map/pallas_call | solution.py:158
  32.9 3.5 %all-to-all-start.2 = ((bf16[8,8,1072]{2,1,0:T(8,128)(2,1)}), bf16[8,8,1072]{2,1,0:T(8,128)(2,1)S(1)}, u32[]{:S(2)}, u32[]{:S(2)}) async-start(bf16[8,8,1072]{2,1,0:T(8,128)(2,1)} %bitcast.87), calls=%async_computation.2 | async-start | bytes 294912 | tf_op jit(solution)/shard_map/all_to_all | solution.py:233
  36.4 0.9 %fusion.42 = (f32[8,8]{0,1:T(8,128)S(1)}, f32[1,1,1,8,8,64]{5,3,4,0,2,1:T(8,128)S(1)}) fusion(bf16[8,8,128]{2,0,1:T(8,128)(2,1)S(1)} %bitcast.88, bf16[64,1280]{1,0:T(8,128)(2,1)} %bitcast.85, pred[8,64]{1,0:T(8,128)(4,1)S(1)} %fusion.36), kind=kOutput, calls=%fused_computation.76 | convolution fusion | flops 1060800 | bytes 49920 | tf_op jit(solution)/shard_map/rtkgh,rbpkh->brkgtp/dot_general | solution.py:35
  37.4 0.2 fusion.26
  37.8 6.6 %all-to-all-done.2 = bf16[8,8,1072]{2,1,0:T(8,128)(2,1)S(1)} async-done(((bf16[8,8,1072]{2,1,0:T(8,128)(2,1)}), bf16[8,8,1072]{2,1,0:T(8,128)(2,1)S(1)}, u32[]{:S(2)}, u32[]{:S(2)}) %all-to-all-start.2) | async-done | bytes 137248 | tf_op jit(solution)/shard_map/all_to_all | solution.py:233
  45.0 0.8 %fusion.11 = bf16[8,1024]{1,0:T(8,128)(2,1)S(1)} fusion(f32[8,1024]{1,0:T(8,128)S(1)} %fusion.15, bf16[8,8,64]{2,0,1:T(8,128)(2,1)S(1)} %get-tuple-element.14, f32[8,8]{0,1:T(8,128)S(1)} %copy.38, bf16[64,1280]{1,0:T(8,128)(2,1)} %bitcast.86, f32[8,8]{0,1:T(8,128)S(1)} %copy.34), kind=kOutput, calls=%fused_computation.20 | convolution fusion | flops 1081344 | bytes 74240 | tf_op jit(solution)/shard_map/brkgtp,rbpkh->brtkgh/dot_general | solution.py:44
  45.9 0.9 %broadcast_in_dim.46 = bf16[32,8,1280]{2,1,0:T(8,128)(2,1)} broadcast(bf16[8,1280]{1,0:T(8,128)(2,1)S(1)} %pad_maximum_fusion.1), dimensions={1,2} | broadcast | bytes 675840 | tf_op jit(solution)/shard_map/broadcast_in_dim | solution.py:174
  46.8 3.9 %all-to-all-start.3 = ((bf16[32,8,1280]{2,1,0:T(8,128)(2,1)}), bf16[32,8,1280]{2,1,0:T(8,128)(2,1)S(1)}, u32[]{:S(2)}, u32[]{:S(2)}) async-start(bf16[32,8,1280]{2,1,0:T(8,128)(2,1)} %broadcast_in_dim.46), calls=%async_computation.3 | async-start | bytes 1310720 | tf_op jit(solution)/shard_map/all_to_all | solution.py:175
  50.8 0.6 copy-done.8
  51.5 0.6 copy-done.10
  52.1 12.5 %all-to-all-done.3 = bf16[32,8,1280]{2,1,0:T(8,128)(2,1)S(1)} async-done(((bf16[32,8,1280]{2,1,0:T(8,128)(2,1)}), bf16[32,8,1280]{2,1,0:T(8,128)(2,1)S(1)}, u32[]{:S(2)}, u32[]{:S(2)}) %all-to-all-start.3) | async-done | bytes 655392 | tf_op jit(solution)/shard_map/all_to_all | solution.py:175
  64.6 1.0 %fusion.13 = f32[256,256]{1,0:T(8,128)} fusion(bf16[1024,256]{1,0:T(8,128)(2,1)S(1)} %copy-done, bf16[256,1280]{1,0:T(8,128)(2,1)S(1)} %bitcast.83), kind=kOutput, calls=%fused_computation.22 | convolution fusion | flops 134217728 | bytes 1310720 | tf_op jit(solution)/shard_map/dot_general | solution.py:252
  65.6 11.5 %all-to-all-start.4 = ((f32[8,32,256]{2,1,0:T(8,128)}), f32[8,32,256]{2,1,0:T(8,128)S(1)}, u32[]{:S(2)}, u32[]{:S(2)}) async-start(f32[8,32,256]{2,1,0:T(8,128)} %bitcast.24), calls=%async_computation.4 | async-start | bytes 524288 | tf_op jit(solution)/shard_map/all_to_all | solution.py:254
  77.1 0.9 %fusion = bf16[4,128,128]{2,1,0:T(8,128)(2,1)} fusion(bf16[4,128,128]{2,1,0:T(8,128)(2,1)S(1)} %copy-done.3, bf16[4,64,128]{2,1,0:T(8,128)(2,1)S(1)} %bitcast.90, pred[4,128]{1,0:T(4,128)(4,1)S(1)} %compare_and_fusion, s32[4,128]{1,0:T(4,128)S(1)} %select_reduce_fusion), kind=kOutput, calls=%fused_computation.2 | convolution fusion | flops 8585216 | bytes 330240 | tf_op jit(solution)/shard_map/rps,rsc->rpc/dot_general | solution.py:91
  78.0 0.9 %fusion.1 = bf16[4,128,128]{2,1,0:T(8,128)(2,1)} fusion(bf16[4,128,128]{2,1,0:T(8,128)(2,1)S(1)} %copy-done.4, bf16[4,64,128]{2,1,0:T(8,128)(2,1)S(1)} %bitcast.89, pred[4,128]{1,0:T(4,128)(4,1)S(1)} %compare_and_fusion, s32[4,128]{1,0:T(4,128)S(1)} %select_reduce_fusion), kind=kOutput, calls=%fused_computation.3 | convolution fusion | flops 8585216 | bytes 330240 | tf_op jit(solution)/shard_map/rps,rsc->rpc/dot_general | solution.py:91
  78.9 4.6 %all-to-all-done.4 = f32[8,32,256]{2,1,0:T(8,128)S(1)} async-done(((f32[8,32,256]{2,1,0:T(8,128)}), f32[8,32,256]{2,1,0:T(8,128)S(1)}, u32[]{:S(2)}, u32[]{:S(2)}) %all-to-all-start.4) | async-done | bytes 262176 | tf_op jit(solution)/shard_map/all_to_all | solution.py:254
  83.5 0.6 reduce_sum.51
  (43 shorter events, 2.0 us)
Async XLA Ops:
  0.6 64.0 %copy-start = (bf16[1024,256]{1,0:T(8,128)(2,1)S(1)}, bf16[1024,256]{1,0:T(8,128)(2,1)}, u32[]{:S(2)}) copy-start(bf16[1024,256]{1,0:T(8,128)(2,1)} %param.15) | copy-start | bytes 1572868
  2.1 17.2 %all-to-all-start = ((bf16[8,8,1280]{2,1,0:T(8,128)(2,1)}), bf16[8,8,1280]{2,1,0:T(8,128)(2,1)S(1)}, u32[]{:S(2)}, u32[]{:S(2)}) async-start(bf16[8,8,1280]{2,1,0:T(8,128)(2,1)} %broadcast_in_dim.42), calls=%async_computation | async-start | bytes 327680 | tf_op jit(solution)/shard_map/all_to_all | solution.py:175
  12.4 1.8 %copy-start.3 = (bf16[4,128,128]{2,1,0:T(8,128)(2,1)S(1)}, bf16[4,128,128]{2,1,0:T(8,128)(2,1)}, u32[]{:S(2)}) copy-start(bf16[4,128,128]{2,1,0:T(8,128)(2,1)} %param.13) | copy-start | bytes 393220
  12.4 1.8 %copy-start.4 = (bf16[4,128,128]{2,1,0:T(8,128)(2,1)S(1)}, bf16[4,128,128]{2,1,0:T(8,128)(2,1)}, u32[]{:S(2)}) copy-start(bf16[4,128,128]{2,1,0:T(8,128)(2,1)} %param.14) | copy-start | bytes 393220
  12.9 0.7 copy-start.9
  19.4 0.7 copy-start.2
  20.0 9.5 %all-to-all-start.1 = ((bf16[4,128,256]{2,1,0:T(8,128)(2,1)}), bf16[4,128,256]{2,1,0:T(8,128)(2,1)S(1)}, u32[]{:S(2)}, u32[]{:S(2)}) async-start(bf16[4,128,256]{2,1,0:T(8,128)(2,1)} %pad_maximum_fusion), calls=%async_computation.1 | async-start | bytes 524288 | tf_op jit(solution)/shard_map/all_to_all | solution.py:211
  29.6 0.7 copy-start.1
  32.9 3.5 %copy-start.5 = (bf16[8,1024]{1,0:T(8,128)(2,1)S(1)}, bf16[8,1024]{1,0:T(8,128)(2,1)}, u32[]{:S(2)}) copy-start(bf16[8,1024]{1,0:T(8,128)(2,1)} %param.10) | copy-start | bytes 49156
  32.9 11.5 %all-to-all-start.2 = ((bf16[8,8,1072]{2,1,0:T(8,128)(2,1)}), bf16[8,8,1072]{2,1,0:T(8,128)(2,1)S(1)}, u32[]{:S(2)}, u32[]{:S(2)}) async-start(bf16[8,8,1072]{2,1,0:T(8,128)(2,1)} %bitcast.87), calls=%async_computation.2 | async-start | bytes 294912 | tf_op jit(solution)/shard_map/all_to_all | solution.py:233
  45.0 0.9 %copy-start.6 = (bf16[8,128]{1,0:T(8,128)(2,1)S(1)}, bf16[8,128]{1,0:T(8,128)(2,1)}, u32[]{:S(2)}) copy-start(bf16[8,128]{1,0:T(8,128)(2,1)} %param.12) | copy-start | bytes 6148
  45.0 0.9 %copy-start.7 = (bf16[8,128]{1,0:T(8,128)(2,1)S(1)}, bf16[8,128]{1,0:T(8,128)(2,1)}, u32[]{:S(2)}) copy-start(bf16[8,128]{1,0:T(8,128)(2,1)} %param.11) | copy-start | bytes 6148
  46.8 17.8 %all-to-all-start.3 = ((bf16[32,8,1280]{2,1,0:T(8,128)(2,1)}), bf16[32,8,1280]{2,1,0:T(8,128)(2,1)S(1)}, u32[]{:S(2)}, u32[]{:S(2)}) async-start(bf16[32,8,1280]{2,1,0:T(8,128)(2,1)} %broadcast_in_dim.46), calls=%async_computation.3 | async-start | bytes 1310720 | tf_op jit(solution)/shard_map/all_to_all | solution.py:175
  50.7 0.7 copy-start.8
  51.4 0.7 copy-start.10
  65.6 17.9 %all-to-all-start.4 = ((f32[8,32,256]{2,1,0:T(8,128)}), f32[8,32,256]{2,1,0:T(8,128)S(1)}, u32[]{:S(2)}, u32[]{:S(2)}) async-start(f32[8,32,256]{2,1,0:T(8,128)} %bitcast.24), calls=%async_computation.4 | async-start | bytes 524288 | tf_op jit(solution)/shard_map/all_to_all | solution.py:254

commit v7 on v6

--- a/solution.py
+++ b/solution.py
@@ -1,3 +1,4 @@
+import functools
 import math
 
 import jax
@@ -102,8 +103,8 @@
     return hi, mid, lo
 
 
-def block_attention_kernel(limit_ref, q_ref, kv_ref, out_ref, stats_ref):
-    blocks, block_len, _ = kv_ref.shape
+def block_attention_kernel(block_len, limit_ref, q_ref, kv_ref, out_ref, stats_ref):
+    blocks = kv_ref.shape[0]
     rows = out_ref.shape[0]
     heads = stats_ref.shape[1] // 2
     score_scale = 1.0 / math.sqrt(HEAD_SIZE)
@@ -116,7 +117,7 @@
         s = (
             lax.dot_general(
                 q,
-                kv_ref[b, :, :HEAD_SIZE],
+                kv_ref[b, :block_len, :HEAD_SIZE],
                 (((1,), (1,)), ((), ())),
                 preferred_element_type=jnp.float32,
             )
@@ -135,7 +136,7 @@
         total = total + jnp.sum(weights, axis=1, keepdims=True)
         out = out + jnp.dot(
             weights.astype(jnp.bfloat16),
-            kv_ref[b, :, HEAD_SIZE:],
+            kv_ref[b, :block_len, HEAD_SIZE:],
             preferred_element_type=jnp.float32,
         )
     out = out.astype(out_ref.dtype)
@@ -150,13 +151,13 @@
         out_ref[:, width + j * 2 * heads : width + (j + 1) * 2 * heads] = part
 
 
-def block_attention(limit, group_rows, blocks_kv, width):
+def block_attention(limit, group_rows, blocks_kv, width, block_len):
     rows = group_rows.shape[0]
     heads = width // HEAD_SIZE
-    blocks, block_len, _ = blocks_kv.shape
+    blocks = blocks_kv.shape[0]
     vmem = pl.BlockSpec(memory_space=pltpu.VMEM)
     return pl.pallas_call(
-        block_attention_kernel,
+        functools.partial(block_attention_kernel, block_len),
         out_shape=jax.ShapeDtypeStruct((rows, width + 6 * heads), jnp.bfloat16),
         in_specs=[pl.BlockSpec(memory_space=pltpu.SMEM), vmem, vmem],
         out_specs=vmem,
@@ -207,14 +208,16 @@
     own_draft = jnp.concatenate([draft_token_keys, draft_token_values], axis=1)
     group_rows = gather_rows(jnp.concatenate([queries, own_draft], axis=1), "bz")
     cache_pair = jnp.concatenate([cached_key_vectors, cached_value_vectors], axis=2)
-    group_rows, cache_pair = lax.optimization_barrier((group_rows, cache_pair))
-    blocks_kv = lax.all_to_all(
-        cache_pair,
-        "bx",
-        split_axis=0,
-        concat_axis=0,
-        tiled=True,
-    )
+    path_pick = (
+        accepted_nodes[my_request][:, None] == jnp.arange(TREE_TOKENS, dtype=jnp.int32)[None, :]
+    ).astype(jnp.bfloat16)
+    path_rows = jnp.dot(
+        path_pick, group_rows[:, width_q:], preferred_element_type=jnp.float32
+    ).astype(jnp.bfloat16)
+    outgoing = jnp.concatenate(
+        [cache_pair, jnp.broadcast_to(path_rows[None], (requests,) + path_rows.shape)], axis=1
+    )
+    blocks_kv = lax.all_to_all(outgoing, "bx", split_axis=0, concat_axis=0, tiled=True)
     tree_keys = group_rows[:, width_q : width_q + cache_width].reshape(
         1, 1, TREE_TOKENS, kv_local, HEAD_SIZE
     )
@@ -227,7 +230,7 @@
     draft_part = partial_softmax(local_queries, tree_keys, tree_values, draft_usable, score_scale)
     source_blocks = jnp.arange(blocks_kv.shape[0], dtype=jnp.int32) * ring + my_z
     limit = lengths[my_request] - source_blocks * block_len
-    packed_out = block_attention(limit, group_rows, blocks_kv, width_q)
+    packed_out = block_attention(limit, group_rows, blocks_kv, width_q, block_len)
     head_count = width_q // HEAD_SIZE
     width_out = width_q
     moved = lax.all_to_all(
@@ -246,10 +249,8 @@
         moved_stats[..., head_count:],
     )
     attention = merge_parts(cache_part, draft_part, HEAD_SIZE)
-    every_row = gather_rows(jnp.concatenate([attention, own_draft], axis=1), blk)
-    gathered_keys = every_row[:, width_q : width_q + cache_width]
-    gathered_values = every_row[:, width_q + cache_width :]
-    partial = jnp.dot(every_row[:, :width_q], out_weight, preferred_element_type=jnp.float32)
+    every_row = gather_rows(attention, blk)
+    partial = jnp.dot(every_row, out_weight, preferred_element_type=jnp.float32)
     out_rows = partial.shape[0] // kv_count
     arrived = lax.all_to_all(
         partial.reshape(kv_count, out_rows, partial.shape[1]),
@@ -262,19 +263,10 @@
     positions_here = my_block * block_len + jnp.arange(block_len, dtype=jnp.int32)
     offset = positions_here[None, :] - lengths[:, None]
     written = (offset >= 0) & (offset < accepted_count[:, None])
-    slot_match = offset[:, :, None] == jnp.arange(ACC, dtype=jnp.int32)[None, None, :]
-    node_ids = jnp.sum(jnp.where(slot_match, accepted_nodes[:, None, :], 0), axis=-1)
-    new_cache_keys = place_rows(
-        gathered_keys.reshape(requests, TREE_TOKENS, cache_width),
-        node_ids,
-        written,
-        cached_key_vectors,
-    )
+    path_all = blocks_kv[:, block_len:, :]
+    new_cache_keys = place_rows(path_all[..., :cache_width], offset, written, cached_key_vectors)
     new_cache_values = place_rows(
-        gathered_values.reshape(requests, TREE_TOKENS, cache_width),
-        node_ids,
-        written,
-        cached_value_vectors,
+        path_all[..., cache_width:], offset, written, cached_value_vectors
     )
     return (projected, new_cache_keys, new_cache_values)
 

time: 85 us -> 84.2 us (level)
  waiting for transfers between devices: 32.4 us -> 29.3 us
  matrix products: 5.58 us -> 7.17 us
  starting transfers between devices: 31.9 us -> 33.2 us
    all_to_all x2, waiting for transfers between devices: 16.8 us -> 13.4 us  [gather_rows(): lax.all_to_all(spread, axis_name, split_axis=0, concat_axis=0, tiled=True)]
    dot_general x2, matrix products: 1.83 us -> 3.25 us  [place_rows(): jnp.einsum('rps,rsc->rpc', selector, sources, preferred_element_type=jnp....]
    all_to_all x1, starting transfers between devices: 11.5 us -> 12.8 us  [on_device(): lax.all_to_all(partial.reshape(kv_count, out_rows, partial.shape[1]), 'kv...]
    unnamed x22 -> x16, local copies, waits for them, and re-layouts: 3.21 us -> 2.03 us
  transfers between devices with their start and end apart: 5 -> 5, of which waited for: 5 -> 5; matrix products, arithmetic and copies ran while one was open for 9% -> 11% of each run, Pallas kernels for 0% -> 0%
where the time goes in v7:
time: 84.2 us; the launch traced here: 83.3 us
  starting transfers between devices  33.2 us (39%)
  waiting for transfers between devices  29.3 us (35%)
  matrix products  7.17 us (9%)
  local copies, waits for them, and re-layouts  6.03 us (7%)
  other arithmetic  4.21 us (5%)
  Pallas kernels  2.61 us (3%)
    all_to_all x2, waiting for transfers between devices, gather_rows(): lax.all_to_all(spread, axis_name, split_axis=0, concat_axis=0, tiled=True)  13.4 us
    all_to_all x2, starting transfers between devices, gather_rows(): lax.all_to_all(spread, axis_name, split_axis=0, concat_axis=0, tiled=True)  12.9 us
    all_to_all x1, starting transfers between devices, on_device(): lax.all_to_all(partial.reshape(kv_count, out_rows, partial.shape[1]), 'kv...  12.8 us
    all_to_all x1, waiting for transfers between devices, on_device(): lax.all_to_all(packed_out.reshape(ring, rows_dev, -1), 'bz', split_axis=0...  6.61 us
    all_to_all x1, waiting for transfers between devices, on_device(): lax.all_to_all(partial.reshape(kv_count, out_rows, partial.shape[1]), 'kv...  4.84 us
    all_to_all x1, waiting for transfers between devices, on_device(): lax.all_to_all(outgoing, 'bx', split_axis=0, concat_axis=0, tiled=True)  4.45 us
    all_to_all x1, starting transfers between devices, on_device(): lax.all_to_all(outgoing, 'bx', split_axis=0, concat_axis=0, tiled=True)  4.01 us
    all_to_all x1, starting transfers between devices, on_device(): lax.all_to_all(packed_out.reshape(ring, rows_dev, -1), 'bz', split_axis=0...  3.51 us
  transfers between devices with their start and end apart: 5, of which 5 were waited for; matrix products, arithmetic and copies ran while one was open for 11% of the time, Pallas kernels for 0%

profile of v7, /device:TPU:1, one launch (start us, length us, event | category | flops | bytes accessed | tf_op | source)
XLA Modules:
  0.0 83.3 jit_solution(1895912340190693121)
XLA Ops:
  0.6 0.8 pad_maximum_fusion.1
  1.5 0.7 broadcast_in_dim.32
  2.1 9.0 %all-to-all-start = ((bf16[8,8,1280]{2,1,0:T(8,128)(2,1)}), bf16[8,8,1280]{2,1,0:T(8,128)(2,1)S(1)}, u32[]{:S(2)}, u32[]{:S(2)}) async-start(bf16[8,8,1280]{2,1,0:T(8,128)(2,1)} %broadcast_in_dim.32), calls=%async_computation | async-start | bytes 327680 | tf_op jit(solution)/shard_map/all_to_all | solution.py:176
  11.2 0.6 copy-done.6
  11.8 0.6 dynamic_slice.10
  12.4 0.7 fusion.40
  13.1 0.2 fusion.16
  13.3 0.2 fusion.10
  14.2 0.7 fusion.39
  15.0 4.3 %all-to-all-done = bf16[8,8,1280]{2,1,0:T(8,128)(2,1)S(1)} async-done(((bf16[8,8,1280]{2,1,0:T(8,128)(2,1)}), bf16[8,8,1280]{2,1,0:T(8,128)(2,1)S(1)}, u32[]{:S(2)}, u32[]{:S(2)}) %all-to-all-start) | async-done | bytes 163872 | tf_op jit(solution)/shard_map/all_to_all | solution.py:176
  19.4 0.2 convolution_convert_fusion.2
  19.6 0.7 pad_maximum_fusion
  20.3 4.0 %all-to-all-start.1 = ((bf16[4,136,256]{2,1,0:T(8,128)(2,1)}), bf16[4,136,256]{2,1,0:T(8,128)(2,1)S(1)}, u32[]{:S(2)}, u32[]{:S(2)}) async-start(bf16[4,136,256]{2,1,0:T(8,128)(2,1)} %pad_maximum_fusion), calls=%async_computation.1 | async-start | bytes 557056 | tf_op jit(solution)/shard_map/all_to_all | solution.py:220
  24.3 1.2 %multiply_subtract_fusion.limit_ref = s32[4]{0:T(128)} fusion(s32[]{:T(128)S(6)} %axis_index.33, s32[]{:T(128)} %bitcast), kind=kLoop, calls=%fused_computation.75 | loop fusion | flops 16 | bytes 24 | tf_op jit(solution)/shard_map/sub | solution.py:232
  25.5 4.4 %all-to-all-done.1.kv_ref = bf16[4,136,256]{2,1,0:T(8,128)(2,1)S(1)} async-done(((bf16[4,136,256]{2,1,0:T(8,128)(2,1)}), bf16[4,136,256]{2,1,0:T(8,128)(2,1)S(1)}, u32[]{:S(2)}, u32[]{:S(2)}) %all-to-all-start.1) | async-done | bytes 278560 | tf_op jit(solution)/shard_map/all_to_all | solution.py:220
  29.9 0.7 copy-done.1
  30.6 2.6 %shard_map.121 = bf16[64,1072]{1,0:T(8,128)(2,1)} custom-call(s32[4]{0:T(128)} %multiply_subtract_fusion.limit_ref, bf16[64,1280]{1,0:T(8,128)(2,1)} %bitcast.84, bf16[4,136,256]{2,1,0:T(8,128)(2,1)} %copy-done.1), custom_call_target="tpu_custom_call" | custom-call | flops 134217728 | bytes 530432 | tf_op jit(solution)/shard_map/pallas_call | solution.py:159
  33.2 3.5 %all-to-all-start.2 = ((bf16[8,8,1072]{2,1,0:T(8,128)(2,1)}), bf16[8,8,1072]{2,1,0:T(8,128)(2,1)S(1)}, u32[]{:S(2)}, u32[]{:S(2)}) async-start(bf16[8,8,1072]{2,1,0:T(8,128)(2,1)} %bitcast.87), calls=%async_computation.2 | async-start | bytes 294912 | tf_op jit(solution)/shard_map/all_to_all | solution.py:236
  36.8 0.9 %fusion.42 = (f32[8,8]{0,1:T(8,128)S(1)}, f32[1,1,1,8,8,64]{5,3,4,0,2,1:T(8,128)S(1)}) fusion(bf16[8,8,128]{2,0,1:T(8,128)(2,1)S(1)} %bitcast.88, bf16[64,1280]{1,0:T(8,128)(2,1)} %bitcast.85, pred[8,64]{1,0:T(8,128)(4,1)S(1)} %fusion.35), kind=kOutput, calls=%fused_computation.76 | convolution fusion | flops 1060800 | bytes 49920 | tf_op jit(solution)/shard_map/rtkgh,rbpkh->brkgtp/dot_general | solution.py:36
  37.8 0.2 fusion.20
  38.2 6.6 %all-to-all-done.2 = bf16[8,8,1072]{2,1,0:T(8,128)(2,1)S(1)} async-done(((bf16[8,8,1072]{2,1,0:T(8,128)(2,1)}), bf16[8,8,1072]{2,1,0:T(8,128)(2,1)S(1)}, u32[]{:S(2)}, u32[]{:S(2)}) %all-to-all-start.2) | async-done | bytes 137248 | tf_op jit(solution)/shard_map/all_to_all | solution.py:236
  45.3 0.8 %fusion.11 = bf16[8,1024]{1,0:T(8,128)(2,1)S(1)} fusion(f32[8,1024]{1,0:T(8,128)S(1)} %fusion.15, bf16[64,1280]{1,0:T(8,128)(2,1)} %bitcast.86, bf16[8,8,64]{2,0,1:T(8,128)(2,1)S(1)} %get-tuple-element.8, f32[8,8]{0,1:T(8,128)S(1)} %copy.29, f32[8,8]{0,1:T(8,128)S(1)} %copy.25), kind=kOutput, calls=%fused_computation.20 | convolution fusion | flops 1081344 | bytes 74240 | tf_op jit(solution)/shard_map/brkgtp,rbpkh->brtkgh/dot_general | solution.py:45
  46.2 0.9 %broadcast_in_dim.37 = bf16[32,8,1024]{2,1,0:T(8,128)(2,1)} broadcast(bf16[8,1024]{1,0:T(8,128)(2,1)S(1)} %fusion.11), dimensions={1,2} | broadcast | bytes 540672 | tf_op jit(solution)/shard_map/broadcast_in_dim | solution.py:175
  47.0 3.9 %all-to-all-start.3 = ((bf16[32,8,1024]{2,1,0:T(8,128)(2,1)}), bf16[32,8,1024]{2,1,0:T(8,128)(2,1)S(1)}, u32[]{:S(2)}, u32[]{:S(2)}) async-start(bf16[32,8,1024]{2,1,0:T(8,128)(2,1)} %broadcast_in_dim.37), calls=%async_computation.3 | async-start | bytes 1048576 | tf_op jit(solution)/shard_map/all_to_all | solution.py:176
  51.0 0.6 copy-done.7
  51.8 1.6 %fusion.1 = bf16[4,128,128]{2,1,0:T(8,128)(2,1)} fusion(bf16[4,128,128]{2,1,0:T(8,128)(2,1)S(1)} %copy-done.3, pred[4,128]{1,0:T(4,128)(4,1)S(1)} %compare_and_fusion, bf16[4,136,256]{2,1,0:T(8,128)(2,1)} %copy-done.1, s32[4,128]{1,0:T(4,128)S(1)} %broadcast_subtract_fusion), kind=kOutput, calls=%fused_computation.3 | convolution fusion | flops 1187840 | bytes 273408 | tf_op jit(solution)/shard_map/rps,rsc->rpc/dot_general | solution.py:92
  53.4 9.1 %all-to-all-done.3 = bf16[32,8,1024]{2,1,0:T(8,128)(2,1)S(1)} async-done(((bf16[32,8,1024]{2,1,0:T(8,128)(2,1)}), bf16[32,8,1024]{2,1,0:T(8,128)(2,1)S(1)}, u32[]{:S(2)}, u32[]{:S(2)}) %all-to-all-start.3) | async-done | bytes 524320 | tf_op jit(solution)/shard_map/all_to_all | solution.py:176
  62.5 1.0 %fusion.13 = f32[8,32,256]{2,1,0:T(8,128)} fusion(bf16[8,32,1024]{2,1,0:T(8,128)(2,1)S(1)} %bitcast.82, bf16[1024,256]{1,0:T(8,128)(2,1)S(1)} %copy-done), kind=kOutput, calls=%fused_computation.23 | convolution fusion | flops 134217728 | bytes 1310720 | tf_op jit(solution)/shard_map/dot_general | solution.py:253
  63.5 12.8 %all-to-all-start.4 = ((f32[8,32,256]{2,1,0:T(8,128)}), f32[8,32,256]{2,1,0:T(8,128)S(1)}, u32[]{:S(2)}, u32[]{:S(2)}) async-start(f32[8,32,256]{2,1,0:T(8,128)} %fusion.13), calls=%async_computation.4 | async-start | bytes 524288 | tf_op jit(solution)/shard_map/all_to_all | solution.py:255
  76.2 1.6 %fusion = bf16[4,128,128]{2,1,0:T(8,128)(2,1)} fusion(bf16[4,128,128]{2,1,0:T(8,128)(2,1)S(1)} %copy-done.4, pred[4,128]{1,0:T(4,128)(4,1)S(1)} %compare_and_fusion, bf16[4,136,256]{2,1,0:T(8,128)(2,1)} %copy-done.1, s32[4,128]{1,0:T(4,128)S(1)} %broadcast_subtract_fusion), kind=kOutput, calls=%fused_computation.2 | convolution fusion | flops 1187840 | bytes 273408 | tf_op jit(solution)/shard_map/rps,rsc->rpc/dot_general | solution.py:92
  77.9 4.8 %all-to-all-done.4 = f32[8,32,256]{2,1,0:T(8,128)S(1)} async-done(((f32[8,32,256]{2,1,0:T(8,128)}), f32[8,32,256]{2,1,0:T(8,128)S(1)}, u32[]{:S(2)}, u32[]{:S(2)}) %all-to-all-start.4) | async-done | bytes 262176 | tf_op jit(solution)/shard_map/all_to_all | solution.py:255
  82.7 0.6 reduce_sum.42
  (37 shorter events, 1.9 us)
Async XLA Ops:
  0.6 61.8 %copy-start = (bf16[1024,256]{1,0:T(8,128)(2,1)S(1)}, bf16[1024,256]{1,0:T(8,128)(2,1)}, u32[]{:S(2)}) copy-start(bf16[1024,256]{1,0:T(8,128)(2,1)} %param.15) | copy-start | bytes 1572868
  2.1 17.2 %all-to-all-start = ((bf16[8,8,1280]{2,1,0:T(8,128)(2,1)}), bf16[8,8,1280]{2,1,0:T(8,128)(2,1)S(1)}, u32[]{:S(2)}, u32[]{:S(2)}) async-start(bf16[8,8,1280]{2,1,0:T(8,128)(2,1)} %broadcast_in_dim.32), calls=%async_computation | async-start | bytes 327680 | tf_op jit(solution)/shard_map/all_to_all | solution.py:176
  11.1 0.7 copy-start.6
  14.0 5.6 %copy-start.3 = (bf16[4,128,128]{2,1,0:T(8,128)(2,1)S(1)}, bf16[4,128,128]{2,1,0:T(8,128)(2,1)}, u32[]{:S(2)}) copy-start(bf16[4,128,128]{2,1,0:T(8,128)(2,1)} %param.14) | copy-start | bytes 393220
  14.0 5.6 %copy-start.4 = (bf16[4,128,128]{2,1,0:T(8,128)(2,1)S(1)}, bf16[4,128,128]{2,1,0:T(8,128)(2,1)}, u32[]{:S(2)}) copy-start(bf16[4,128,128]{2,1,0:T(8,128)(2,1)} %param.13) | copy-start | bytes 393220
  19.4 0.9 %copy-start.2 = (bf16[8,8,1280]{2,1,0:T(8,128)(2,1)}, bf16[8,8,1280]{2,1,0:T(8,128)(2,1)S(1)}, u32[]{:S(2)}) copy-start(bf16[8,8,1280]{2,1,0:T(8,128)(2,1)S(1)} %all-to-all-done) | copy-start | bytes 491524
  20.3 9.6 %all-to-all-start.1 = ((bf16[4,136,256]{2,1,0:T(8,128)(2,1)}), bf16[4,136,256]{2,1,0:T(8,128)(2,1)S(1)}, u32[]{:S(2)}, u32[]{:S(2)}) async-start(bf16[4,136,256]{2,1,0:T(8,128)(2,1)} %pad_maximum_fusion), calls=%async_computation.1 | async-start | bytes 557056 | tf_op jit(solution)/shard_map/all_to_all | solution.py:220
  29.9 0.7 copy-start.1
  33.2 3.5 %copy-start.5 = (bf16[8,1024]{1,0:T(8,128)(2,1)S(1)}, bf16[8,1024]{1,0:T(8,128)(2,1)}, u32[]{:S(2)}) copy-start(bf16[8,1024]{1,0:T(8,128)(2,1)} %param.10) | copy-start | bytes 49156
  33.2 11.5 %all-to-all-start.2 = ((bf16[8,8,1072]{2,1,0:T(8,128)(2,1)}), bf16[8,8,1072]{2,1,0:T(8,128)(2,1)S(1)}, u32[]{:S(2)}, u32[]{:S(2)}) async-start(bf16[8,8,1072]{2,1,0:T(8,128)(2,1)} %bitcast.87), calls=%async_computation.2 | async-start | bytes 294912 | tf_op jit(solution)/shard_map/all_to_all | solution.py:236
  47.0 15.4 %all-to-all-start.3 = ((bf16[32,8,1024]{2,1,0:T(8,128)(2,1)}), bf16[32,8,1024]{2,1,0:T(8,128)(2,1)S(1)}, u32[]{:S(2)}, u32[]{:S(2)}) async-start(bf16[32,8,1024]{2,1,0:T(8,128)(2,1)} %broadcast_in_dim.37), calls=%async_computation.3 | async-start | bytes 1048576 | tf_op jit(solution)/shard_map/all_to_all | solution.py:176
  51.0 0.7 copy-start.7
  63.5 19.3 %all-to-all-start.4 = ((f32[8,32,256]{2,1,0:T(8,128)}), f32[8,32,256]{2,1,0:T(8,128)S(1)}, u32[]{:S(2)}, u32[]{:S(2)}) async-start(f32[8,32,256]{2,1,0:T(8,128)} %fusion.13), calls=%async_computation.4 | async-start | bytes 524288 | tf_op jit(solution)/shard_map/all_to_all | solution.py:255

commit v8 on v7

--- a/solution.py
+++ b/solution.py
@@ -168,6 +168,11 @@
             bytes_accessed=2 * (rows * width + 2 * blocks * block_len * HEAD_SIZE + rows * (width + 6 * heads)),
         ),
     )(limit, group_rows, blocks_kv)
+
+
+def shifted(block, axis_name, shift):
+    count = lax.axis_size(axis_name)
+    return lax.ppermute(block, axis_name, [(i, (i + shift) % count) for i in range(count)])
 
 
 def gather_rows(block, axis_name):
@@ -214,10 +219,15 @@
     path_rows = jnp.dot(
         path_pick, group_rows[:, width_q:], preferred_element_type=jnp.float32
     ).astype(jnp.bfloat16)
-    outgoing = jnp.concatenate(
-        [cache_pair, jnp.broadcast_to(path_rows[None], (requests,) + path_rows.shape)], axis=1
-    )
-    blocks_kv = lax.all_to_all(outgoing, "bx", split_axis=0, concat_axis=0, tiled=True)
+    lanes = cache_pair.shape[0]
+    ahead = jnp.roll(cache_pair, -my_x, axis=0)
+    blocks_kv = jnp.stack(
+        [ahead[0]] + [shifted(ahead[k], "bx", k) for k in range(1, lanes)], axis=0
+    )
+    path_rel = jnp.stack(
+        [path_rows] + [shifted(path_rows, "bx", k) for k in range(1, lanes)], axis=0
+    )
+    source_x = (my_x - jnp.arange(lanes, dtype=jnp.int32)) % lanes
     tree_keys = group_rows[:, width_q : width_q + cache_width].reshape(
         1, 1, TREE_TOKENS, kv_local, HEAD_SIZE
     )
@@ -228,7 +238,7 @@
     own_reach = lax.dynamic_slice_in_dim(reachable, node_start, rows_dev, 1)
     draft_usable = (own_reach > 0.5)[None, :, None, None, :, :]
     draft_part = partial_softmax(local_queries, tree_keys, tree_values, draft_usable, score_scale)
-    source_blocks = jnp.arange(blocks_kv.shape[0], dtype=jnp.int32) * ring + my_z
+    source_blocks = source_x * ring + my_z
     limit = lengths[my_request] - source_blocks * block_len
     packed_out = block_attention(limit, group_rows, blocks_kv, width_q, block_len)
     head_count = width_q // HEAD_SIZE
@@ -263,7 +273,7 @@
     positions_here = my_block * block_len + jnp.arange(block_len, dtype=jnp.int32)
     offset = positions_here[None, :] - lengths[:, None]
     written = (offset >= 0) & (offset < accepted_count[:, None])
-    path_all = blocks_kv[:, block_len:, :]
+    path_all = jnp.roll(path_rel[(-jnp.arange(lanes)) % lanes], my_x, axis=0)
     new_cache_keys = place_rows(path_all[..., :cache_width], offset, written, cached_key_vectors)
     new_cache_values = place_rows(
         path_all[..., cache_width:], offset, written, cached_value_vectors

time: 84.2 us -> 78.1 us (0.928)
  waiting for transfers between devices: 29.3 us -> 16.9 us
  starting transfers between devices: 33.2 us -> 39.9 us
    all_to_all x2, waiting for transfers between devices: 13.4 us -> 2.9 us  [gather_rows(): lax.all_to_all(spread, axis_name, split_axis=0, concat_axis=0, tiled=True)]
    ppermute x0 -> x6, starting transfers between devices: none -> 9.69 us  [shifted(): lax.ppermute(block, axis_name, [(i, (i + shift) % count) for i in range(c...]
    all_to_all x1 -> x0, waiting for transfers between devices: 4.45 us -> none  [on_device(): lax.all_to_all(outgoing, 'bx', split_axis=0, concat_axis=0, tiled=True)]
    all_to_all x1 -> x0, starting transfers between devices: 4.01 us -> none  [on_device(): lax.all_to_all(outgoing, 'bx', split_axis=0, concat_axis=0, tiled=True)]
    all_to_all x1, starting transfers between devices: 3.51 us -> 6.77 us  [on_device(): lax.all_to_all(packed_out.reshape(ring, rows_dev, -1), 'bz', split_axis=0...]
    all_to_all x1, starting transfers between devices: 12.8 us -> 10.3 us  [on_device(): lax.all_to_all(partial.reshape(kv_count, out_rows, partial.shape[1]), 'kv...]
    ppermute x0 -> x6, waiting for transfers between devices: none -> 1.62 us  [shifted(): lax.ppermute(block, axis_name, [(i, (i + shift) % count) for i in range(c...]
    dot_general x2, matrix products: 3.25 us -> 1.86 us  [place_rows(): jnp.einsum('rps,rsc->rpc', selector, sources, preferred_element_type=jnp....]
  transfers between devices with their start and end apart: 5 -> 10, of which waited for: 5 -> 5; matrix products, arithmetic and copies ran while one was open for 11% -> 13% of each run, Pallas kernels for 0% -> 0%
where the time goes in v8:
time: 78.1 us; the launch traced here: 77 us
  starting transfers between devices  39.9 us (51%)
  waiting for transfers between devices  16.9 us (22%)
  matrix products  6.54 us (8%)
  local copies, waits for them, and re-layouts  5.9 us (8%)
  other arithmetic  4.43 us (6%)
  Pallas kernels  2.6 us (3%)
  between operations  0.82 us (1%)
    all_to_all x2, starting transfers between devices, gather_rows(): lax.all_to_all(spread, axis_name, split_axis=0, concat_axis=0, tiled=True)  13.2 us
    all_to_all x1, starting transfers between devices, on_device(): lax.all_to_all(partial.reshape(kv_count, out_rows, partial.shape[1]), 'kv...  10.3 us
    ppermute x6, starting transfers between devices, shifted(): lax.ppermute(block, axis_name, [(i, (i + shift) % count) for i in range(c...  9.69 us
    all_to_all x1, waiting for transfers between devices, on_device(): lax.all_to_all(packed_out.reshape(ring, rows_dev, -1), 'bz', split_axis=0...  6.82 us
    all_to_all x1, starting transfers between devices, on_device(): lax.all_to_all(packed_out.reshape(ring, rows_dev, -1), 'bz', split_axis=0...  6.77 us
    all_to_all x1, waiting for transfers between devices, on_device(): lax.all_to_all(partial.reshape(kv_count, out_rows, partial.shape[1]), 'kv...  5.54 us
    all_to_all x2, waiting for transfers between devices, gather_rows(): lax.all_to_all(spread, axis_name, split_axis=0, concat_axis=0, tiled=True)  2.9 us
    pallas_call x1, Pallas kernels, block_attention(): pl.pallas_call(functools.partial(block_attention_kernel, block_len), out_...  2.6 us
  transfers between devices with their start and end apart: 10, of which 5 were waited for; matrix products, arithmetic and copies ran while one was open for 13% of the time, Pallas kernels for 0%

profile of v8, /device:TPU:1, one launch (start us, length us, event | category | flops | bytes accessed | tf_op | source)
XLA Modules:
  0.0 77.0 jit_solution(5332895601328307166)
XLA Ops:
  0.6 0.8 %pad_maximum_fusion.1 = bf16[8,1280]{1,0:T(8,128)(2,1)S(1)} fusion(bf16[8,128]{1,0:T(8,128)(2,1)} %param.12, bf16[8,128]{1,0:T(8,128)(2,1)} %param.11, bf16[8,1024]{1,0:T(8,128)(2,1)} %param.10), kind=kLoop, calls=%fused_computation.56 | loop fusion | flops 61440 | bytes 40960 | tf_op jit(solution)/shard_map/concatenate | solution.py:214
  1.5 0.7 broadcast_in_dim.30
  2.1 9.1 %all-to-all-start = ((bf16[8,8,1280]{2,1,0:T(8,128)(2,1)}), bf16[8,8,1280]{2,1,0:T(8,128)(2,1)S(1)}, u32[]{:S(2)}, u32[]{:S(2)}) async-start(bf16[8,8,1280]{2,1,0:T(8,128)(2,1)} %broadcast_in_dim.30), calls=%async_computation | async-start | bytes 327680 | tf_op jit(solution)/shard_map/all_to_all | solution.py:181
  11.5 1.3 %collective-permute-start = (bf16[128,256]{1,0:T(8,128)(2,1)S(1)}, bf16[128,256]{1,0:T(8,128)(2,1)S(1)}, u32[]{:S(2)}, u32[]{:S(2)}) collective-permute-start(bf16[128,256]{1,0:T(8,128)(2,1)S(1)} %get-tuple-element.9), channel_id=1, source_target_pairs={{0,8},{8,16},{16,24},{24,0},{1,9},{9,17},{17,25},{25,1},{2,10},{10... | collective-permute-start | bytes 196616 | tf_op jit(solution)/shard_map/ppermute | solution.py:175
  12.8 2.5 %collective-permute-start.1 = (bf16[128,256]{1,0:T(8,128)(2,1)S(1)}, bf16[128,256]{1,0:T(8,128)(2,1)S(1)}, u32[]{:S(2)}, u32[]{:S(2)}) collective-permute-start(bf16[128,256]{1,0:T(8,128)(2,1)S(1)} %get-tuple-element.8), channel_id=1, source_target_pairs={{0,16},{8,24},{16,0},{24,8},{1,17},{9,25},{17,1},{25,9},{2,18},{10... | collective-permute-start | bytes 196616 | tf_op jit(solution)/shard_map/ppermute | solution.py:175
  15.2 1.2 %collective-permute-start.2 = (bf16[128,256]{1,0:T(8,128)(2,1)S(1)}, bf16[128,256]{1,0:T(8,128)(2,1)S(1)}, u32[]{:S(2)}, u32[]{:S(2)}) collective-permute-start(bf16[128,256]{1,0:T(8,128)(2,1)S(1)} %get-tuple-element.10), channel_id=1, source_target_pairs={{0,24},{8,0},{16,8},{24,16},{1,25},{9,1},{17,9},{25,17},{2,26},{10... | collective-permute-start | bytes 196616 | tf_op jit(solution)/shard_map/ppermute | solution.py:175
  16.4 0.7 fusion.50
  18.3 0.6 copy-done.5
  19.6 1.2 %fusion.48.limit_ref = s32[4]{0:T(128)} fusion(s32[]{:T(128)S(6)} %axis_index.33, s32[]{:T(128)S(6)} %axis_index.15, s32[]{:T(128)} %bitcast), kind=kLoop, calls=%fused_computation.100 | loop fusion | flops 64 | bytes 28 | tf_op jit(solution)/shard_map/sub | solution.py:242
  20.8 0.7 fusion.51
  21.5 0.7 pad_maximum_fusion.kv_ref
  22.2 0.7 copy-done.1
  22.9 2.6 %shard_map.121 = bf16[64,1072]{1,0:T(8,128)(2,1)} custom-call(s32[4]{0:T(128)} %fusion.48.limit_ref, bf16[64,1280]{1,0:T(8,128)(2,1)} %bitcast.98, bf16[4,128,256]{2,1,0:T(8,128)(2,1)} %pad_maximum_fusion.kv_ref), custom_call_target="tpu_custom_call" | custom-call | flops 134217728 | bytes 530432 | tf_op jit(solution)/shard_map/pallas_call | solution.py:159
  25.5 6.8 %all-to-all-start.1 = ((bf16[8,8,1072]{2,1,0:T(8,128)(2,1)}), bf16[8,8,1072]{2,1,0:T(8,128)(2,1)S(1)}, u32[]{:S(2)}, u32[]{:S(2)}) async-start(bf16[8,8,1072]{2,1,0:T(8,128)(2,1)} %bitcast.102), calls=%async_computation.1 | async-start | bytes 294912 | tf_op jit(solution)/shard_map/all_to_all | solution.py:246
  32.3 0.9 %fusion.54 = (f32[8,8]{0,1:T(8,128)S(1)}, f32[1,1,1,8,8,64]{5,3,4,0,2,1:T(8,128)S(1)}) fusion(bf16[8,8,128]{2,0,1:T(8,128)(2,1)S(1)} %bitcast.103, bf16[64,1280]{1,0:T(8,128)(2,1)} %bitcast.99, pred[8,64]{1,0:T(8,128)(4,1)S(1)} %fusion.39), kind=kOutput, calls=%fused_computation.107 | convolution fusion | flops 1060800 | bytes 49920 | tf_op jit(solution)/shard_map/rtkgh,rbpkh->brkgtp/dot_general | solution.py:36
  33.7 6.8 %all-to-all-done.1 = bf16[8,8,1072]{2,1,0:T(8,128)(2,1)S(1)} async-done(((bf16[8,8,1072]{2,1,0:T(8,128)(2,1)}), bf16[8,8,1072]{2,1,0:T(8,128)(2,1)S(1)}, u32[]{:S(2)}, u32[]{:S(2)}) %all-to-all-start.1) | async-done | bytes 137248 | tf_op jit(solution)/shard_map/all_to_all | solution.py:246
  41.0 0.8 %fusion.11 = bf16[8,1024]{1,0:T(8,128)(2,1)S(1)} fusion(f32[8,1024]{1,0:T(8,128)S(1)} %fusion.18, bf16[64,1280]{1,0:T(8,128)(2,1)} %bitcast.100, bf16[8,8,64]{2,0,1:T(8,128)(2,1)S(1)} %get-tuple-element.12, f32[8,8]{0,1:T(8,128)S(1)} %copy.29, f32[8,8]{0,1:T(8,128)S(1)} %copy.25), kind=kOutput, calls=%fused_computation.21 | convolution fusion | flops 1081344 | bytes 74240 | tf_op jit(solution)/shard_map/brkgtp,rbpkh->brtkgh/dot_general | solution.py:45
  41.9 0.9 %broadcast_in_dim.34 = bf16[32,8,1024]{2,1,0:T(8,128)(2,1)} broadcast(bf16[8,1024]{1,0:T(8,128)(2,1)S(1)} %fusion.11), dimensions={1,2} | broadcast | bytes 540672 | tf_op jit(solution)/shard_map/broadcast_in_dim | solution.py:180
  42.8 4.0 %all-to-all-start.2 = ((bf16[32,8,1024]{2,1,0:T(8,128)(2,1)}), bf16[32,8,1024]{2,1,0:T(8,128)(2,1)S(1)}, u32[]{:S(2)}, u32[]{:S(2)}) async-start(bf16[32,8,1024]{2,1,0:T(8,128)(2,1)} %broadcast_in_dim.34), calls=%async_computation.2 | async-start | bytes 1048576 | tf_op jit(solution)/shard_map/all_to_all | solution.py:181
  46.9 0.9 %convolution_convert_fusion.2 = bf16[8,256]{1,0:T(8,128)(2,1)S(1)} fusion(bf16[64,1280]{1,0:T(8,128)(2,1)} %bitcast.101, s32[8]{0:T(128)S(1)} %fusion.51), kind=kOutput, calls=%fused_computation.23 | convolution fusion | flops 264704 | bytes 36896 | tf_op jit(solution)/shard_map/dot_general | solution.py:219
  47.8 1.2 %collective-permute-start.3 = (bf16[8,256]{1,0:T(8,128)(2,1)S(1)}, bf16[8,256]{1,0:T(8,128)(2,1)S(1)}, u32[]{:S(2)}, u32[]{:S(2)}) collective-permute-start(bf16[8,256]{1,0:T(8,128)(2,1)S(1)} %convolution_convert_fusion.2), channel_id=1, source_target_pairs={{0,8},{8,16},{16,24},{24,0},{1,9},{9,17},{17,25},{25,1},{2,10},{10... | collective-permute-start | bytes 12296 | tf_op jit(solution)/shard_map/ppermute | solution.py:175
  49.0 2.5 %collective-permute-start.4 = (bf16[8,256]{1,0:T(8,128)(2,1)S(1)}, bf16[8,256]{1,0:T(8,128)(2,1)S(1)}, u32[]{:S(2)}, u32[]{:S(2)}) collective-permute-start(bf16[8,256]{1,0:T(8,128)(2,1)S(1)} %convolution_convert_fusion.2), channel_id=1, source_target_pairs={{0,16},{8,24},{16,0},{24,8},{1,17},{9,25},{17,1},{25,9},{2,18},{10... | collective-permute-start | bytes 12296 | tf_op jit(solution)/shard_map/ppermute | solution.py:175
  51.5 1.1 %collective-permute-start.5 = (bf16[8,256]{1,0:T(8,128)(2,1)S(1)}, bf16[8,256]{1,0:T(8,128)(2,1)S(1)}, u32[]{:S(2)}, u32[]{:S(2)}) collective-permute-start(bf16[8,256]{1,0:T(8,128)(2,1)S(1)} %convolution_convert_fusion.2), channel_id=1, source_target_pairs={{0,24},{8,0},{16,8},{24,16},{1,25},{9,1},{17,9},{25,17},{2,26},{10... | collective-permute-start | bytes 12296 | tf_op jit(solution)/shard_map/ppermute | solution.py:175
  52.6 0.6 collective-permute-done.4
  53.3 1.0 %collective-permute-done.5 = bf16[8,256]{1,0:T(8,128)(2,1)S(1)} collective-permute-done((bf16[8,256]{1,0:T(8,128)(2,1)S(1)}, bf16[8,256]{1,0:T(8,128)(2,1)S(1)}, u32[]{:S(2)}, u32[]{:S(2)}) %collective-permute-start.5) | collective-permute-done | bytes 4128 | tf_op jit(solution)/shard_map/ppermute | solution.py:175
  54.8 0.9 %fusion = bf16[4,128,128]{2,1,0:T(8,128)(2,1)} fusion(bf16[4,128,128]{2,1,0:T(8,128)(2,1)S(1)} %copy-done.2, pred[4,128]{1,0:T(4,128)(4,1)S(1)} %compare_and_fusion, bf16[4,8,256]{2,1,0:T(8,128)(2,1)S(1)} %fusion.26, s32[4,128]{1,0:T(4,128)S(1)} %broadcast_subtract_fusion), kind=kOutput, calls=%fused_computation.3 | convolution fusion | flops 1187840 | bytes 273408 | tf_op jit(solution)/shard_map/rps,rsc->rpc/dot_general | solution.py:92
  55.8 2.9 %all-to-all-done.2 = bf16[32,8,1024]{2,1,0:T(8,128)(2,1)S(1)} async-done(((bf16[32,8,1024]{2,1,0:T(8,128)(2,1)}), bf16[32,8,1024]{2,1,0:T(8,128)(2,1)S(1)}, u32[]{:S(2)}, u32[]{:S(2)}) %all-to-all-start.2) | async-done | bytes 524320 | tf_op jit(solution)/shard_map/all_to_all | solution.py:181
  58.7 1.0 %fusion.13 = f32[8,32,256]{2,1,0:T(8,128)} fusion(bf16[8,32,1024]{2,1,0:T(8,128)(2,1)S(1)} %bitcast.97, bf16[1024,256]{1,0:T(8,128)(2,1)S(1)} %copy-done), kind=kOutput, calls=%fused_computation.28 | convolution fusion | flops 134217728 | bytes 1310720 | tf_op jit(solution)/shard_map/dot_general | solution.py:263
  59.7 10.3 %all-to-all-start.3 = ((f32[8,32,256]{2,1,0:T(8,128)}), f32[8,32,256]{2,1,0:T(8,128)S(1)}, u32[]{:S(2)}, u32[]{:S(2)}) async-start(f32[8,32,256]{2,1,0:T(8,128)} %fusion.13), calls=%async_computation.3 | async-start | bytes 524288 | tf_op jit(solution)/shard_map/all_to_all | solution.py:265
  69.9 0.9 %fusion.1 = bf16[4,128,128]{2,1,0:T(8,128)(2,1)} fusion(bf16[4,128,128]{2,1,0:T(8,128)(2,1)S(1)} %copy-done.3, pred[4,128]{1,0:T(4,128)(4,1)S(1)} %compare_and_fusion, bf16[4,8,256]{2,1,0:T(8,128)(2,1)S(1)} %fusion.26, s32[4,128]{1,0:T(4,128)S(1)} %broadcast_subtract_fusion), kind=kOutput, calls=%fused_computation.4 | convolution fusion | flops 1187840 | bytes 273408 | tf_op jit(solution)/shard_map/rps,rsc->rpc/dot_general | solution.py:92
  70.9 5.5 %all-to-all-done.3 = f32[8,32,256]{2,1,0:T(8,128)S(1)} async-done(((f32[8,32,256]{2,1,0:T(8,128)}), f32[8,32,256]{2,1,0:T(8,128)S(1)}, u32[]{:S(2)}, u32[]{:S(2)}) %all-to-all-start.3) | async-done | bytes 262176 | tf_op jit(solution)/shard_map/all_to_all | solution.py:265
  76.4 0.6 reduce_sum.42
  (51 shorter events, 3.8 us)
Async XLA Ops:
  0.6 58.0 %copy-start = (bf16[1024,256]{1,0:T(8,128)(2,1)S(1)}, bf16[1024,256]{1,0:T(8,128)(2,1)}, u32[]{:S(2)}) copy-start(bf16[1024,256]{1,0:T(8,128)(2,1)} %param.15) | copy-start | bytes 1572868
  2.1 9.1 %copy-start.2 = (bf16[4,128,128]{2,1,0:T(8,128)(2,1)S(1)}, bf16[4,128,128]{2,1,0:T(8,128)(2,1)}, u32[]{:S(2)}) copy-start(bf16[4,128,128]{2,1,0:T(8,128)(2,1)} %param.13) | copy-start | bytes 393220
  2.1 9.1 %copy-start.3 = (bf16[4,128,128]{2,1,0:T(8,128)(2,1)S(1)}, bf16[4,128,128]{2,1,0:T(8,128)(2,1)}, u32[]{:S(2)}) copy-start(bf16[4,128,128]{2,1,0:T(8,128)(2,1)} %param.14) | copy-start | bytes 393220
  2.1 20.1 %all-to-all-start = ((bf16[8,8,1280]{2,1,0:T(8,128)(2,1)}), bf16[8,8,1280]{2,1,0:T(8,128)(2,1)S(1)}, u32[]{:S(2)}, u32[]{:S(2)}) async-start(bf16[8,8,1280]{2,1,0:T(8,128)(2,1)} %broadcast_in_dim.30), calls=%async_computation | async-start | bytes 327680 | tf_op jit(solution)/shard_map/all_to_all | solution.py:181
  11.5 10.0 %collective-permute-start = (bf16[128,256]{1,0:T(8,128)(2,1)S(1)}, bf16[128,256]{1,0:T(8,128)(2,1)S(1)}, u32[]{:S(2)}, u32[]{:S(2)}) collective-permute-start(bf16[128,256]{1,0:T(8,128)(2,1)S(1)} %get-tuple-element.9), channel_id=1, source_target_pairs={{0,8},{8,16},{16,24},{24,0},{1,9},{9,17},{17,25},{25,1},{2,10},{10... | collective-permute-start | bytes 196616 | tf_op jit(solution)/shard_map/ppermute | solution.py:175
  12.8 8.7 %collective-permute-start.1 = (bf16[128,256]{1,0:T(8,128)(2,1)S(1)}, bf16[128,256]{1,0:T(8,128)(2,1)S(1)}, u32[]{:S(2)}, u32[]{:S(2)}) collective-permute-start(bf16[128,256]{1,0:T(8,128)(2,1)S(1)} %get-tuple-element.8), channel_id=1, source_target_pairs={{0,16},{8,24},{16,0},{24,8},{1,17},{9,25},{17,1},{25,9},{2,18},{10... | collective-permute-start | bytes 196616 | tf_op jit(solution)/shard_map/ppermute | solution.py:175
  15.2 6.3 %collective-permute-start.2 = (bf16[128,256]{1,0:T(8,128)(2,1)S(1)}, bf16[128,256]{1,0:T(8,128)(2,1)S(1)}, u32[]{:S(2)}, u32[]{:S(2)}) collective-permute-start(bf16[128,256]{1,0:T(8,128)(2,1)S(1)} %get-tuple-element.10), channel_id=1, source_target_pairs={{0,24},{8,0},{16,8},{24,16},{1,25},{9,1},{17,9},{25,17},{2,26},{10... | collective-permute-start | bytes 196616 | tf_op jit(solution)/shard_map/ppermute | solution.py:175
  18.3 0.7 copy-start.5
  22.2 0.7 copy-start.1
  25.5 6.8 %copy-start.4 = (bf16[8,1024]{1,0:T(8,128)(2,1)S(1)}, bf16[8,1024]{1,0:T(8,128)(2,1)}, u32[]{:S(2)}) copy-start(bf16[8,1024]{1,0:T(8,128)(2,1)} %param.10) | copy-start | bytes 49156
  25.5 15.0 %all-to-all-start.1 = ((bf16[8,8,1072]{2,1,0:T(8,128)(2,1)}), bf16[8,8,1072]{2,1,0:T(8,128)(2,1)S(1)}, u32[]{:S(2)}, u32[]{:S(2)}) async-start(bf16[8,8,1072]{2,1,0:T(8,128)(2,1)} %bitcast.102), calls=%async_computation.1 | async-start | bytes 294912 | tf_op jit(solution)/shard_map/all_to_all | solution.py:246
  42.7 4.0 %copy-start.6 = (s32[4]{0:T(128)S(1)}, s32[4]{0:T(128)}, u32[]{:S(2)}) copy-start(s32[4]{0:T(128)} %param.19) | copy-start | bytes 52
  42.8 15.9 %all-to-all-start.2 = ((bf16[32,8,1024]{2,1,0:T(8,128)(2,1)}), bf16[32,8,1024]{2,1,0:T(8,128)(2,1)S(1)}, u32[]{:S(2)}, u32[]{:S(2)}) async-start(bf16[32,8,1024]{2,1,0:T(8,128)(2,1)} %broadcast_in_dim.34), calls=%async_computation.2 | async-start | bytes 1048576 | tf_op jit(solution)/shard_map/all_to_all | solution.py:181
  47.8 4.8 %collective-permute-start.3 = (bf16[8,256]{1,0:T(8,128)(2,1)S(1)}, bf16[8,256]{1,0:T(8,128)(2,1)S(1)}, u32[]{:S(2)}, u32[]{:S(2)}) collective-permute-start(bf16[8,256]{1,0:T(8,128)(2,1)S(1)} %convolution_convert_fusion.2), channel_id=1, source_target_pairs={{0,8},{8,16},{16,24},{24,0},{1,9},{9,17},{17,25},{25,1},{2,10},{10... | collective-permute-start | bytes 12296 | tf_op jit(solution)/shard_map/ppermute | solution.py:175
  49.0 4.3 %collective-permute-start.4 = (bf16[8,256]{1,0:T(8,128)(2,1)S(1)}, bf16[8,256]{1,0:T(8,128)(2,1)S(1)}, u32[]{:S(2)}, u32[]{:S(2)}) collective-permute-start(bf16[8,256]{1,0:T(8,128)(2,1)S(1)} %convolution_convert_fusion.2), channel_id=1, source_target_pairs={{0,16},{8,24},{16,0},{24,8},{1,17},{9,25},{17,1},{25,9},{2,18},{10... | collective-permute-start | bytes 12296 | tf_op jit(solution)/shard_map/ppermute | solution.py:175
  51.5 2.8 %collective-permute-start.5 = (bf16[8,256]{1,0:T(8,128)(2,1)S(1)}, bf16[8,256]{1,0:T(8,128)(2,1)S(1)}, u32[]{:S(2)}, u32[]{:S(2)}) collective-permute-start(bf16[8,256]{1,0:T(8,128)(2,1)S(1)} %convolution_convert_fusion.2), channel_id=1, source_target_pairs={{0,24},{8,0},{16,8},{24,16},{1,25},{9,1},{17,9},{25,17},{2,26},{10... | collective-permute-start | bytes 12296 | tf_op jit(solution)/shard_map/ppermute | solution.py:175
  59.7 16.7 %all-to-all-start.3 = ((f32[8,32,256]{2,1,0:T(8,128)}), f32[8,32,256]{2,1,0:T(8,128)S(1)}, u32[]{:S(2)}, u32[]{:S(2)}) async-start(f32[8,32,256]{2,1,0:T(8,128)} %fusion.13), calls=%async_computation.3 | async-start | bytes 524288 | tf_op jit(solution)/shard_map/all_to_all | solution.py:265

commit v9 on v8

--- a/solution.py
+++ b/solution.py
@@ -103,8 +103,9 @@
     return hi, mid, lo
 
 
-def block_attention_kernel(block_len, limit_ref, q_ref, kv_ref, out_ref, stats_ref):
-    blocks = kv_ref.shape[0]
+def block_attention_kernel(block_len, limit_ref, q_ref, *refs):
+    kv_refs, (out_ref, stats_ref) = refs[:-2], refs[-2:]
+    blocks = len(kv_refs)
     rows = out_ref.shape[0]
     heads = stats_ref.shape[1] // 2
     score_scale = 1.0 / math.sqrt(HEAD_SIZE)
@@ -117,7 +118,7 @@
         s = (
             lax.dot_general(
                 q,
-                kv_ref[b, :block_len, :HEAD_SIZE],
+                kv_refs[b][:block_len, :HEAD_SIZE],
                 (((1,), (1,)), ((), ())),
                 preferred_element_type=jnp.float32,
             )
@@ -136,7 +137,7 @@
         total = total + jnp.sum(weights, axis=1, keepdims=True)
         out = out + jnp.dot(
             weights.astype(jnp.bfloat16),
-            kv_ref[b, :block_len, HEAD_SIZE:],
+            kv_refs[b][:block_len, HEAD_SIZE:],
             preferred_element_type=jnp.float32,
         )
     out = out.astype(out_ref.dtype)
@@ -154,12 +155,12 @@
 def block_attention(limit, group_rows, blocks_kv, width, block_len):
     rows = group_rows.shape[0]
     heads = width // HEAD_SIZE
-    blocks = blocks_kv.shape[0]
+    blocks = len(blocks_kv)
     vmem = pl.BlockSpec(memory_space=pltpu.VMEM)
     return pl.pallas_call(
         functools.partial(block_attention_kernel, block_len),
         out_shape=jax.ShapeDtypeStruct((rows, width + 6 * heads), jnp.bfloat16),
-        in_specs=[pl.BlockSpec(memory_space=pltpu.SMEM), vmem, vmem],
+        in_specs=[pl.BlockSpec(memory_space=pltpu.SMEM), vmem] + [vmem] * blocks,
         out_specs=vmem,
         scratch_shapes=[pltpu.VMEM((rows, 2 * heads), jnp.float32)],
         cost_estimate=pl.CostEstimate(
@@ -167,7 +168,7 @@
             transcendentals=rows * heads * blocks * block_len,
             bytes_accessed=2 * (rows * width + 2 * blocks * block_len * HEAD_SIZE + rows * (width + 6 * heads)),
         ),
-    )(limit, group_rows, blocks_kv)
+    )(limit, group_rows, *blocks_kv)
 
 
 def shifted(block, axis_name, shift):
@@ -221,9 +222,7 @@
     ).astype(jnp.bfloat16)
     lanes = cache_pair.shape[0]
     ahead = jnp.roll(cache_pair, -my_x, axis=0)
-    blocks_kv = jnp.stack(
-        [ahead[0]] + [shifted(ahead[k], "bx", k) for k in range(1, lanes)], axis=0
-    )
+    blocks_kv = [ahead[0]] + [shifted(ahead[k], "bx", k) for k in range(1, lanes)]
     path_rel = jnp.stack(
         [path_rows] + [shifted(path_rows, "bx", k) for k in range(1, lanes)], axis=0
     )

time: 78.1 us -> 78 us (level)
  no operation moved by 1% of the time
where the time goes in v9:
time: 78 us; the launch traced here: 76.9 us
  starting transfers between devices  39.8 us (51%)
  waiting for transfers between devices  16.9 us (22%)
  matrix products  6.55 us (8%)
  local copies, waits for them, and re-layouts  6.52 us (8%)
  other arithmetic  3.72 us (5%)
  Pallas kernels  2.58 us (3%)
  between operations  0.84 us (1%)
    all_to_all x2, starting transfers between devices, gather_rows(): lax.all_to_all(spread, axis_name, split_axis=0, concat_axis=0, tiled=True)  13.2 us
    all_to_all x1, starting transfers between devices, on_device(): lax.all_to_all(partial.reshape(kv_count, out_rows, partial.shape[1]), 'kv...  10.2 us
    ppermute x6, starting transfers between devices, shifted(): lax.ppermute(block, axis_name, [(i, (i + shift) % count) for i in range(c...  9.61 us
    all_to_all x1, waiting for transfers between devices, on_device(): lax.all_to_all(packed_out.reshape(ring, rows_dev, -1), 'bz', split_axis=0...  6.82 us
    all_to_all x1, starting transfers between devices, on_device(): lax.all_to_all(packed_out.reshape(ring, rows_dev, -1), 'bz', split_axis=0...  6.77 us
    all_to_all x1, waiting for transfers between devices, on_device(): lax.all_to_all(partial.reshape(kv_count, out_rows, partial.shape[1]), 'kv...  5.54 us
    all_to_all x2, waiting for transfers between devices, gather_rows(): lax.all_to_all(spread, axis_name, split_axis=0, concat_axis=0, tiled=True)  2.9 us
    pallas_call x1, Pallas kernels, block_attention(): pl.pallas_call(functools.partial(block_attention_kernel, block_len), out_...  2.58 us
  transfers between devices with their start and end apart: 10, of which 5 were waited for; matrix products, arithmetic and copies ran while one was open for 13% of the time, Pallas kernels for 0%

profile of v9, /device:TPU:1, one launch (start us, length us, event | category | flops | bytes accessed | tf_op | source)
XLA Modules:
  0.0 76.9 jit_solution(7307027110528553978)
XLA Ops:
  0.6 0.8 %pad_maximum_fusion = bf16[8,1280]{1,0:T(8,128)(2,1)S(1)} fusion(bf16[8,128]{1,0:T(8,128)(2,1)} %param.12, bf16[8,128]{1,0:T(8,128)(2,1)} %param.11, bf16[8,1024]{1,0:T(8,128)(2,1)} %param.10), kind=kLoop, calls=%fused_computation.56 | loop fusion | flops 61440 | bytes 40960 | tf_op jit(solution)/shard_map/concatenate | solution.py:215
  1.5 0.7 broadcast_in_dim.30
  2.1 9.1 %all-to-all-start = ((bf16[8,8,1280]{2,1,0:T(8,128)(2,1)}), bf16[8,8,1280]{2,1,0:T(8,128)(2,1)S(1)}, u32[]{:S(2)}, u32[]{:S(2)}) async-start(bf16[8,8,1280]{2,1,0:T(8,128)(2,1)} %broadcast_in_dim.30), calls=%async_computation | async-start | bytes 327680 | tf_op jit(solution)/shard_map/all_to_all | solution.py:182
  11.4 0.6 slice_bitcast_fusion
  12.1 1.2 %collective-permute-start = (bf16[128,256]{1,0:T(8,128)(2,1)S(1)}, bf16[128,256]{1,0:T(8,128)(2,1)S(1)}, u32[]{:S(2)}, u32[]{:S(2)}) collective-permute-start(bf16[128,256]{1,0:T(8,128)(2,1)S(1)} %get-tuple-element.9), channel_id=1, source_target_pairs={{0,8},{8,16},{16,24},{24,0},{1,9},{9,17},{17,25},{25,1},{2,10},{10... | collective-permute-start | bytes 196616 | tf_op jit(solution)/shard_map/ppermute | solution.py:176
  13.3 2.5 %collective-permute-start.1 = (bf16[128,256]{1,0:T(8,128)(2,1)S(1)}, bf16[128,256]{1,0:T(8,128)(2,1)S(1)}, u32[]{:S(2)}, u32[]{:S(2)}) collective-permute-start(bf16[128,256]{1,0:T(8,128)(2,1)S(1)} %get-tuple-element.8), channel_id=1, source_target_pairs={{0,16},{8,24},{16,0},{24,8},{1,17},{9,25},{17,1},{25,9},{2,18},{10... | collective-permute-start | bytes 196616 | tf_op jit(solution)/shard_map/ppermute | solution.py:176
  15.8 1.2 %collective-permute-start.2 = (bf16[128,256]{1,0:T(8,128)(2,1)S(1)}, bf16[128,256]{1,0:T(8,128)(2,1)S(1)}, u32[]{:S(2)}, u32[]{:S(2)}) collective-permute-start(bf16[128,256]{1,0:T(8,128)(2,1)S(1)} %get-tuple-element.7), channel_id=1, source_target_pairs={{0,24},{8,0},{16,8},{24,16},{1,25},{9,1},{17,9},{25,17},{2,26},{10... | collective-permute-start | bytes 196616 | tf_op jit(solution)/shard_map/ppermute | solution.py:176
  16.9 0.7 fusion.50
  18.9 0.6 copy-done.8
  19.5 0.6 dynamic_slice.18
  20.1 1.2 %fusion.48.limit_ref = s32[4]{0:T(128)} fusion(s32[]{:T(128)S(6)} %axis_index.33, s32[]{:T(128)S(6)} %axis_index.15, s32[]{:T(128)} %bitcast), kind=kLoop, calls=%fused_computation.100 | loop fusion | flops 64 | bytes 28 | tf_op jit(solution)/shard_map/sub | solution.py:241
  21.4 0.7 fusion.51
  22.8 2.6 %shard_map.121 = bf16[64,1072]{1,0:T(8,128)(2,1)} custom-call(s32[4]{0:T(128)} %fusion.48.limit_ref, bf16[64,1280]{1,0:T(8,128)(2,1)} %bitcast.97, bf16[128,256]{1,0:T(8,128)(2,1)} %get-tuple-element.10.refs_0_, bf16[128,256]{1,0:T(8,128)(2,1)} %copy-done.5, bf16[128,256]{1,0:T(8,128)(2,1)} %copy-done.6, bf16[128,256]{1,0:T(8,128)(2,1)} %copy-done.7), custom_call_target="tpu_custom_call" | custom-call | flops 134217728 | bytes 530432 | tf_op jit(solution)/shard_map/pallas_call | solution.py:160
  25.4 6.8 %all-to-all-start.1 = ((bf16[8,8,1072]{2,1,0:T(8,128)(2,1)}), bf16[8,8,1072]{2,1,0:T(8,128)(2,1)S(1)}, u32[]{:S(2)}, u32[]{:S(2)}) async-start(bf16[8,8,1072]{2,1,0:T(8,128)(2,1)} %bitcast.101), calls=%async_computation.1 | async-start | bytes 294912 | tf_op jit(solution)/shard_map/all_to_all | solution.py:245
  32.1 0.9 %fusion.53 = (f32[8,8]{0,1:T(8,128)S(1)}, f32[1,1,1,8,8,64]{5,3,4,0,2,1:T(8,128)S(1)}) fusion(bf16[8,8,128]{2,0,1:T(8,128)(2,1)S(1)} %bitcast.102, bf16[64,1280]{1,0:T(8,128)(2,1)} %bitcast.98, pred[8,64]{1,0:T(8,128)(4,1)S(1)} %fusion.39), kind=kOutput, calls=%fused_computation.106 | convolution fusion | flops 1060800 | bytes 49920 | tf_op jit(solution)/shard_map/rtkgh,rbpkh->brkgtp/dot_general | solution.py:36
  33.5 6.8 %all-to-all-done.1 = bf16[8,8,1072]{2,1,0:T(8,128)(2,1)S(1)} async-done(((bf16[8,8,1072]{2,1,0:T(8,128)(2,1)}), bf16[8,8,1072]{2,1,0:T(8,128)(2,1)S(1)}, u32[]{:S(2)}, u32[]{:S(2)}) %all-to-all-start.1) | async-done | bytes 137248 | tf_op jit(solution)/shard_map/all_to_all | solution.py:245
  40.9 0.8 %fusion.11 = bf16[8,1024]{1,0:T(8,128)(2,1)S(1)} fusion(f32[8,1024]{1,0:T(8,128)S(1)} %fusion.18, bf16[64,1280]{1,0:T(8,128)(2,1)} %bitcast.99, bf16[8,8,64]{2,0,1:T(8,128)(2,1)S(1)} %get-tuple-element.12, f32[8,8]{0,1:T(8,128)S(1)} %copy.29, f32[8,8]{0,1:T(8,128)S(1)} %copy.25), kind=kOutput, calls=%fused_computation.21 | convolution fusion | flops 1081344 | bytes 74240 | tf_op jit(solution)/shard_map/brkgtp,rbpkh->brtkgh/dot_general | solution.py:45
  41.7 0.9 %broadcast_in_dim.34 = bf16[32,8,1024]{2,1,0:T(8,128)(2,1)} broadcast(bf16[8,1024]{1,0:T(8,128)(2,1)S(1)} %fusion.11), dimensions={1,2} | broadcast | bytes 540672 | tf_op jit(solution)/shard_map/broadcast_in_dim | solution.py:181
  42.6 4.0 %all-to-all-start.2 = ((bf16[32,8,1024]{2,1,0:T(8,128)(2,1)}), bf16[32,8,1024]{2,1,0:T(8,128)(2,1)S(1)}, u32[]{:S(2)}, u32[]{:S(2)}) async-start(bf16[32,8,1024]{2,1,0:T(8,128)(2,1)} %broadcast_in_dim.34), calls=%async_computation.2 | async-start | bytes 1048576 | tf_op jit(solution)/shard_map/all_to_all | solution.py:182
  46.7 0.9 %convolution_convert_fusion.2 = bf16[8,256]{1,0:T(8,128)(2,1)S(1)} fusion(bf16[64,1280]{1,0:T(8,128)(2,1)} %bitcast.100, s32[8]{0:T(128)S(1)} %fusion.51), kind=kOutput, calls=%fused_computation.23 | convolution fusion | flops 264704 | bytes 36896 | tf_op jit(solution)/shard_map/dot_general | solution.py:220
  47.7 1.2 %collective-permute-start.3 = (bf16[8,256]{1,0:T(8,128)(2,1)S(1)}, bf16[8,256]{1,0:T(8,128)(2,1)S(1)}, u32[]{:S(2)}, u32[]{:S(2)}) collective-permute-start(bf16[8,256]{1,0:T(8,128)(2,1)S(1)} %convolution_convert_fusion.2), channel_id=1, source_target_pairs={{0,8},{8,16},{16,24},{24,0},{1,9},{9,17},{17,25},{25,1},{2,10},{10... | collective-permute-start | bytes 12296 | tf_op jit(solution)/shard_map/ppermute | solution.py:176
  48.8 2.5 %collective-permute-start.4 = (bf16[8,256]{1,0:T(8,128)(2,1)S(1)}, bf16[8,256]{1,0:T(8,128)(2,1)S(1)}, u32[]{:S(2)}, u32[]{:S(2)}) collective-permute-start(bf16[8,256]{1,0:T(8,128)(2,1)S(1)} %convolution_convert_fusion.2), channel_id=1, source_target_pairs={{0,16},{8,24},{16,0},{24,8},{1,17},{9,25},{17,1},{25,9},{2,18},{10... | collective-permute-start | bytes 12296 | tf_op jit(solution)/shard_map/ppermute | solution.py:176
  51.3 1.1 %collective-permute-start.5 = (bf16[8,256]{1,0:T(8,128)(2,1)S(1)}, bf16[8,256]{1,0:T(8,128)(2,1)S(1)}, u32[]{:S(2)}, u32[]{:S(2)}) collective-permute-start(bf16[8,256]{1,0:T(8,128)(2,1)S(1)} %convolution_convert_fusion.2), channel_id=1, source_target_pairs={{0,24},{8,0},{16,8},{24,16},{1,25},{9,1},{17,9},{25,17},{2,26},{10... | collective-permute-start | bytes 12296 | tf_op jit(solution)/shard_map/ppermute | solution.py:176
  52.5 0.6 collective-permute-done.4
  53.1 1.0 %collective-permute-done.5 = bf16[8,256]{1,0:T(8,128)(2,1)S(1)} collective-permute-done((bf16[8,256]{1,0:T(8,128)(2,1)S(1)}, bf16[8,256]{1,0:T(8,128)(2,1)S(1)}, u32[]{:S(2)}, u32[]{:S(2)}) %collective-permute-start.5) | collective-permute-done | bytes 4128 | tf_op jit(solution)/shard_map/ppermute | solution.py:176
  54.7 0.9 %fusion = bf16[4,128,128]{2,1,0:T(8,128)(2,1)} fusion(bf16[4,128,128]{2,1,0:T(8,128)(2,1)S(1)} %copy-done.2, pred[4,128]{1,0:T(4,128)(4,1)S(1)} %compare_and_fusion, bf16[4,8,256]{2,1,0:T(8,128)(2,1)S(1)} %fusion.26, s32[4,128]{1,0:T(4,128)S(1)} %broadcast_subtract_fusion), kind=kOutput, calls=%fused_computation.3 | convolution fusion | flops 1187840 | bytes 273408 | tf_op jit(solution)/shard_map/rps,rsc->rpc/dot_general | solution.py:92
  55.6 2.9 %all-to-all-done.2 = bf16[32,8,1024]{2,1,0:T(8,128)(2,1)S(1)} async-done(((bf16[32,8,1024]{2,1,0:T(8,128)(2,1)}), bf16[32,8,1024]{2,1,0:T(8,128)(2,1)S(1)}, u32[]{:S(2)}, u32[]{:S(2)}) %all-to-all-start.2) | async-done | bytes 524320 | tf_op jit(solution)/shard_map/all_to_all | solution.py:182
  58.5 1.0 %fusion.13 = f32[8,32,256]{2,1,0:T(8,128)} fusion(bf16[8,32,1024]{2,1,0:T(8,128)(2,1)S(1)} %bitcast.96, bf16[1024,256]{1,0:T(8,128)(2,1)S(1)} %copy-done), kind=kOutput, calls=%fused_computation.28 | convolution fusion | flops 134217728 | bytes 1310720 | tf_op jit(solution)/shard_map/dot_general | solution.py:262
  59.5 10.2 %all-to-all-start.3 = ((f32[8,32,256]{2,1,0:T(8,128)}), f32[8,32,256]{2,1,0:T(8,128)S(1)}, u32[]{:S(2)}, u32[]{:S(2)}) async-start(f32[8,32,256]{2,1,0:T(8,128)} %fusion.13), calls=%async_computation.3 | async-start | bytes 524288 | tf_op jit(solution)/shard_map/all_to_all | solution.py:264
  69.8 0.9 %fusion.1 = bf16[4,128,128]{2,1,0:T(8,128)(2,1)} fusion(bf16[4,128,128]{2,1,0:T(8,128)(2,1)S(1)} %copy-done.3, pred[4,128]{1,0:T(4,128)(4,1)S(1)} %compare_and_fusion, bf16[4,8,256]{2,1,0:T(8,128)(2,1)S(1)} %fusion.26, s32[4,128]{1,0:T(4,128)S(1)} %broadcast_subtract_fusion), kind=kOutput, calls=%fused_computation.4 | convolution fusion | flops 1187840 | bytes 273408 | tf_op jit(solution)/shard_map/rps,rsc->rpc/dot_general | solution.py:92
  70.7 5.5 %all-to-all-done.3 = f32[8,32,256]{2,1,0:T(8,128)S(1)} async-done(((f32[8,32,256]{2,1,0:T(8,128)}), f32[8,32,256]{2,1,0:T(8,128)S(1)}, u32[]{:S(2)}, u32[]{:S(2)}) %all-to-all-start.3) | async-done | bytes 262176 | tf_op jit(solution)/shard_map/all_to_all | solution.py:264
  76.3 0.6 reduce_sum.42
  (56 shorter events, 3.8 us)
Async XLA Ops:
  0.6 57.9 %copy-start = (bf16[1024,256]{1,0:T(8,128)(2,1)S(1)}, bf16[1024,256]{1,0:T(8,128)(2,1)}, u32[]{:S(2)}) copy-start(bf16[1024,256]{1,0:T(8,128)(2,1)} %param.15) | copy-start | bytes 1572868
  2.1 9.1 %copy-start.2 = (bf16[4,128,128]{2,1,0:T(8,128)(2,1)S(1)}, bf16[4,128,128]{2,1,0:T(8,128)(2,1)}, u32[]{:S(2)}) copy-start(bf16[4,128,128]{2,1,0:T(8,128)(2,1)} %param.13) | copy-start | bytes 393220
  2.1 9.1 %copy-start.3 = (bf16[4,128,128]{2,1,0:T(8,128)(2,1)S(1)}, bf16[4,128,128]{2,1,0:T(8,128)(2,1)}, u32[]{:S(2)}) copy-start(bf16[4,128,128]{2,1,0:T(8,128)(2,1)} %param.14) | copy-start | bytes 393220
  2.1 20.0 %all-to-all-start = ((bf16[8,8,1280]{2,1,0:T(8,128)(2,1)}), bf16[8,8,1280]{2,1,0:T(8,128)(2,1)S(1)}, u32[]{:S(2)}, u32[]{:S(2)}) async-start(bf16[8,8,1280]{2,1,0:T(8,128)(2,1)} %broadcast_in_dim.30), calls=%async_computation | async-start | bytes 327680 | tf_op jit(solution)/shard_map/all_to_all | solution.py:182
  12.1 10.0 %collective-permute-start = (bf16[128,256]{1,0:T(8,128)(2,1)S(1)}, bf16[128,256]{1,0:T(8,128)(2,1)S(1)}, u32[]{:S(2)}, u32[]{:S(2)}) collective-permute-start(bf16[128,256]{1,0:T(8,128)(2,1)S(1)} %get-tuple-element.9), channel_id=1, source_target_pairs={{0,8},{8,16},{16,24},{24,0},{1,9},{9,17},{17,25},{25,1},{2,10},{10... | collective-permute-start | bytes 196616 | tf_op jit(solution)/shard_map/ppermute | solution.py:176
  13.3 8.8 %collective-permute-start.1 = (bf16[128,256]{1,0:T(8,128)(2,1)S(1)}, bf16[128,256]{1,0:T(8,128)(2,1)S(1)}, u32[]{:S(2)}, u32[]{:S(2)}) collective-permute-start(bf16[128,256]{1,0:T(8,128)(2,1)S(1)} %get-tuple-element.8), channel_id=1, source_target_pairs={{0,16},{8,24},{16,0},{24,8},{1,17},{9,25},{17,1},{25,9},{2,18},{10... | collective-permute-start | bytes 196616 | tf_op jit(solution)/shard_map/ppermute | solution.py:176
  15.8 6.3 %collective-permute-start.2 = (bf16[128,256]{1,0:T(8,128)(2,1)S(1)}, bf16[128,256]{1,0:T(8,128)(2,1)S(1)}, u32[]{:S(2)}, u32[]{:S(2)}) collective-permute-start(bf16[128,256]{1,0:T(8,128)(2,1)S(1)} %get-tuple-element.7), channel_id=1, source_target_pairs={{0,24},{8,0},{16,8},{24,16},{1,25},{9,1},{17,9},{25,17},{2,26},{10... | collective-permute-start | bytes 196616 | tf_op jit(solution)/shard_map/ppermute | solution.py:176
  18.9 0.7 copy-start.8
  22.1 0.6 copy-start.5
  22.1 0.6 copy-start.6
  22.1 0.6 copy-start.7
  22.1 0.7 copy-start.1
  25.4 6.8 %copy-start.4 = (bf16[8,1024]{1,0:T(8,128)(2,1)S(1)}, bf16[8,1024]{1,0:T(8,128)(2,1)}, u32[]{:S(2)}) copy-start(bf16[8,1024]{1,0:T(8,128)(2,1)} %param.10) | copy-start | bytes 49156
  25.4 15.0 %all-to-all-start.1 = ((bf16[8,8,1072]{2,1,0:T(8,128)(2,1)}), bf16[8,8,1072]{2,1,0:T(8,128)(2,1)S(1)}, u32[]{:S(2)}, u32[]{:S(2)}) async-start(bf16[8,8,1072]{2,1,0:T(8,128)(2,1)} %bitcast.101), calls=%async_computation.1 | async-start | bytes 294912 | tf_op jit(solution)/shard_map/all_to_all | solution.py:245
  42.6 4.0 %copy-start.9 = (s32[4]{0:T(128)S(1)}, s32[4]{0:T(128)}, u32[]{:S(2)}) copy-start(s32[4]{0:T(128)} %param.19) | copy-start | bytes 52
  42.6 15.9 %all-to-all-start.2 = ((bf16[32,8,1024]{2,1,0:T(8,128)(2,1)}), bf16[32,8,1024]{2,1,0:T(8,128)(2,1)S(1)}, u32[]{:S(2)}, u32[]{:S(2)}) async-start(bf16[32,8,1024]{2,1,0:T(8,128)(2,1)} %broadcast_in_dim.34), calls=%async_computation.2 | async-start | bytes 1048576 | tf_op jit(solution)/shard_map/all_to_all | solution.py:182
  47.7 4.8 %collective-permute-start.3 = (bf16[8,256]{1,0:T(8,128)(2,1)S(1)}, bf16[8,256]{1,0:T(8,128)(2,1)S(1)}, u32[]{:S(2)}, u32[]{:S(2)}) collective-permute-start(bf16[8,256]{1,0:T(8,128)(2,1)S(1)} %convolution_convert_fusion.2), channel_id=1, source_target_pairs={{0,8},{8,16},{16,24},{24,0},{1,9},{9,17},{17,25},{25,1},{2,10},{10... | collective-permute-start | bytes 12296 | tf_op jit(solution)/shard_map/ppermute | solution.py:176
  48.8 4.3 %collective-permute-start.4 = (bf16[8,256]{1,0:T(8,128)(2,1)S(1)}, bf16[8,256]{1,0:T(8,128)(2,1)S(1)}, u32[]{:S(2)}, u32[]{:S(2)}) collective-permute-start(bf16[8,256]{1,0:T(8,128)(2,1)S(1)} %convolution_convert_fusion.2), channel_id=1, source_target_pairs={{0,16},{8,24},{16,0},{24,8},{1,17},{9,25},{17,1},{25,9},{2,18},{10... | collective-permute-start | bytes 12296 | tf_op jit(solution)/shard_map/ppermute | solution.py:176
  51.3 2.8 %collective-permute-start.5 = (bf16[8,256]{1,0:T(8,128)(2,1)S(1)}, bf16[8,256]{1,0:T(8,128)(2,1)S(1)}, u32[]{:S(2)}, u32[]{:S(2)}) collective-permute-start(bf16[8,256]{1,0:T(8,128)(2,1)S(1)} %convolution_convert_fusion.2), channel_id=1, source_target_pairs={{0,24},{8,0},{16,8},{24,16},{1,25},{9,1},{17,9},{25,17},{2,26},{10... | collective-permute-start | bytes 12296 | tf_op jit(solution)/shard_map/ppermute | solution.py:176
  59.5 16.7 %all-to-all-start.3 = ((f32[8,32,256]{2,1,0:T(8,128)}), f32[8,32,256]{2,1,0:T(8,128)S(1)}, u32[]{:S(2)}, u32[]{:S(2)}) async-start(f32[8,32,256]{2,1,0:T(8,128)} %fusion.13), calls=%async_computation.3 | async-start | bytes 524288 | tf_op jit(solution)/shard_map/all_to_all | solution.py:264

commit v10 on v9

--- a/solution.py
+++ b/solution.py
@@ -176,11 +176,34 @@
     return lax.ppermute(block, axis_name, [(i, (i + shift) % count) for i in range(count)])
 
 
-def gather_rows(block, axis_name):
+def spread_kernel(*refs):
+    pieces, out_ref = refs[:-1], refs[-1]
+    count = out_ref.shape[0]
+    start = 0
+    for piece in pieces:
+        width = piece.shape[1]
+        out_ref[:, :, start : start + width] = jnp.broadcast_to(
+            piece[...][None], (count,) + piece.shape
+        )
+        start += width
+
+
+def gather_rows(pieces, axis_name):
     count = lax.axis_size(axis_name)
-    spread = jnp.broadcast_to(block[None], (count,) + block.shape)
+    rows = pieces[0].shape[0]
+    width = sum(piece.shape[1] for piece in pieces)
+    vmem = pl.BlockSpec(memory_space=pltpu.VMEM)
+    spread = pl.pallas_call(
+        spread_kernel,
+        out_shape=jax.ShapeDtypeStruct((count, rows, width), pieces[0].dtype),
+        in_specs=[vmem] * len(pieces),
+        out_specs=vmem,
+        cost_estimate=pl.CostEstimate(
+            flops=0, transcendentals=0, bytes_accessed=2 * (count + 1) * rows * width
+        ),
+    )(*pieces)
     moved = lax.all_to_all(spread, axis_name, split_axis=0, concat_axis=0, tiled=True)
-    return moved.reshape((count * block.shape[0],) + block.shape[1:])
+    return moved.reshape((count * rows, width))
 
 
 def on_device(
@@ -211,8 +234,7 @@
     my_request = my_x
     node_start = my_z * rows_dev
     local_queries = queries.reshape(1, rows_dev, kv_local, query_group_width, HEAD_SIZE)
-    own_draft = jnp.concatenate([draft_token_keys, draft_token_values], axis=1)
-    group_rows = gather_rows(jnp.concatenate([queries, own_draft], axis=1), "bz")
+    group_rows = gather_rows([queries, draft_token_keys, draft_token_values], "bz")
     cache_pair = jnp.concatenate([cached_key_vectors, cached_value_vectors], axis=2)
     path_pick = (
         accepted_nodes[my_request][:, None] == jnp.arange(TREE_TOKENS, dtype=jnp.int32)[None, :]
@@ -258,7 +280,7 @@
         moved_stats[..., head_count:],
     )
     attention = merge_parts(cache_part, draft_part, HEAD_SIZE)
-    every_row = gather_rows(attention, blk)
+    every_row = gather_rows([attention], blk)
     partial = jnp.dot(every_row, out_weight, preferred_element_type=jnp.float32)
     out_rows = partial.shape[0] // kv_count
     arrived = lax.all_to_all(

time: 78 us -> 79.3 us (1.017)
  Pallas kernels: 2.58 us -> 5.61 us
  local copies, waits for them, and re-layouts: 6.52 us -> 4.99 us
  other arithmetic: 3.72 us -> 2.91 us
    pallas_call x0 -> x2, Pallas kernels: none -> 3.03 us  [gather_rows(): pl.pallas_call(spread_kernel, out_shape=jax.ShapeDtypeStruct((count, rows...]
    broadcast_in_dim x2 -> x0, local copies, waits for them, and re-layouts: 1.53 us -> none  [gather_rows(): spread = jnp.broadcast_to(block[None], (count,) + block.shape)]
    concatenate x1 -> x0, other arithmetic: 0.81 us -> none  [on_device(): jnp.concatenate([queries, own_draft], axis=1)]
where the time goes in v10:
time: 79.3 us; the launch traced here: 78.2 us
  starting transfers between devices  39.8 us (50%)
  waiting for transfers between devices  16.9 us (21%)
  matrix products  7.16 us (9%)
  Pallas kernels  5.61 us (7%)
  local copies, waits for them, and re-layouts  4.99 us (6%)
  other arithmetic  2.91 us (4%)
  between operations  0.84 us (1%)
    all_to_all x2, starting transfers between devices, gather_rows(): lax.all_to_all(spread, axis_name, split_axis=0, concat_axis=0, tiled=True)  13.2 us
    all_to_all x1, starting transfers between devices, on_device(): lax.all_to_all(partial.reshape(kv_count, out_rows, partial.shape[1]), 'kv...  10.2 us
    ppermute x6, starting transfers between devices, shifted(): lax.ppermute(block, axis_name, [(i, (i + shift) % count) for i in range(c...  9.61 us
    all_to_all x1, waiting for transfers between devices, on_device(): lax.all_to_all(packed_out.reshape(ring, rows_dev, -1), 'bz', split_axis=0...  6.82 us
    all_to_all x1, starting transfers between devices, on_device(): lax.all_to_all(packed_out.reshape(ring, rows_dev, -1), 'bz', split_axis=0...  6.77 us
    all_to_all x1, waiting for transfers between devices, on_device(): lax.all_to_all(partial.reshape(kv_count, out_rows, partial.shape[1]), 'kv...  5.54 us
    pallas_call x2, Pallas kernels, gather_rows(): pl.pallas_call(spread_kernel, out_shape=jax.ShapeDtypeStruct((count, rows...  3.03 us
    all_to_all x2, waiting for transfers between devices, gather_rows(): lax.all_to_all(spread, axis_name, split_axis=0, concat_axis=0, tiled=True)  2.9 us
  transfers between devices with their start and end apart: 10, of which 5 were waited for; matrix products, arithmetic and copies ran while one was open for 13% of the time, Pallas kernels for 0%

profile of v10, /device:TPU:1, one launch (start us, length us, event | category | flops | bytes accessed | tf_op | source)
XLA Modules:
  0.0 78.2 jit_solution(12371426270872117445)
XLA Ops:
  0.6 1.5 %shard_map.121 = bf16[8,8,1280]{2,1,0:T(8,128)(2,1)} custom-call(bf16[8,1024]{1,0:T(8,128)(2,1)} %refs_0_.1, bf16[8,128]{1,0:T(8,128)(2,1)} %refs_1_.1, bf16[8,128]{1,0:T(8,128)(2,1)} %refs_2_.1), custom_call_target="tpu_custom_call" | custom-call | bytes 184320 | tf_op jit(solution)/shard_map/pallas_call | solution.py:196
  2.1 9.1 %all-to-all-start = ((bf16[8,8,1280]{2,1,0:T(8,128)(2,1)}), bf16[8,8,1280]{2,1,0:T(8,128)(2,1)S(1)}, u32[]{:S(2)}, u32[]{:S(2)}) async-start(bf16[8,8,1280]{2,1,0:T(8,128)(2,1)} %shard_map.121), calls=%async_computation | async-start | bytes 327680 | tf_op jit(solution)/shard_map/all_to_all | solution.py:205
  11.4 0.6 slice_bitcast_fusion
  12.1 1.2 %collective-permute-start = (bf16[128,256]{1,0:T(8,128)(2,1)S(1)}, bf16[128,256]{1,0:T(8,128)(2,1)S(1)}, u32[]{:S(2)}, u32[]{:S(2)}) collective-permute-start(bf16[128,256]{1,0:T(8,128)(2,1)S(1)} %get-tuple-element.9), channel_id=1, source_target_pairs={{0,8},{8,16},{16,24},{24,0},{1,9},{9,17},{17,25},{25,1},{2,10},{10... | collective-permute-start | bytes 196616 | tf_op jit(solution)/shard_map/ppermute | solution.py:176
  13.3 2.5 %collective-permute-start.1 = (bf16[128,256]{1,0:T(8,128)(2,1)S(1)}, bf16[128,256]{1,0:T(8,128)(2,1)S(1)}, u32[]{:S(2)}, u32[]{:S(2)}) collective-permute-start(bf16[128,256]{1,0:T(8,128)(2,1)S(1)} %get-tuple-element.8), channel_id=1, source_target_pairs={{0,16},{8,24},{16,0},{24,8},{1,17},{9,25},{17,1},{25,9},{2,18},{10... | collective-permute-start | bytes 196616 | tf_op jit(solution)/shard_map/ppermute | solution.py:176
  15.7 1.2 %collective-permute-start.2 = (bf16[128,256]{1,0:T(8,128)(2,1)S(1)}, bf16[128,256]{1,0:T(8,128)(2,1)S(1)}, u32[]{:S(2)}, u32[]{:S(2)}) collective-permute-start(bf16[128,256]{1,0:T(8,128)(2,1)S(1)} %get-tuple-element.7), channel_id=1, source_target_pairs={{0,24},{8,0},{16,8},{24,16},{1,25},{9,1},{17,9},{25,17},{2,26},{10... | collective-permute-start | bytes 196616 | tf_op jit(solution)/shard_map/ppermute | solution.py:176
  16.9 0.7 fusion.50
  18.8 0.6 copy-done.8
  19.5 0.6 dynamic_slice.18
  20.1 1.2 %fusion.48.limit_ref = s32[4]{0:T(128)} fusion(s32[]{:T(128)S(6)} %axis_index.33, s32[]{:T(128)S(6)} %axis_index.15, s32[]{:T(128)} %bitcast), kind=kLoop, calls=%fused_computation.99 | loop fusion | flops 64 | bytes 28 | tf_op jit(solution)/shard_map/sub | solution.py:263
  21.4 0.7 fusion.51
  22.1 0.6 copy-done.5
  22.8 2.6 %shard_map.122 = bf16[64,1072]{1,0:T(8,128)(2,1)} custom-call(s32[4]{0:T(128)} %fusion.48.limit_ref, bf16[64,1280]{1,0:T(8,128)(2,1)} %bitcast.97, bf16[128,256]{1,0:T(8,128)(2,1)} %get-tuple-element.10.refs_0_, bf16[128,256]{1,0:T(8,128)(2,1)} %copy-done.5, bf16[128,256]{1,0:T(8,128)(2,1)} %copy-done.6, bf16[128,256]{1,0:T(8,128)(2,1)} %copy-done.7), custom_call_target="tpu_custom_call" | custom-call | flops 134217728 | bytes 530432 | tf_op jit(solution)/shard_map/pallas_call | solution.py:160
  25.3 6.8 %all-to-all-start.1 = ((bf16[8,8,1072]{2,1,0:T(8,128)(2,1)}), bf16[8,8,1072]{2,1,0:T(8,128)(2,1)S(1)}, u32[]{:S(2)}, u32[]{:S(2)}) async-start(bf16[8,8,1072]{2,1,0:T(8,128)(2,1)} %bitcast.101), calls=%async_computation.1 | async-start | bytes 294912 | tf_op jit(solution)/shard_map/all_to_all | solution.py:267
  32.1 0.9 %fusion.53 = (f32[8,8]{0,1:T(8,128)S(1)}, f32[1,1,1,8,8,64]{5,3,4,0,2,1:T(8,128)S(1)}) fusion(bf16[8,8,128]{2,0,1:T(8,128)(2,1)S(1)} %bitcast.102, bf16[64,1280]{1,0:T(8,128)(2,1)} %bitcast.98, pred[8,64]{1,0:T(8,128)(4,1)S(1)} %fusion.39), kind=kOutput, calls=%fused_computation.105 | convolution fusion | flops 1060800 | bytes 49920 | tf_op jit(solution)/shard_map/rtkgh,rbpkh->brkgtp/dot_general | solution.py:36
  33.5 6.8 %all-to-all-done.1 = bf16[8,8,1072]{2,1,0:T(8,128)(2,1)S(1)} async-done(((bf16[8,8,1072]{2,1,0:T(8,128)(2,1)}), bf16[8,8,1072]{2,1,0:T(8,128)(2,1)S(1)}, u32[]{:S(2)}, u32[]{:S(2)}) %all-to-all-start.1) | async-done | bytes 137248 | tf_op jit(solution)/shard_map/all_to_all | solution.py:267
  40.9 1.5 %fusion.11.refs_0_ = bf16[8,1024]{1,0:T(8,128)(2,1)} fusion(f32[8,1024]{1,0:T(8,128)S(1)} %fusion.18, bf16[64,1280]{1,0:T(8,128)(2,1)} %bitcast.99, bf16[8,8,64]{2,0,1:T(8,128)(2,1)S(1)} %get-tuple-element.12, f32[8,8]{0,1:T(8,128)S(1)} %copy.29, f32[8,8]{0,1:T(8,128)S(1)} %copy.25), kind=kOutput, calls=%fused_computation.21 | convolution fusion | flops 1081344 | bytes 74240 | tf_op jit(solution)/shard_map/brkgtp,rbpkh->brtkgh/dot_general | solution.py:45
  42.3 1.6 %shard_map.123 = bf16[32,8,1024]{2,1,0:T(8,128)(2,1)} custom-call(bf16[8,1024]{1,0:T(8,128)(2,1)} %fusion.11.refs_0_), custom_call_target="tpu_custom_call" | custom-call | bytes 540672 | tf_op jit(solution)/shard_map/pallas_call | solution.py:196
  43.9 4.0 %all-to-all-start.2 = ((bf16[32,8,1024]{2,1,0:T(8,128)(2,1)}), bf16[32,8,1024]{2,1,0:T(8,128)(2,1)S(1)}, u32[]{:S(2)}, u32[]{:S(2)}) async-start(bf16[32,8,1024]{2,1,0:T(8,128)(2,1)} %shard_map.123), calls=%async_computation.2 | async-start | bytes 1048576 | tf_op jit(solution)/shard_map/all_to_all | solution.py:205
  48.0 0.9 %convolution_convert_fusion.2 = bf16[8,256]{1,0:T(8,128)(2,1)S(1)} fusion(bf16[64,1280]{1,0:T(8,128)(2,1)} %bitcast.100, s32[8]{0:T(128)S(1)} %fusion.51), kind=kOutput, calls=%fused_computation.23 | convolution fusion | flops 264704 | bytes 36896 | tf_op jit(solution)/shard_map/dot_general | solution.py:242
  49.0 1.2 %collective-permute-start.3 = (bf16[8,256]{1,0:T(8,128)(2,1)S(1)}, bf16[8,256]{1,0:T(8,128)(2,1)S(1)}, u32[]{:S(2)}, u32[]{:S(2)}) collective-permute-start(bf16[8,256]{1,0:T(8,128)(2,1)S(1)} %convolution_convert_fusion.2), channel_id=1, source_target_pairs={{0,8},{8,16},{16,24},{24,0},{1,9},{9,17},{17,25},{25,1},{2,10},{10... | collective-permute-start | bytes 12296 | tf_op jit(solution)/shard_map/ppermute | solution.py:176
  50.1 2.5 %collective-permute-start.4 = (bf16[8,256]{1,0:T(8,128)(2,1)S(1)}, bf16[8,256]{1,0:T(8,128)(2,1)S(1)}, u32[]{:S(2)}, u32[]{:S(2)}) collective-permute-start(bf16[8,256]{1,0:T(8,128)(2,1)S(1)} %convolution_convert_fusion.2), channel_id=1, source_target_pairs={{0,16},{8,24},{16,0},{24,8},{1,17},{9,25},{17,1},{25,9},{2,18},{10... | collective-permute-start | bytes 12296 | tf_op jit(solution)/shard_map/ppermute | solution.py:176
  52.6 1.1 %collective-permute-start.5 = (bf16[8,256]{1,0:T(8,128)(2,1)S(1)}, bf16[8,256]{1,0:T(8,128)(2,1)S(1)}, u32[]{:S(2)}, u32[]{:S(2)}) collective-permute-start(bf16[8,256]{1,0:T(8,128)(2,1)S(1)} %convolution_convert_fusion.2), channel_id=1, source_target_pairs={{0,24},{8,0},{16,8},{24,16},{1,25},{9,1},{17,9},{25,17},{2,26},{10... | collective-permute-start | bytes 12296 | tf_op jit(solution)/shard_map/ppermute | solution.py:176
  53.8 0.6 collective-permute-done.4
  54.4 1.0 %collective-permute-done.5 = bf16[8,256]{1,0:T(8,128)(2,1)S(1)} collective-permute-done((bf16[8,256]{1,0:T(8,128)(2,1)S(1)}, bf16[8,256]{1,0:T(8,128)(2,1)S(1)}, u32[]{:S(2)}, u32[]{:S(2)}) %collective-permute-start.5) | collective-permute-done | bytes 4128 | tf_op jit(solution)/shard_map/ppermute | solution.py:176
  56.0 0.9 %fusion = bf16[4,128,128]{2,1,0:T(8,128)(2,1)} fusion(bf16[4,128,128]{2,1,0:T(8,128)(2,1)S(1)} %copy-done.2, pred[4,128]{1,0:T(4,128)(4,1)S(1)} %compare_and_fusion, bf16[4,8,256]{2,1,0:T(8,128)(2,1)S(1)} %fusion.26, s32[4,128]{1,0:T(4,128)S(1)} %broadcast_subtract_fusion), kind=kOutput, calls=%fused_computation.3 | convolution fusion | flops 1187840 | bytes 273408 | tf_op jit(solution)/shard_map/rps,rsc->rpc/dot_general | solution.py:92
  56.9 2.9 %all-to-all-done.2 = bf16[32,8,1024]{2,1,0:T(8,128)(2,1)S(1)} async-done(((bf16[32,8,1024]{2,1,0:T(8,128)(2,1)}), bf16[32,8,1024]{2,1,0:T(8,128)(2,1)S(1)}, u32[]{:S(2)}, u32[]{:S(2)}) %all-to-all-start.2) | async-done | bytes 524320 | tf_op jit(solution)/shard_map/all_to_all | solution.py:205
  59.8 1.0 %fusion.13 = f32[8,32,256]{2,1,0:T(8,128)} fusion(bf16[8,32,1024]{2,1,0:T(8,128)(2,1)S(1)} %bitcast.96, bf16[1024,256]{1,0:T(8,128)(2,1)S(1)} %copy-done), kind=kOutput, calls=%fused_computation.28 | convolution fusion | flops 134217728 | bytes 1310720 | tf_op jit(solution)/shard_map/dot_general | solution.py:284
  60.8 10.2 %all-to-all-start.3 = ((f32[8,32,256]{2,1,0:T(8,128)}), f32[8,32,256]{2,1,0:T(8,128)S(1)}, u32[]{:S(2)}, u32[]{:S(2)}) async-start(f32[8,32,256]{2,1,0:T(8,128)} %fusion.13), calls=%async_computation.3 | async-start | bytes 524288 | tf_op jit(solution)/shard_map/all_to_all | solution.py:286
  71.1 0.9 %fusion.1 = bf16[4,128,128]{2,1,0:T(8,128)(2,1)} fusion(bf16[4,128,128]{2,1,0:T(8,128)(2,1)S(1)} %copy-done.3, pred[4,128]{1,0:T(4,128)(4,1)S(1)} %compare_and_fusion, bf16[4,8,256]{2,1,0:T(8,128)(2,1)S(1)} %fusion.26, s32[4,128]{1,0:T(4,128)S(1)} %broadcast_subtract_fusion), kind=kOutput, calls=%fused_computation.4 | convolution fusion | flops 1187840 | bytes 273408 | tf_op jit(solution)/shard_map/rps,rsc->rpc/dot_general | solution.py:92
  72.0 5.5 %all-to-all-done.3 = f32[8,32,256]{2,1,0:T(8,128)S(1)} async-done(((f32[8,32,256]{2,1,0:T(8,128)}), f32[8,32,256]{2,1,0:T(8,128)S(1)}, u32[]{:S(2)}, u32[]{:S(2)}) %all-to-all-start.3) | async-done | bytes 262176 | tf_op jit(solution)/shard_map/all_to_all | solution.py:286
  77.6 0.6 reduce_sum.42
  (55 shorter events, 3.2 us)
Async XLA Ops:
  0.6 59.2 %copy-start = (bf16[1024,256]{1,0:T(8,128)(2,1)S(1)}, bf16[1024,256]{1,0:T(8,128)(2,1)}, u32[]{:S(2)}) copy-start(bf16[1024,256]{1,0:T(8,128)(2,1)} %param.15) | copy-start | bytes 1572868
  2.1 9.1 %copy-start.2 = (bf16[4,128,128]{2,1,0:T(8,128)(2,1)S(1)}, bf16[4,128,128]{2,1,0:T(8,128)(2,1)}, u32[]{:S(2)}) copy-start(bf16[4,128,128]{2,1,0:T(8,128)(2,1)} %param.13) | copy-start | bytes 393220
  2.1 9.1 %copy-start.3 = (bf16[4,128,128]{2,1,0:T(8,128)(2,1)S(1)}, bf16[4,128,128]{2,1,0:T(8,128)(2,1)}, u32[]{:S(2)}) copy-start(bf16[4,128,128]{2,1,0:T(8,128)(2,1)} %param.14) | copy-start | bytes 393220
  2.1 20.0 %all-to-all-start = ((bf16[8,8,1280]{2,1,0:T(8,128)(2,1)}), bf16[8,8,1280]{2,1,0:T(8,128)(2,1)S(1)}, u32[]{:S(2)}, u32[]{:S(2)}) async-start(bf16[8,8,1280]{2,1,0:T(8,128)(2,1)} %shard_map.121), calls=%async_computation | async-start | bytes 327680 | tf_op jit(solution)/shard_map/all_to_all | solution.py:205
  12.1 10.0 %collective-permute-start = (bf16[128,256]{1,0:T(8,128)(2,1)S(1)}, bf16[128,256]{1,0:T(8,128)(2,1)S(1)}, u32[]{:S(2)}, u32[]{:S(2)}) collective-permute-start(bf16[128,256]{1,0:T(8,128)(2,1)S(1)} %get-tuple-element.9), channel_id=1, source_target_pairs={{0,8},{8,16},{16,24},{24,0},{1,9},{9,17},{17,25},{25,1},{2,10},{10... | collective-permute-start | bytes 196616 | tf_op jit(solution)/shard_map/ppermute | solution.py:176
  13.3 8.8 %collective-permute-start.1 = (bf16[128,256]{1,0:T(8,128)(2,1)S(1)}, bf16[128,256]{1,0:T(8,128)(2,1)S(1)}, u32[]{:S(2)}, u32[]{:S(2)}) collective-permute-start(bf16[128,256]{1,0:T(8,128)(2,1)S(1)} %get-tuple-element.8), channel_id=1, source_target_pairs={{0,16},{8,24},{16,0},{24,8},{1,17},{9,25},{17,1},{25,9},{2,18},{10... | collective-permute-start | bytes 196616 | tf_op jit(solution)/shard_map/ppermute | solution.py:176
  15.7 6.3 %collective-permute-start.2 = (bf16[128,256]{1,0:T(8,128)(2,1)S(1)}, bf16[128,256]{1,0:T(8,128)(2,1)S(1)}, u32[]{:S(2)}, u32[]{:S(2)}) collective-permute-start(bf16[128,256]{1,0:T(8,128)(2,1)S(1)} %get-tuple-element.7), channel_id=1, source_target_pairs={{0,24},{8,0},{16,8},{24,16},{1,25},{9,1},{17,9},{25,17},{2,26},{10... | collective-permute-start | bytes 196616 | tf_op jit(solution)/shard_map/ppermute | solution.py:176
  18.8 0.7 copy-start.8
  22.0 0.6 copy-start.5
  22.0 0.6 copy-start.6
  22.1 0.6 copy-start.7
  22.1 0.7 copy-start.1
  25.3 6.8 %copy-start.4 = (bf16[8,1024]{1,0:T(8,128)(2,1)S(1)}, bf16[8,1024]{1,0:T(8,128)(2,1)}, u32[]{:S(2)}) copy-start(bf16[8,1024]{1,0:T(8,128)(2,1)} %refs_0_.1) | copy-start | bytes 49156
  25.3 15.0 %all-to-all-start.1 = ((bf16[8,8,1072]{2,1,0:T(8,128)(2,1)}), bf16[8,8,1072]{2,1,0:T(8,128)(2,1)S(1)}, u32[]{:S(2)}, u32[]{:S(2)}) async-start(bf16[8,8,1072]{2,1,0:T(8,128)(2,1)} %bitcast.101), calls=%async_computation.1 | async-start | bytes 294912 | tf_op jit(solution)/shard_map/all_to_all | solution.py:267
  43.9 4.0 %copy-start.9 = (s32[4]{0:T(128)S(1)}, s32[4]{0:T(128)}, u32[]{:S(2)}) copy-start(s32[4]{0:T(128)} %param.19) | copy-start | bytes 52
  43.9 15.9 %all-to-all-start.2 = ((bf16[32,8,1024]{2,1,0:T(8,128)(2,1)}), bf16[32,8,1024]{2,1,0:T(8,128)(2,1)S(1)}, u32[]{:S(2)}, u32[]{:S(2)}) async-start(bf16[32,8,1024]{2,1,0:T(8,128)(2,1)} %shard_map.123), calls=%async_computation.2 | async-start | bytes 1048576 | tf_op jit(solution)/shard_map/all_to_all | solution.py:205
  49.0 4.8 %collective-permute-start.3 = (bf16[8,256]{1,0:T(8,128)(2,1)S(1)}, bf16[8,256]{1,0:T(8,128)(2,1)S(1)}, u32[]{:S(2)}, u32[]{:S(2)}) collective-permute-start(bf16[8,256]{1,0:T(8,128)(2,1)S(1)} %convolution_convert_fusion.2), channel_id=1, source_target_pairs={{0,8},{8,16},{16,24},{24,0},{1,9},{9,17},{17,25},{25,1},{2,10},{10... | collective-permute-start | bytes 12296 | tf_op jit(solution)/shard_map/ppermute | solution.py:176
  50.1 4.3 %collective-permute-start.4 = (bf16[8,256]{1,0:T(8,128)(2,1)S(1)}, bf16[8,256]{1,0:T(8,128)(2,1)S(1)}, u32[]{:S(2)}, u32[]{:S(2)}) collective-permute-start(bf16[8,256]{1,0:T(8,128)(2,1)S(1)} %convolution_convert_fusion.2), channel_id=1, source_target_pairs={{0,16},{8,24},{16,0},{24,8},{1,17},{9,25},{17,1},{25,9},{2,18},{10... | collective-permute-start | bytes 12296 | tf_op jit(solution)/shard_map/ppermute | solution.py:176
  52.6 2.8 %collective-permute-start.5 = (bf16[8,256]{1,0:T(8,128)(2,1)S(1)}, bf16[8,256]{1,0:T(8,128)(2,1)S(1)}, u32[]{:S(2)}, u32[]{:S(2)}) collective-permute-start(bf16[8,256]{1,0:T(8,128)(2,1)S(1)} %convolution_convert_fusion.2), channel_id=1, source_target_pairs={{0,24},{8,0},{16,8},{24,16},{1,25},{9,1},{17,9},{25,17},{2,26},{10... | collective-permute-start | bytes 12296 | tf_op jit(solution)/shard_map/ppermute | solution.py:176
  60.8 16.7 %all-to-all-start.3 = ((f32[8,32,256]{2,1,0:T(8,128)}), f32[8,32,256]{2,1,0:T(8,128)S(1)}, u32[]{:S(2)}, u32[]{:S(2)}) async-start(f32[8,32,256]{2,1,0:T(8,128)} %fusion.13), calls=%async_computation.3 | async-start | bytes 524288 | tf_op jit(solution)/shard_map/all_to_all | solution.py:286

commit v11 on v9

--- a/solution.py
+++ b/solution.py
@@ -174,6 +174,59 @@
 def shifted(block, axis_name, shift):
     count = lax.axis_size(axis_name)
     return lax.ppermute(block, axis_name, [(i, (i + shift) % count) for i in range(count)])
+
+
+def merge_kernel(moved_ref, dout_ref, dpeak_ref, dsum_ref, out_ref):
+    sources = moved_ref.shape[0]
+    width = dout_ref.shape[1]
+    heads = width // HEAD_SIZE
+    peaks, sums = [], []
+    for s in range(sources):
+        part = [
+            moved_ref[s, :, width + j * 2 * heads : width + (j + 1) * 2 * heads].astype(jnp.float32)
+            for j in range(3)
+        ]
+        stats = (part[0] + part[1]) + part[2]
+        peaks.append(stats[:, :heads])
+        sums.append(stats[:, heads:])
+    draft_peak = dpeak_ref[...]
+    overall = peaks[0]
+    for peak in peaks[1:]:
+        overall = jnp.maximum(overall, peak)
+    overall = jnp.maximum(overall, draft_peak)
+    factors = [jnp.exp(peak - overall) for peak in peaks]
+    draft_factor = jnp.exp(draft_peak - overall)
+    den = factors[0] * sums[0]
+    for factor, total in zip(factors[1:], sums[1:]):
+        den = den + factor * total
+    den = den + draft_factor * dsum_ref[...]
+    count = out_ref.shape[0]
+    for h in range(heads):
+        cols = slice(h * HEAD_SIZE, (h + 1) * HEAD_SIZE)
+        num = factors[0][:, h : h + 1] * moved_ref[0, :, cols].astype(jnp.float32)
+        for s in range(1, sources):
+            num = num + factors[s][:, h : h + 1] * moved_ref[s, :, cols].astype(jnp.float32)
+        num = num + draft_factor[:, h : h + 1] * dout_ref[:, cols]
+        att = (num / den[:, h : h + 1]).astype(out_ref.dtype)
+        out_ref[:, :, cols] = jnp.broadcast_to(att[None], (count,) + att.shape)
+
+
+def merge_and_spread(moved, draft_part, count):
+    draft_out, draft_peak, draft_sum = draft_part
+    rows = moved.shape[1]
+    width = draft_out.shape[-1]
+    vmem = pl.BlockSpec(memory_space=pltpu.VMEM)
+    return pl.pallas_call(
+        merge_kernel,
+        out_shape=jax.ShapeDtypeStruct((count, rows, width), jnp.bfloat16),
+        in_specs=[vmem] * 4,
+        out_specs=vmem,
+        cost_estimate=pl.CostEstimate(
+            flops=4 * moved.shape[0] * rows * width,
+            transcendentals=2 * moved.shape[0] * rows * width // HEAD_SIZE,
+            bytes_accessed=2 * moved.size + 4 * rows * width + 2 * count * rows * width,
+        ),
+    )(moved, draft_out[0], draft_peak[0], draft_sum[0])
 
 
 def gather_rows(block, axis_name):
@@ -245,20 +298,10 @@
     moved = lax.all_to_all(
         packed_out.reshape(ring, rows_dev, -1), "bz", split_axis=0, concat_axis=0, tiled=True
     )
-    parts = [
-        moved[..., width_out + j * 2 * head_count : width_out + (j + 1) * 2 * head_count].astype(
-            jnp.float32
-        )
-        for j in range(3)
-    ]
-    moved_stats = (parts[0] + parts[1]) + parts[2]
-    cache_part = (
-        moved[..., :width_out],
-        moved_stats[..., :head_count],
-        moved_stats[..., head_count:],
-    )
-    attention = merge_parts(cache_part, draft_part, HEAD_SIZE)
-    every_row = gather_rows(attention, blk)
+    spread = merge_and_spread(moved, draft_part, lax.axis_size(blk))
+    every_row = lax.all_to_all(spread, blk, split_axis=0, concat_axis=0, tiled=True).reshape(
+        -1, width_q
+    )
     partial = jnp.dot(every_row, out_weight, preferred_element_type=jnp.float32)
     out_rows = partial.shape[0] // kv_count
     arrived = lax.all_to_all(

time: 78 us -> 78.5 us (level)
  waiting for transfers between devices: 16.9 us -> 14.2 us
  Pallas kernels: 2.58 us -> 4.66 us
    all_to_all x2 -> x1, starting transfers between devices: 13.2 us -> 9.13 us  [gather_rows(): lax.all_to_all(spread, axis_name, split_axis=0, concat_axis=0, tiled=True)]
    all_to_all x0 -> x1, starting transfers between devices: none -> 4.02 us  [on_device(): lax.all_to_all(spread, blk, split_axis=0, concat_axis=0, tiled=True)]
    all_to_all x2 -> x1, waiting for transfers between devices: 2.9 us -> 0.01 us  [gather_rows(): lax.all_to_all(spread, axis_name, split_axis=0, concat_axis=0, tiled=True)]
    all_to_all x0 -> x1, waiting for transfers between devices: none -> 2.9 us  [on_device(): lax.all_to_all(spread, blk, split_axis=0, concat_axis=0, tiled=True)]
    all_to_all x1, waiting for transfers between devices: 6.82 us -> 4.18 us  [on_device(): lax.all_to_all(packed_out.reshape(ring, rows_dev, -1), 'bz', split_axis=0...]
    pallas_call x0 -> x1, Pallas kernels: none -> 2.08 us  [merge_and_spread(): pl.pallas_call(merge_kernel, out_shape=jax.ShapeDtypeStruct((count, rows,...]
    broadcast_in_dim x2 -> x1, local copies, waits for them, and re-layouts: 1.53 us -> 0.67 us  [gather_rows(): spread = jnp.broadcast_to(block[None], (count,) + block.shape)]
    unnamed x20 -> x22, local copies, waits for them, and re-layouts: 1.34 us -> 2.01 us
  transfers between devices with their start and end apart: 10 -> 10, of which waited for: 5 -> 5; matrix products, arithmetic and copies ran while one was open for 13% -> 17% of each run, Pallas kernels for 0% -> 0%
where the time goes in v11:
time: 78.5 us; the launch traced here: 77.4 us
  starting transfers between devices  39.8 us (51%)
  waiting for transfers between devices  14.2 us (18%)
  local copies, waits for them, and re-layouts  7.3 us (9%)
  matrix products  7.15 us (9%)
  Pallas kernels  4.66 us (6%)
  other arithmetic  3.43 us (4%)
  between operations  0.83 us (1%)
    all_to_all x1, starting transfers between devices, on_device(): lax.all_to_all(partial.reshape(kv_count, out_rows, partial.shape[1]), 'kv...  10.3 us
    ppermute x6, starting transfers between devices, shifted(): lax.ppermute(block, axis_name, [(i, (i + shift) % count) for i in range(c...  9.61 us
    all_to_all x1, starting transfers between devices, gather_rows(): lax.all_to_all(spread, axis_name, split_axis=0, concat_axis=0, tiled=True)  9.13 us
    all_to_all x1, starting transfers between devices, on_device(): lax.all_to_all(packed_out.reshape(ring, rows_dev, -1), 'bz', split_axis=0...  6.77 us
    all_to_all x1, waiting for transfers between devices, on_device(): lax.all_to_all(partial.reshape(kv_count, out_rows, partial.shape[1]), 'kv...  5.54 us
    all_to_all x1, waiting for transfers between devices, on_device(): lax.all_to_all(packed_out.reshape(ring, rows_dev, -1), 'bz', split_axis=0...  4.18 us
    all_to_all x1, starting transfers between devices, on_device(): lax.all_to_all(spread, blk, split_axis=0, concat_axis=0, tiled=True)  4.02 us
    all_to_all x1, waiting for transfers between devices, on_device(): lax.all_to_all(spread, blk, split_axis=0, concat_axis=0, tiled=True)  2.9 us
  transfers between devices with their start and end apart: 10, of which 5 were waited for; matrix products, arithmetic and copies ran while one was open for 17% of the time, Pallas kernels for 0%

profile of v11, /device:TPU:1, one launch (start us, length us, event | category | flops | bytes accessed | tf_op | source)
XLA Modules:
  0.0 77.4 jit_solution(2752258280538576956)
XLA Ops:
  0.6 0.8 %pad_maximum_fusion = bf16[8,1280]{1,0:T(8,128)(2,1)S(1)} fusion(bf16[8,128]{1,0:T(8,128)(2,1)} %param.12, bf16[8,128]{1,0:T(8,128)(2,1)} %param.11, bf16[8,1024]{1,0:T(8,128)(2,1)} %param.10), kind=kLoop, calls=%fused_computation.45 | loop fusion | flops 61440 | bytes 40960 | tf_op jit(solution)/shard_map/concatenate | solution.py:268
  1.5 0.7 broadcast_in_dim.28
  2.1 9.1 %all-to-all-start = ((bf16[8,8,1280]{2,1,0:T(8,128)(2,1)}), bf16[8,8,1280]{2,1,0:T(8,128)(2,1)S(1)}, u32[]{:S(2)}, u32[]{:S(2)}) async-start(bf16[8,8,1280]{2,1,0:T(8,128)(2,1)} %broadcast_in_dim.28), calls=%async_computation | async-start | bytes 327680 | tf_op jit(solution)/shard_map/all_to_all | solution.py:235
  11.4 0.6 slice_bitcast_fusion
  12.1 1.2 %collective-permute-start = (bf16[128,256]{1,0:T(8,128)(2,1)S(1)}, bf16[128,256]{1,0:T(8,128)(2,1)S(1)}, u32[]{:S(2)}, u32[]{:S(2)}) collective-permute-start(bf16[128,256]{1,0:T(8,128)(2,1)S(1)} %get-tuple-element.5), channel_id=1, source_target_pairs={{0,8},{8,16},{16,24},{24,0},{1,9},{9,17},{17,25},{25,1},{2,10},{10... | collective-permute-start | bytes 196616 | tf_op jit(solution)/shard_map/ppermute | solution.py:176
  13.3 2.5 %collective-permute-start.1 = (bf16[128,256]{1,0:T(8,128)(2,1)S(1)}, bf16[128,256]{1,0:T(8,128)(2,1)S(1)}, u32[]{:S(2)}, u32[]{:S(2)}) collective-permute-start(bf16[128,256]{1,0:T(8,128)(2,1)S(1)} %get-tuple-element.4), channel_id=1, source_target_pairs={{0,16},{8,24},{16,0},{24,8},{1,17},{9,25},{17,1},{25,9},{2,18},{10... | collective-permute-start | bytes 196616 | tf_op jit(solution)/shard_map/ppermute | solution.py:176
  15.7 1.2 %collective-permute-start.2 = (bf16[128,256]{1,0:T(8,128)(2,1)S(1)}, bf16[128,256]{1,0:T(8,128)(2,1)S(1)}, u32[]{:S(2)}, u32[]{:S(2)}) collective-permute-start(bf16[128,256]{1,0:T(8,128)(2,1)S(1)} %get-tuple-element.3), channel_id=1, source_target_pairs={{0,24},{8,0},{16,8},{24,16},{1,25},{9,1},{17,9},{25,17},{2,26},{10... | collective-permute-start | bytes 196616 | tf_op jit(solution)/shard_map/ppermute | solution.py:176
  16.9 0.7 fusion.42
  18.9 0.6 copy-done.9
  20.1 1.2 %fusion.40.limit_ref = s32[4]{0:T(128)} fusion(s32[]{:T(128)S(6)} %axis_index.33, s32[]{:T(128)S(6)} %axis_index.15, s32[]{:T(128)} %bitcast), kind=kLoop, calls=%fused_computation.84 | loop fusion | flops 64 | bytes 28 | tf_op jit(solution)/shard_map/sub | solution.py:294
  21.4 0.7 fusion.43
  22.8 2.6 %shard_map.121 = bf16[64,1072]{1,0:T(8,128)(2,1)} custom-call(s32[4]{0:T(128)} %fusion.40.limit_ref, bf16[64,1280]{1,0:T(8,128)(2,1)} %bitcast.71, bf16[128,256]{1,0:T(8,128)(2,1)} %get-tuple-element.6.refs_0_, bf16[128,256]{1,0:T(8,128)(2,1)} %copy-done.6, bf16[128,256]{1,0:T(8,128)(2,1)} %copy-done.7, bf16[128,256]{1,0:T(8,128)(2,1)} %copy-done.8), custom_call_target="tpu_custom_call" | custom-call | flops 134217728 | bytes 530432 | tf_op jit(solution)/shard_map/pallas_call | solution.py:160
  25.4 6.8 %all-to-all-start.1 = ((bf16[8,8,1072]{2,1,0:T(8,128)(2,1)}), bf16[8,8,1072]{2,1,0:T(8,128)(2,1)S(1)}, u32[]{:S(2)}, u32[]{:S(2)}) async-start(bf16[8,8,1072]{2,1,0:T(8,128)(2,1)} %bitcast.75), calls=%async_computation.1 | async-start | bytes 294912 | tf_op jit(solution)/shard_map/all_to_all | solution.py:298
  32.2 0.9 %fusion.44 = (f32[8,8]{0,1:T(8,128)S(1)}, f32[1,1,1,8,8,64]{5,3,4,0,2,1:T(8,128)S(1)}) fusion(bf16[8,8,128]{2,0,1:T(8,128)(2,1)S(1)} %bitcast.76, bf16[64,1280]{1,0:T(8,128)(2,1)} %bitcast.72, pred[8,64]{1,0:T(8,128)(4,1)S(1)} %fusion.33), kind=kOutput, calls=%fused_computation.90 | convolution fusion | flops 1060800 | bytes 49920 | tf_op jit(solution)/shard_map/rtkgh,rbpkh->brkgtp/dot_general | solution.py:36
  33.4 0.7 copy.23
  34.1 0.7 copy.21
  34.8 1.5 %convolution_bitcast_fusion.dout_ref = f32[8,1024]{1,0:T(8,128)} fusion(bf16[64,1280]{1,0:T(8,128)(2,1)} %bitcast.73, bf16[8,8,64]{2,0,1:T(8,128)(2,1)S(1)} %get-tuple-element.8), kind=kOutput, calls=%fused_computation.13 | convolution fusion | flops 1048576 | bytes 57344 | tf_op jit(solution)/shard_map/brkgtp,rbpkh->brtkgh/dot_general | solution.py:45
  36.2 4.2 %all-to-all-done.1.moved_ref = bf16[8,8,1072]{2,1,0:T(8,128)(2,1)S(1)} async-done(((bf16[8,8,1072]{2,1,0:T(8,128)(2,1)}), bf16[8,8,1072]{2,1,0:T(8,128)(2,1)S(1)}, u32[]{:S(2)}, u32[]{:S(2)}) %all-to-all-start.1) | async-done | bytes 137248 | tf_op jit(solution)/shard_map/all_to_all | solution.py:298
  40.4 0.7 copy-done.2
  41.0 2.1 %shard_map.122 = bf16[32,8,1024]{2,1,0:T(8,128)(2,1)} custom-call(bf16[8,8,1072]{2,1,0:T(8,128)(2,1)} %copy-done.2, f32[8,1024]{1,0:T(8,128)} %convolution_bitcast_fusion.dout_ref, f32[8,8]{1,0:T(8,128)} %bitcast.79, f32[8,8]{1,0:T(8,128)} %bitcast.78), custom_call_target="tpu_custom_call" | custom-call | flops 262144 | bytes 694272 | tf_op jit(solution)/shard_map/pallas_call | solution.py:219
  43.1 4.0 %all-to-all-start.2 = ((bf16[32,8,1024]{2,1,0:T(8,128)(2,1)}), bf16[32,8,1024]{2,1,0:T(8,128)(2,1)S(1)}, u32[]{:S(2)}, u32[]{:S(2)}) async-start(bf16[32,8,1024]{2,1,0:T(8,128)(2,1)} %shard_map.122), calls=%async_computation.2 | async-start | bytes 1048576 | tf_op jit(solution)/shard_map/all_to_all | solution.py:302
  47.2 0.9 %convolution_convert_fusion.2 = bf16[8,256]{1,0:T(8,128)(2,1)S(1)} fusion(bf16[64,1280]{1,0:T(8,128)(2,1)} %bitcast.74, s32[8]{0:T(128)S(1)} %fusion.43), kind=kOutput, calls=%fused_computation.19 | convolution fusion | flops 264704 | bytes 36896 | tf_op jit(solution)/shard_map/dot_general | solution.py:273
  48.2 1.2 %collective-permute-start.3 = (bf16[8,256]{1,0:T(8,128)(2,1)S(1)}, bf16[8,256]{1,0:T(8,128)(2,1)S(1)}, u32[]{:S(2)}, u32[]{:S(2)}) collective-permute-start(bf16[8,256]{1,0:T(8,128)(2,1)S(1)} %convolution_convert_fusion.2), channel_id=1, source_target_pairs={{0,8},{8,16},{16,24},{24,0},{1,9},{9,17},{17,25},{25,1},{2,10},{10... | collective-permute-start | bytes 12296 | tf_op jit(solution)/shard_map/ppermute | solution.py:176
  49.4 2.5 %collective-permute-start.4 = (bf16[8,256]{1,0:T(8,128)(2,1)S(1)}, bf16[8,256]{1,0:T(8,128)(2,1)S(1)}, u32[]{:S(2)}, u32[]{:S(2)}) collective-permute-start(bf16[8,256]{1,0:T(8,128)(2,1)S(1)} %convolution_convert_fusion.2), channel_id=1, source_target_pairs={{0,16},{8,24},{16,0},{24,8},{1,17},{9,25},{17,1},{25,9},{2,18},{10... | collective-permute-start | bytes 12296 | tf_op jit(solution)/shard_map/ppermute | solution.py:176
  51.9 1.1 %collective-permute-start.5 = (bf16[8,256]{1,0:T(8,128)(2,1)S(1)}, bf16[8,256]{1,0:T(8,128)(2,1)S(1)}, u32[]{:S(2)}, u32[]{:S(2)}) collective-permute-start(bf16[8,256]{1,0:T(8,128)(2,1)S(1)} %convolution_convert_fusion.2), channel_id=1, source_target_pairs={{0,24},{8,0},{16,8},{24,16},{1,25},{9,1},{17,9},{25,17},{2,26},{10... | collective-permute-start | bytes 12296 | tf_op jit(solution)/shard_map/ppermute | solution.py:176
  53.6 1.0 %collective-permute-done.5 = bf16[8,256]{1,0:T(8,128)(2,1)S(1)} collective-permute-done((bf16[8,256]{1,0:T(8,128)(2,1)S(1)}, bf16[8,256]{1,0:T(8,128)(2,1)S(1)}, u32[]{:S(2)}, u32[]{:S(2)}) %collective-permute-start.5) | collective-permute-done | bytes 4128 | tf_op jit(solution)/shard_map/ppermute | solution.py:176
  55.2 0.9 %fusion = bf16[4,128,128]{2,1,0:T(8,128)(2,1)} fusion(bf16[4,128,128]{2,1,0:T(8,128)(2,1)S(1)} %copy-done.3, pred[4,128]{1,0:T(4,128)(4,1)S(1)} %compare_and_fusion, bf16[4,8,256]{2,1,0:T(8,128)(2,1)S(1)} %fusion.20, s32[4,128]{1,0:T(4,128)S(1)} %broadcast_subtract_fusion), kind=kOutput, calls=%fused_computation.3 | convolution fusion | flops 1187840 | bytes 273408 | tf_op jit(solution)/shard_map/rps,rsc->rpc/dot_general | solution.py:92
  56.2 2.9 %all-to-all-done.2 = bf16[32,8,1024]{2,1,0:T(8,128)(2,1)S(1)} async-done(((bf16[32,8,1024]{2,1,0:T(8,128)(2,1)}), bf16[32,8,1024]{2,1,0:T(8,128)(2,1)S(1)}, u32[]{:S(2)}, u32[]{:S(2)}) %all-to-all-start.2) | async-done | bytes 524320 | tf_op jit(solution)/shard_map/all_to_all | solution.py:302
  59.1 1.0 %fusion.9 = f32[8,32,256]{2,1,0:T(8,128)} fusion(bf16[8,32,1024]{2,1,0:T(8,128)(2,1)S(1)} %bitcast.70, bf16[1024,256]{1,0:T(8,128)(2,1)S(1)} %copy-done), kind=kOutput, calls=%fused_computation.24 | convolution fusion | flops 134217728 | bytes 1310720 | tf_op jit(solution)/shard_map/dot_general | solution.py:305
  60.0 10.3 %all-to-all-start.3 = ((f32[8,32,256]{2,1,0:T(8,128)}), f32[8,32,256]{2,1,0:T(8,128)S(1)}, u32[]{:S(2)}, u32[]{:S(2)}) async-start(f32[8,32,256]{2,1,0:T(8,128)} %fusion.9), calls=%async_computation.3 | async-start | bytes 524288 | tf_op jit(solution)/shard_map/all_to_all | solution.py:307
  70.3 0.9 %fusion.1 = bf16[4,128,128]{2,1,0:T(8,128)(2,1)} fusion(bf16[4,128,128]{2,1,0:T(8,128)(2,1)S(1)} %copy-done.4, pred[4,128]{1,0:T(4,128)(4,1)S(1)} %compare_and_fusion, bf16[4,8,256]{2,1,0:T(8,128)(2,1)S(1)} %fusion.20, s32[4,128]{1,0:T(4,128)S(1)} %broadcast_subtract_fusion), kind=kOutput, calls=%fused_computation.4 | convolution fusion | flops 1187840 | bytes 273408 | tf_op jit(solution)/shard_map/rps,rsc->rpc/dot_general | solution.py:92
  71.2 5.5 %all-to-all-done.3 = f32[8,32,256]{2,1,0:T(8,128)S(1)} async-done(((f32[8,32,256]{2,1,0:T(8,128)}), f32[8,32,256]{2,1,0:T(8,128)S(1)}, u32[]{:S(2)}, u32[]{:S(2)}) %all-to-all-start.3) | async-done | bytes 262176 | tf_op jit(solution)/shard_map/all_to_all | solution.py:307
  (49 shorter events, 5.0 us)
Async XLA Ops:
  0.6 58.4 %copy-start = (bf16[1024,256]{1,0:T(8,128)(2,1)S(1)}, bf16[1024,256]{1,0:T(8,128)(2,1)}, u32[]{:S(2)}) copy-start(bf16[1024,256]{1,0:T(8,128)(2,1)} %param.15) | copy-start | bytes 1572868
  2.1 9.1 %copy-start.3 = (bf16[4,128,128]{2,1,0:T(8,128)(2,1)S(1)}, bf16[4,128,128]{2,1,0:T(8,128)(2,1)}, u32[]{:S(2)}) copy-start(bf16[4,128,128]{2,1,0:T(8,128)(2,1)} %param.13) | copy-start | bytes 393220
  2.1 9.1 %copy-start.4 = (bf16[4,128,128]{2,1,0:T(8,128)(2,1)S(1)}, bf16[4,128,128]{2,1,0:T(8,128)(2,1)}, u32[]{:S(2)}) copy-start(bf16[4,128,128]{2,1,0:T(8,128)(2,1)} %param.14) | copy-start | bytes 393220
  2.1 20.0 %all-to-all-start = ((bf16[8,8,1280]{2,1,0:T(8,128)(2,1)}), bf16[8,8,1280]{2,1,0:T(8,128)(2,1)S(1)}, u32[]{:S(2)}, u32[]{:S(2)}) async-start(bf16[8,8,1280]{2,1,0:T(8,128)(2,1)} %broadcast_in_dim.28), calls=%async_computation | async-start | bytes 327680 | tf_op jit(solution)/shard_map/all_to_all | solution.py:235
  12.1 10.0 %collective-permute-start = (bf16[128,256]{1,0:T(8,128)(2,1)S(1)}, bf16[128,256]{1,0:T(8,128)(2,1)S(1)}, u32[]{:S(2)}, u32[]{:S(2)}) collective-permute-start(bf16[128,256]{1,0:T(8,128)(2,1)S(1)} %get-tuple-element.5), channel_id=1, source_target_pairs={{0,8},{8,16},{16,24},{24,0},{1,9},{9,17},{17,25},{25,1},{2,10},{10... | collective-permute-start | bytes 196616 | tf_op jit(solution)/shard_map/ppermute | solution.py:176
  13.3 8.8 %collective-permute-start.1 = (bf16[128,256]{1,0:T(8,128)(2,1)S(1)}, bf16[128,256]{1,0:T(8,128)(2,1)S(1)}, u32[]{:S(2)}, u32[]{:S(2)}) collective-permute-start(bf16[128,256]{1,0:T(8,128)(2,1)S(1)} %get-tuple-element.4), channel_id=1, source_target_pairs={{0,16},{8,24},{16,0},{24,8},{1,17},{9,25},{17,1},{25,9},{2,18},{10... | collective-permute-start | bytes 196616 | tf_op jit(solution)/shard_map/ppermute | solution.py:176
  15.7 6.4 %collective-permute-start.2 = (bf16[128,256]{1,0:T(8,128)(2,1)S(1)}, bf16[128,256]{1,0:T(8,128)(2,1)S(1)}, u32[]{:S(2)}, u32[]{:S(2)}) collective-permute-start(bf16[128,256]{1,0:T(8,128)(2,1)S(1)} %get-tuple-element.3), channel_id=1, source_target_pairs={{0,24},{8,0},{16,8},{24,16},{1,25},{9,1},{17,9},{25,17},{2,26},{10... | collective-permute-start | bytes 196616 | tf_op jit(solution)/shard_map/ppermute | solution.py:176
  18.8 0.7 copy-start.9
  22.1 0.6 copy-start.6
  22.1 0.6 copy-start.7
  22.1 0.6 copy-start.8
  22.1 0.7 copy-start.1
  25.4 6.8 %copy-start.5 = (bf16[8,1024]{1,0:T(8,128)(2,1)S(1)}, bf16[8,1024]{1,0:T(8,128)(2,1)}, u32[]{:S(2)}) copy-start(bf16[8,1024]{1,0:T(8,128)(2,1)} %param.10) | copy-start | bytes 49156
  25.4 15.0 %all-to-all-start.1 = ((bf16[8,8,1072]{2,1,0:T(8,128)(2,1)}), bf16[8,8,1072]{2,1,0:T(8,128)(2,1)S(1)}, u32[]{:S(2)}, u32[]{:S(2)}) async-start(bf16[8,8,1072]{2,1,0:T(8,128)(2,1)} %bitcast.75), calls=%async_computation.1 | async-start | bytes 294912 | tf_op jit(solution)/shard_map/all_to_all | solution.py:298
  40.4 0.7 copy-start.2
  43.1 4.0 %copy-start.10 = (s32[4]{0:T(128)S(1)}, s32[4]{0:T(128)}, u32[]{:S(2)}) copy-start(s32[4]{0:T(128)} %param.19) | copy-start | bytes 52
  43.1 15.9 %all-to-all-start.2 = ((bf16[32,8,1024]{2,1,0:T(8,128)(2,1)}), bf16[32,8,1024]{2,1,0:T(8,128)(2,1)S(1)}, u32[]{:S(2)}, u32[]{:S(2)}) async-start(bf16[32,8,1024]{2,1,0:T(8,128)(2,1)} %shard_map.122), calls=%async_computation.2 | async-start | bytes 1048576 | tf_op jit(solution)/shard_map/all_to_all | solution.py:302
  48.2 4.8 %collective-permute-start.3 = (bf16[8,256]{1,0:T(8,128)(2,1)S(1)}, bf16[8,256]{1,0:T(8,128)(2,1)S(1)}, u32[]{:S(2)}, u32[]{:S(2)}) collective-permute-start(bf16[8,256]{1,0:T(8,128)(2,1)S(1)} %convolution_convert_fusion.2), channel_id=1, source_target_pairs={{0,8},{8,16},{16,24},{24,0},{1,9},{9,17},{17,25},{25,1},{2,10},{10... | collective-permute-start | bytes 12296 | tf_op jit(solution)/shard_map/ppermute | solution.py:176
  49.4 4.3 %collective-permute-start.4 = (bf16[8,256]{1,0:T(8,128)(2,1)S(1)}, bf16[8,256]{1,0:T(8,128)(2,1)S(1)}, u32[]{:S(2)}, u32[]{:S(2)}) collective-permute-start(bf16[8,256]{1,0:T(8,128)(2,1)S(1)} %convolution_convert_fusion.2), channel_id=1, source_target_pairs={{0,16},{8,24},{16,0},{24,8},{1,17},{9,25},{17,1},{25,9},{2,18},{10... | collective-permute-start | bytes 12296 | tf_op jit(solution)/shard_map/ppermute | solution.py:176
  51.9 2.8 %collective-permute-start.5 = (bf16[8,256]{1,0:T(8,128)(2,1)S(1)}, bf16[8,256]{1,0:T(8,128)(2,1)S(1)}, u32[]{:S(2)}, u32[]{:S(2)}) collective-permute-start(bf16[8,256]{1,0:T(8,128)(2,1)S(1)} %convolution_convert_fusion.2), channel_id=1, source_target_pairs={{0,24},{8,0},{16,8},{24,16},{1,25},{9,1},{17,9},{25,17},{2,26},{10... | collective-permute-start | bytes 12296 | tf_op jit(solution)/shard_map/ppermute | solution.py:176
  60.0 16.7 %all-to-all-start.3 = ((f32[8,32,256]{2,1,0:T(8,128)}), f32[8,32,256]{2,1,0:T(8,128)S(1)}, u32[]{:S(2)}, u32[]{:S(2)}) async-start(f32[8,32,256]{2,1,0:T(8,128)} %fusion.9), calls=%async_computation.3 | async-start | bytes 524288 | tf_op jit(solution)/shard_map/all_to_all | solution.py:307

commit v12 on v9

--- a/solution.py
+++ b/solution.py
@@ -221,8 +221,10 @@
         path_pick, group_rows[:, width_q:], preferred_element_type=jnp.float32
     ).astype(jnp.bfloat16)
     lanes = cache_pair.shape[0]
-    ahead = jnp.roll(cache_pair, -my_x, axis=0)
-    blocks_kv = [ahead[0]] + [shifted(ahead[k], "bx", k) for k in range(1, lanes)]
+    blocks_kv = [lax.dynamic_index_in_dim(cache_pair, my_x, 0, False)] + [
+        shifted(lax.dynamic_index_in_dim(cache_pair, (my_x + k) % lanes, 0, False), "bx", k)
+        for k in range(1, lanes)
+    ]
     path_rel = jnp.stack(
         [path_rows] + [shifted(path_rows, "bx", k) for k in range(1, lanes)], axis=0
     )

time: 78 us -> 78.8 us (1.010)
  local copies, waits for them, and re-layouts: 6.52 us -> 7.43 us
    unnamed x20 -> x21, local copies, waits for them, and re-layouts: 1.34 us -> 2.21 us
where the time goes in v12:
time: 78.8 us; the launch traced here: 77.7 us
  starting transfers between devices  39.8 us (51%)
  waiting for transfers between devices  16.9 us (21%)
  local copies, waits for them, and re-layouts  7.43 us (9%)
  matrix products  6.55 us (8%)
  other arithmetic  3.57 us (5%)
  Pallas kernels  2.58 us (3%)
  between operations  0.86 us (1%)
    all_to_all x2, starting transfers between devices, gather_rows(): lax.all_to_all(spread, axis_name, split_axis=0, concat_axis=0, tiled=True)  13.2 us
    all_to_all x1, starting transfers between devices, on_device(): lax.all_to_all(partial.reshape(kv_count, out_rows, partial.shape[1]), 'kv...  10.3 us
    ppermute x6, starting transfers between devices, shifted(): lax.ppermute(block, axis_name, [(i, (i + shift) % count) for i in range(c...  9.61 us
    all_to_all x1, waiting for transfers between devices, on_device(): lax.all_to_all(packed_out.reshape(ring, rows_dev, -1), 'bz', split_axis=0...  6.82 us
    all_to_all x1, starting transfers between devices, on_device(): lax.all_to_all(packed_out.reshape(ring, rows_dev, -1), 'bz', split_axis=0...  6.77 us
    all_to_all x1, waiting for transfers between devices, on_device(): lax.all_to_all(partial.reshape(kv_count, out_rows, partial.shape[1]), 'kv...  5.54 us
    all_to_all x2, waiting for transfers between devices, gather_rows(): lax.all_to_all(spread, axis_name, split_axis=0, concat_axis=0, tiled=True)  2.9 us
    pallas_call x1, Pallas kernels, block_attention(): pl.pallas_call(functools.partial(block_attention_kernel, block_len), out_...  2.58 us
  transfers between devices with their start and end apart: 10, of which 5 were waited for; matrix products, arithmetic and copies ran while one was open for 13% of the time, Pallas kernels for 0%

profile of v12, /device:TPU:1, one launch (start us, length us, event | category | flops | bytes accessed | tf_op | source)
XLA Modules:
  0.0 77.7 jit_solution(3559575802730604706)
XLA Ops:
  0.6 0.8 %pad_maximum_fusion = bf16[8,1280]{1,0:T(8,128)(2,1)S(1)} fusion(bf16[8,128]{1,0:T(8,128)(2,1)} %param.12, bf16[8,128]{1,0:T(8,128)(2,1)} %param.11, bf16[8,1024]{1,0:T(8,128)(2,1)} %param.10), kind=kLoop, calls=%fused_computation.49 | loop fusion | flops 61440 | bytes 40960 | tf_op jit(solution)/shard_map/concatenate | solution.py:215
  1.5 0.7 broadcast_in_dim.30
  2.1 9.1 %all-to-all-start = ((bf16[8,8,1280]{2,1,0:T(8,128)(2,1)}), bf16[8,8,1280]{2,1,0:T(8,128)(2,1)S(1)}, u32[]{:S(2)}, u32[]{:S(2)}) async-start(bf16[8,8,1280]{2,1,0:T(8,128)(2,1)} %broadcast_in_dim.30), calls=%async_computation | async-start | bytes 327680 | tf_op jit(solution)/shard_map/all_to_all | solution.py:182
  11.3 0.8 %copy-done.3 = bf16[4,128,128]{2,1,0:T(8,128)(2,1)S(1)} copy-done((bf16[4,128,128]{2,1,0:T(8,128)(2,1)S(1)}, bf16[4,128,128]{2,1,0:T(8,128)(2,1)}, u32[]{:S(2)}) %copy-start.3) | copy-done | bytes 131096
  12.2 0.7 dynamic-slice_bitcast_fusion
  12.9 1.2 %collective-permute-start = (bf16[128,256]{1,0:T(8,128)(2,1)S(1)}, bf16[128,256]{1,0:T(8,128)(2,1)S(1)}, u32[]{:S(2)}, u32[]{:S(2)}) collective-permute-start(bf16[128,256]{1,0:T(8,128)(2,1)S(1)} %get-tuple-element.9), channel_id=1, source_target_pairs={{0,8},{8,16},{16,24},{24,0},{1,9},{9,17},{17,25},{25,1},{2,10},{10... | collective-permute-start | bytes 196616 | tf_op jit(solution)/shard_map/ppermute | solution.py:176
  14.1 2.5 %collective-permute-start.1 = (bf16[128,256]{1,0:T(8,128)(2,1)S(1)}, bf16[128,256]{1,0:T(8,128)(2,1)S(1)}, u32[]{:S(2)}, u32[]{:S(2)}) collective-permute-start(bf16[128,256]{1,0:T(8,128)(2,1)S(1)} %get-tuple-element.8), channel_id=1, source_target_pairs={{0,16},{8,24},{16,0},{24,8},{1,17},{9,25},{17,1},{25,9},{2,18},{10... | collective-permute-start | bytes 196616 | tf_op jit(solution)/shard_map/ppermute | solution.py:176
  16.5 1.2 %collective-permute-start.2 = (bf16[128,256]{1,0:T(8,128)(2,1)S(1)}, bf16[128,256]{1,0:T(8,128)(2,1)S(1)}, u32[]{:S(2)}, u32[]{:S(2)}) collective-permute-start(bf16[128,256]{1,0:T(8,128)(2,1)S(1)} %get-tuple-element.7), channel_id=1, source_target_pairs={{0,24},{8,0},{16,8},{24,16},{1,25},{9,1},{17,9},{25,17},{2,26},{10... | collective-permute-start | bytes 196616 | tf_op jit(solution)/shard_map/ppermute | solution.py:176
  17.7 0.7 fusion.47
  19.6 0.6 copy-done.8
  20.9 1.2 %fusion.45.limit_ref = s32[4]{0:T(128)} fusion(s32[]{:T(128)S(6)} %axis_index.33, s32[]{:T(128)S(6)} %axis_index.15, s32[]{:T(128)} %bitcast), kind=kLoop, calls=%fused_computation.95 | loop fusion | flops 64 | bytes 28 | tf_op jit(solution)/shard_map/sub | solution.py:243
  22.2 0.7 fusion.48
  23.6 2.6 %shard_map.121 = bf16[64,1072]{1,0:T(8,128)(2,1)} custom-call(s32[4]{0:T(128)} %fusion.45.limit_ref, bf16[64,1280]{1,0:T(8,128)(2,1)} %bitcast.97, bf16[128,256]{1,0:T(8,128)(2,1)} %get-tuple-element.10.refs_0_, bf16[128,256]{1,0:T(8,128)(2,1)} %copy-done.5, bf16[128,256]{1,0:T(8,128)(2,1)} %copy-done.6, bf16[128,256]{1,0:T(8,128)(2,1)} %copy-done.7), custom_call_target="tpu_custom_call" | custom-call | flops 134217728 | bytes 530432 | tf_op jit(solution)/shard_map/pallas_call | solution.py:160
  26.1 6.8 %all-to-all-start.1 = ((bf16[8,8,1072]{2,1,0:T(8,128)(2,1)}), bf16[8,8,1072]{2,1,0:T(8,128)(2,1)S(1)}, u32[]{:S(2)}, u32[]{:S(2)}) async-start(bf16[8,8,1072]{2,1,0:T(8,128)(2,1)} %bitcast.101), calls=%async_computation.1 | async-start | bytes 294912 | tf_op jit(solution)/shard_map/all_to_all | solution.py:247
  32.9 0.9 %fusion.50 = (f32[8,8]{0,1:T(8,128)S(1)}, f32[1,1,1,8,8,64]{5,3,4,0,2,1:T(8,128)S(1)}) fusion(bf16[8,8,128]{2,0,1:T(8,128)(2,1)S(1)} %bitcast.102, bf16[64,1280]{1,0:T(8,128)(2,1)} %bitcast.98, pred[8,64]{1,0:T(8,128)(4,1)S(1)} %fusion.36), kind=kOutput, calls=%fused_computation.101 | convolution fusion | flops 1060800 | bytes 49920 | tf_op jit(solution)/shard_map/rtkgh,rbpkh->brkgtp/dot_general | solution.py:36
  34.3 6.8 %all-to-all-done.1 = bf16[8,8,1072]{2,1,0:T(8,128)(2,1)S(1)} async-done(((bf16[8,8,1072]{2,1,0:T(8,128)(2,1)}), bf16[8,8,1072]{2,1,0:T(8,128)(2,1)S(1)}, u32[]{:S(2)}, u32[]{:S(2)}) %all-to-all-start.1) | async-done | bytes 137248 | tf_op jit(solution)/shard_map/all_to_all | solution.py:247
  41.7 0.8 %fusion.11 = bf16[8,1024]{1,0:T(8,128)(2,1)S(1)} fusion(f32[8,1024]{1,0:T(8,128)S(1)} %fusion.15, bf16[64,1280]{1,0:T(8,128)(2,1)} %bitcast.99, bf16[8,8,64]{2,0,1:T(8,128)(2,1)S(1)} %get-tuple-element.12, f32[8,8]{0,1:T(8,128)S(1)} %copy.29, f32[8,8]{0,1:T(8,128)S(1)} %copy.25), kind=kOutput, calls=%fused_computation.21 | convolution fusion | flops 1081344 | bytes 74240 | tf_op jit(solution)/shard_map/brkgtp,rbpkh->brtkgh/dot_general | solution.py:45
  42.5 0.9 %broadcast_in_dim.34 = bf16[32,8,1024]{2,1,0:T(8,128)(2,1)} broadcast(bf16[8,1024]{1,0:T(8,128)(2,1)S(1)} %fusion.11), dimensions={1,2} | broadcast | bytes 540672 | tf_op jit(solution)/shard_map/broadcast_in_dim | solution.py:181
  43.4 4.0 %all-to-all-start.2 = ((bf16[32,8,1024]{2,1,0:T(8,128)(2,1)}), bf16[32,8,1024]{2,1,0:T(8,128)(2,1)S(1)}, u32[]{:S(2)}, u32[]{:S(2)}) async-start(bf16[32,8,1024]{2,1,0:T(8,128)(2,1)} %broadcast_in_dim.34), calls=%async_computation.2 | async-start | bytes 1048576 | tf_op jit(solution)/shard_map/all_to_all | solution.py:182
  47.5 0.9 %convolution_convert_fusion.2 = bf16[8,256]{1,0:T(8,128)(2,1)S(1)} fusion(bf16[64,1280]{1,0:T(8,128)(2,1)} %bitcast.100, s32[8]{0:T(128)S(1)} %fusion.48), kind=kOutput, calls=%fused_computation.23 | convolution fusion | flops 264704 | bytes 36896 | tf_op jit(solution)/shard_map/dot_general | solution.py:220
  48.4 1.2 %collective-permute-start.3 = (bf16[8,256]{1,0:T(8,128)(2,1)S(1)}, bf16[8,256]{1,0:T(8,128)(2,1)S(1)}, u32[]{:S(2)}, u32[]{:S(2)}) collective-permute-start(bf16[8,256]{1,0:T(8,128)(2,1)S(1)} %convolution_convert_fusion.2), channel_id=1, source_target_pairs={{0,8},{8,16},{16,24},{24,0},{1,9},{9,17},{17,25},{25,1},{2,10},{10... | collective-permute-start | bytes 12296 | tf_op jit(solution)/shard_map/ppermute | solution.py:176
  49.6 2.5 %collective-permute-start.4 = (bf16[8,256]{1,0:T(8,128)(2,1)S(1)}, bf16[8,256]{1,0:T(8,128)(2,1)S(1)}, u32[]{:S(2)}, u32[]{:S(2)}) collective-permute-start(bf16[8,256]{1,0:T(8,128)(2,1)S(1)} %convolution_convert_fusion.2), channel_id=1, source_target_pairs={{0,16},{8,24},{16,0},{24,8},{1,17},{9,25},{17,1},{25,9},{2,18},{10... | collective-permute-start | bytes 12296 | tf_op jit(solution)/shard_map/ppermute | solution.py:176
  52.1 1.1 %collective-permute-start.5 = (bf16[8,256]{1,0:T(8,128)(2,1)S(1)}, bf16[8,256]{1,0:T(8,128)(2,1)S(1)}, u32[]{:S(2)}, u32[]{:S(2)}) collective-permute-start(bf16[8,256]{1,0:T(8,128)(2,1)S(1)} %convolution_convert_fusion.2), channel_id=1, source_target_pairs={{0,24},{8,0},{16,8},{24,16},{1,25},{9,1},{17,9},{25,17},{2,26},{10... | collective-permute-start | bytes 12296 | tf_op jit(solution)/shard_map/ppermute | solution.py:176
  53.3 0.6 collective-permute-done.4
  53.9 1.0 %collective-permute-done.5 = bf16[8,256]{1,0:T(8,128)(2,1)S(1)} collective-permute-done((bf16[8,256]{1,0:T(8,128)(2,1)S(1)}, bf16[8,256]{1,0:T(8,128)(2,1)S(1)}, u32[]{:S(2)}, u32[]{:S(2)}) %collective-permute-start.5) | collective-permute-done | bytes 4128 | tf_op jit(solution)/shard_map/ppermute | solution.py:176
  55.5 0.9 %fusion = bf16[4,128,128]{2,1,0:T(8,128)(2,1)} fusion(bf16[4,128,128]{2,1,0:T(8,128)(2,1)S(1)} %copy-done.2, pred[4,128]{1,0:T(4,128)(4,1)S(1)} %compare_and_fusion, bf16[4,8,256]{2,1,0:T(8,128)(2,1)S(1)} %fusion.23, s32[4,128]{1,0:T(4,128)S(1)} %broadcast_subtract_fusion), kind=kOutput, calls=%fused_computation.3 | convolution fusion | flops 1187840 | bytes 273408 | tf_op jit(solution)/shard_map/rps,rsc->rpc/dot_general | solution.py:92
  56.4 2.9 %all-to-all-done.2 = bf16[32,8,1024]{2,1,0:T(8,128)(2,1)S(1)} async-done(((bf16[32,8,1024]{2,1,0:T(8,128)(2,1)}), bf16[32,8,1024]{2,1,0:T(8,128)(2,1)S(1)}, u32[]{:S(2)}, u32[]{:S(2)}) %all-to-all-start.2) | async-done | bytes 524320 | tf_op jit(solution)/shard_map/all_to_all | solution.py:182
  59.3 1.0 %fusion.13 = f32[8,32,256]{2,1,0:T(8,128)} fusion(bf16[8,32,1024]{2,1,0:T(8,128)(2,1)S(1)} %bitcast.96, bf16[1024,256]{1,0:T(8,128)(2,1)S(1)} %copy-done), kind=kOutput, calls=%fused_computation.24 | convolution fusion | flops 134217728 | bytes 1310720 | tf_op jit(solution)/shard_map/dot_general | solution.py:264
  60.3 10.3 %all-to-all-start.3 = ((f32[8,32,256]{2,1,0:T(8,128)}), f32[8,32,256]{2,1,0:T(8,128)S(1)}, u32[]{:S(2)}, u32[]{:S(2)}) async-start(f32[8,32,256]{2,1,0:T(8,128)} %fusion.13), calls=%async_computation.3 | async-start | bytes 524288 | tf_op jit(solution)/shard_map/all_to_all | solution.py:266
  70.6 0.9 %fusion.1 = bf16[4,128,128]{2,1,0:T(8,128)(2,1)} fusion(bf16[4,128,128]{2,1,0:T(8,128)(2,1)S(1)} %copy-done.3, pred[4,128]{1,0:T(4,128)(4,1)S(1)} %compare_and_fusion, bf16[4,8,256]{2,1,0:T(8,128)(2,1)S(1)} %fusion.23, s32[4,128]{1,0:T(4,128)S(1)} %broadcast_subtract_fusion), kind=kOutput, calls=%fused_computation.4 | convolution fusion | flops 1187840 | bytes 273408 | tf_op jit(solution)/shard_map/rps,rsc->rpc/dot_general | solution.py:92
  71.5 5.5 %all-to-all-done.3 = f32[8,32,256]{2,1,0:T(8,128)S(1)} async-done(((f32[8,32,256]{2,1,0:T(8,128)}), f32[8,32,256]{2,1,0:T(8,128)S(1)}, u32[]{:S(2)}, u32[]{:S(2)}) %all-to-all-start.3) | async-done | bytes 262176 | tf_op jit(solution)/shard_map/all_to_all | solution.py:266
  77.0 0.6 reduce_sum.42
  (57 shorter events, 4.3 us)
Async XLA Ops:
  0.6 58.7 %copy-start = (bf16[1024,256]{1,0:T(8,128)(2,1)S(1)}, bf16[1024,256]{1,0:T(8,128)(2,1)}, u32[]{:S(2)}) copy-start(bf16[1024,256]{1,0:T(8,128)(2,1)} %param.15) | copy-start | bytes 1572868
  2.1 9.1 %copy-start.2 = (bf16[4,128,128]{2,1,0:T(8,128)(2,1)S(1)}, bf16[4,128,128]{2,1,0:T(8,128)(2,1)}, u32[]{:S(2)}) copy-start(bf16[4,128,128]{2,1,0:T(8,128)(2,1)} %param.13) | copy-start | bytes 393220
  2.1 20.8 %all-to-all-start = ((bf16[8,8,1280]{2,1,0:T(8,128)(2,1)}), bf16[8,8,1280]{2,1,0:T(8,128)(2,1)S(1)}, u32[]{:S(2)}, u32[]{:S(2)}) async-start(bf16[8,8,1280]{2,1,0:T(8,128)(2,1)} %broadcast_in_dim.30), calls=%async_computation | async-start | bytes 327680 | tf_op jit(solution)/shard_map/all_to_all | solution.py:182
  11.3 0.9 %copy-start.3 = (bf16[4,128,128]{2,1,0:T(8,128)(2,1)S(1)}, bf16[4,128,128]{2,1,0:T(8,128)(2,1)}, u32[]{:S(2)}) copy-start(bf16[4,128,128]{2,1,0:T(8,128)(2,1)} %param.14) | copy-start | bytes 393220
  12.9 10.0 %collective-permute-start = (bf16[128,256]{1,0:T(8,128)(2,1)S(1)}, bf16[128,256]{1,0:T(8,128)(2,1)S(1)}, u32[]{:S(2)}, u32[]{:S(2)}) collective-permute-start(bf16[128,256]{1,0:T(8,128)(2,1)S(1)} %get-tuple-element.9), channel_id=1, source_target_pairs={{0,8},{8,16},{16,24},{24,0},{1,9},{9,17},{17,25},{25,1},{2,10},{10... | collective-permute-start | bytes 196616 | tf_op jit(solution)/shard_map/ppermute | solution.py:176
  14.1 8.8 %collective-permute-start.1 = (bf16[128,256]{1,0:T(8,128)(2,1)S(1)}, bf16[128,256]{1,0:T(8,128)(2,1)S(1)}, u32[]{:S(2)}, u32[]{:S(2)}) collective-permute-start(bf16[128,256]{1,0:T(8,128)(2,1)S(1)} %get-tuple-element.8), channel_id=1, source_target_pairs={{0,16},{8,24},{16,0},{24,8},{1,17},{9,25},{17,1},{25,9},{2,18},{10... | collective-permute-start | bytes 196616 | tf_op jit(solution)/shard_map/ppermute | solution.py:176
  16.5 6.3 %collective-permute-start.2 = (bf16[128,256]{1,0:T(8,128)(2,1)S(1)}, bf16[128,256]{1,0:T(8,128)(2,1)S(1)}, u32[]{:S(2)}, u32[]{:S(2)}) collective-permute-start(bf16[128,256]{1,0:T(8,128)(2,1)S(1)} %get-tuple-element.7), channel_id=1, source_target_pairs={{0,24},{8,0},{16,8},{24,16},{1,25},{9,1},{17,9},{25,17},{2,26},{10... | collective-permute-start | bytes 196616 | tf_op jit(solution)/shard_map/ppermute | solution.py:176
  19.6 0.7 copy-start.8
  22.8 0.6 copy-start.5
  22.9 0.6 copy-start.6
  22.9 0.6 copy-start.7
  22.9 0.7 copy-start.1
  26.1 6.8 %copy-start.4 = (bf16[8,1024]{1,0:T(8,128)(2,1)S(1)}, bf16[8,1024]{1,0:T(8,128)(2,1)}, u32[]{:S(2)}) copy-start(bf16[8,1024]{1,0:T(8,128)(2,1)} %param.10) | copy-start | bytes 49156
  26.1 15.0 %all-to-all-start.1 = ((bf16[8,8,1072]{2,1,0:T(8,128)(2,1)}), bf16[8,8,1072]{2,1,0:T(8,128)(2,1)S(1)}, u32[]{:S(2)}, u32[]{:S(2)}) async-start(bf16[8,8,1072]{2,1,0:T(8,128)(2,1)} %bitcast.101), calls=%async_computation.1 | async-start | bytes 294912 | tf_op jit(solution)/shard_map/all_to_all | solution.py:247
  43.4 4.0 %copy-start.9 = (s32[4]{0:T(128)S(1)}, s32[4]{0:T(128)}, u32[]{:S(2)}) copy-start(s32[4]{0:T(128)} %param.19) | copy-start | bytes 52
  43.4 15.9 %all-to-all-start.2 = ((bf16[32,8,1024]{2,1,0:T(8,128)(2,1)}), bf16[32,8,1024]{2,1,0:T(8,128)(2,1)S(1)}, u32[]{:S(2)}, u32[]{:S(2)}) async-start(bf16[32,8,1024]{2,1,0:T(8,128)(2,1)} %broadcast_in_dim.34), calls=%async_computation.2 | async-start | bytes 1048576 | tf_op jit(solution)/shard_map/all_to_all | solution.py:182
  48.4 4.8 %collective-permute-start.3 = (bf16[8,256]{1,0:T(8,128)(2,1)S(1)}, bf16[8,256]{1,0:T(8,128)(2,1)S(1)}, u32[]{:S(2)}, u32[]{:S(2)}) collective-permute-start(bf16[8,256]{1,0:T(8,128)(2,1)S(1)} %convolution_convert_fusion.2), channel_id=1, source_target_pairs={{0,8},{8,16},{16,24},{24,0},{1,9},{9,17},{17,25},{25,1},{2,10},{10... | collective-permute-start | bytes 12296 | tf_op jit(solution)/shard_map/ppermute | solution.py:176
  49.6 4.3 %collective-permute-start.4 = (bf16[8,256]{1,0:T(8,128)(2,1)S(1)}, bf16[8,256]{1,0:T(8,128)(2,1)S(1)}, u32[]{:S(2)}, u32[]{:S(2)}) collective-permute-start(bf16[8,256]{1,0:T(8,128)(2,1)S(1)} %convolution_convert_fusion.2), channel_id=1, source_target_pairs={{0,16},{8,24},{16,0},{24,8},{1,17},{9,25},{17,1},{25,9},{2,18},{10... | collective-permute-start | bytes 12296 | tf_op jit(solution)/shard_map/ppermute | solution.py:176
  52.1 2.8 %collective-permute-start.5 = (bf16[8,256]{1,0:T(8,128)(2,1)S(1)}, bf16[8,256]{1,0:T(8,128)(2,1)S(1)}, u32[]{:S(2)}, u32[]{:S(2)}) collective-permute-start(bf16[8,256]{1,0:T(8,128)(2,1)S(1)} %convolution_convert_fusion.2), channel_id=1, source_target_pairs={{0,24},{8,0},{16,8},{24,16},{1,25},{9,1},{17,9},{25,17},{2,26},{10... | collective-permute-start | bytes 12296 | tf_op jit(solution)/shard_map/ppermute | solution.py:176
  60.3 16.7 %all-to-all-start.3 = ((f32[8,32,256]{2,1,0:T(8,128)}), f32[8,32,256]{2,1,0:T(8,128)S(1)}, u32[]{:S(2)}, u32[]{:S(2)}) async-start(f32[8,32,256]{2,1,0:T(8,128)} %fusion.13), calls=%async_computation.3 | async-start | bytes 524288 | tf_op jit(solution)/shard_map/all_to_all | solution.py:266

commit v13 on v9

--- a/solution.py
+++ b/solution.py
@@ -10,7 +10,6 @@
 
 HEAD_SIZE = 128
 TREE_TOKENS = 64
-ACC = 8
 
 
 NEG_FLOOR = -1e30
@@ -22,7 +21,7 @@
         (parent_rows[:, :, None] == node_ids[None, None, :]) & (node_ids[None, :, None] >= 1)
     ).astype(jnp.float32)
     reachable = jnp.eye(TREE_TOKENS, dtype=jnp.float32)[None] + parent_link
-    for doubling in range((TREE_TOKENS - 1).bit_length()):
+    for _ in range((TREE_TOKENS - 1).bit_length()):
         reachable = jnp.minimum(
             reachable
             + jnp.einsum("rij,rjk->rik", reachable, reachable, precision=lax.Precision.HIGHEST),
@@ -183,7 +182,7 @@
     return moved.reshape((count * block.shape[0],) + block.shape[1:])
 
 
-def on_device(
+def on_device_body(
     queries,
     draft_token_keys,
     draft_token_values,
@@ -202,7 +201,6 @@
     my_x = lax.axis_index("bx")
     my_z = lax.axis_index("bz")
     rows_dev, width_q = queries.shape
-    requests = lengths.shape[0]
     cache_width = cached_key_vectors.shape[2]
     kv_local = cache_width // HEAD_SIZE
     query_group_width = width_q // (kv_local * HEAD_SIZE)
@@ -287,7 +285,7 @@
     grid_mesh = Mesh(mesh.devices.reshape(kv_size, requests, ring), ("kv", "bx", "bz"))
     blk = ("bx", "bz")
     return jax.shard_map(
-        on_device,
+        on_device_body,
         mesh=grid_mesh,
         in_specs=(
             P(blk, "kv"),

time: 78 us -> 78 us (level)
  no operation moved by 1% of the time
where the time goes in v13:
time: 78 us; the launch traced here: 76.9 us
  starting transfers between devices  39.8 us (51%)
  waiting for transfers between devices  16.9 us (22%)
  matrix products  6.55 us (8%)
  local copies, waits for them, and re-layouts  6.52 us (8%)
  other arithmetic  3.72 us (5%)
  Pallas kernels  2.58 us (3%)
  between operations  0.84 us (1%)
    all_to_all x2, starting transfers between devices, gather_rows(): lax.all_to_all(spread, axis_name, split_axis=0, concat_axis=0, tiled=True)  13.2 us
    all_to_all x1, starting transfers between devices, on_device_body(): lax.all_to_all(partial.reshape(kv_count, out_rows, partial.shape[1]), 'kv...  10.2 us
    ppermute x6, starting transfers between devices, shifted(): lax.ppermute(block, axis_name, [(i, (i + shift) % count) for i in range(c...  9.61 us
    all_to_all x1, waiting for transfers between devices, on_device_body(): lax.all_to_all(packed_out.reshape(ring, rows_dev, -1), 'bz', split_axis=0...  6.82 us
    all_to_all x1, starting transfers between devices, on_device_body(): lax.all_to_all(packed_out.reshape(ring, rows_dev, -1), 'bz', split_axis=0...  6.77 us
    all_to_all x1, waiting for transfers between devices, on_device_body(): lax.all_to_all(partial.reshape(kv_count, out_rows, partial.shape[1]), 'kv...  5.54 us
    all_to_all x2, waiting for transfers between devices, gather_rows(): lax.all_to_all(spread, axis_name, split_axis=0, concat_axis=0, tiled=True)  2.9 us
    pallas_call x1, Pallas kernels, block_attention(): pl.pallas_call(functools.partial(block_attention_kernel, block_len), out_...  2.58 us
  transfers between devices with their start and end apart: 10, of which 5 were waited for; matrix products, arithmetic and copies ran while one was open for 13% of the time, Pallas kernels for 0%

profile of v13, /device:TPU:1, one launch (start us, length us, event | category | flops | bytes accessed | tf_op | source)
XLA Modules:
  0.0 76.9 jit_solution(7307027110528553978)
XLA Ops:
  0.6 0.8 %pad_maximum_fusion = bf16[8,1280]{1,0:T(8,128)(2,1)S(1)} fusion(bf16[8,128]{1,0:T(8,128)(2,1)} %param.12, bf16[8,128]{1,0:T(8,128)(2,1)} %param.11, bf16[8,1024]{1,0:T(8,128)(2,1)} %param.10), kind=kLoop, calls=%fused_computation.56 | loop fusion | flops 61440 | bytes 40960 | tf_op jit(solution)/shard_map/concatenate | solution.py:213
  1.5 0.7 broadcast_in_dim.30
  2.1 9.1 %all-to-all-start = ((bf16[8,8,1280]{2,1,0:T(8,128)(2,1)}), bf16[8,8,1280]{2,1,0:T(8,128)(2,1)S(1)}, u32[]{:S(2)}, u32[]{:S(2)}) async-start(bf16[8,8,1280]{2,1,0:T(8,128)(2,1)} %broadcast_in_dim.30), calls=%async_computation | async-start | bytes 327680 | tf_op jit(solution)/shard_map/all_to_all | solution.py:181
  11.4 0.6 slice_bitcast_fusion
  12.1 1.2 %collective-permute-start = (bf16[128,256]{1,0:T(8,128)(2,1)S(1)}, bf16[128,256]{1,0:T(8,128)(2,1)S(1)}, u32[]{:S(2)}, u32[]{:S(2)}) collective-permute-start(bf16[128,256]{1,0:T(8,128)(2,1)S(1)} %get-tuple-element.9), channel_id=1, source_target_pairs={{0,8},{8,16},{16,24},{24,0},{1,9},{9,17},{17,25},{25,1},{2,10},{10... | collective-permute-start | bytes 196616 | tf_op jit(solution)/shard_map/ppermute | solution.py:175
  13.3 2.5 %collective-permute-start.1 = (bf16[128,256]{1,0:T(8,128)(2,1)S(1)}, bf16[128,256]{1,0:T(8,128)(2,1)S(1)}, u32[]{:S(2)}, u32[]{:S(2)}) collective-permute-start(bf16[128,256]{1,0:T(8,128)(2,1)S(1)} %get-tuple-element.8), channel_id=1, source_target_pairs={{0,16},{8,24},{16,0},{24,8},{1,17},{9,25},{17,1},{25,9},{2,18},{10... | collective-permute-start | bytes 196616 | tf_op jit(solution)/shard_map/ppermute | solution.py:175
  15.8 1.2 %collective-permute-start.2 = (bf16[128,256]{1,0:T(8,128)(2,1)S(1)}, bf16[128,256]{1,0:T(8,128)(2,1)S(1)}, u32[]{:S(2)}, u32[]{:S(2)}) collective-permute-start(bf16[128,256]{1,0:T(8,128)(2,1)S(1)} %get-tuple-element.7), channel_id=1, source_target_pairs={{0,24},{8,0},{16,8},{24,16},{1,25},{9,1},{17,9},{25,17},{2,26},{10... | collective-permute-start | bytes 196616 | tf_op jit(solution)/shard_map/ppermute | solution.py:175
  16.9 0.7 fusion.50
  18.9 0.6 copy-done.8
  19.5 0.6 dynamic_slice.18
  20.1 1.2 %fusion.48.limit_ref = s32[4]{0:T(128)} fusion(s32[]{:T(128)S(6)} %axis_index.33, s32[]{:T(128)S(6)} %axis_index.15, s32[]{:T(128)} %bitcast), kind=kLoop, calls=%fused_computation.100 | loop fusion | flops 64 | bytes 28 | tf_op jit(solution)/shard_map/sub | solution.py:239
  21.4 0.7 fusion.51
  22.8 2.6 %shard_map.121 = bf16[64,1072]{1,0:T(8,128)(2,1)} custom-call(s32[4]{0:T(128)} %fusion.48.limit_ref, bf16[64,1280]{1,0:T(8,128)(2,1)} %bitcast.97, bf16[128,256]{1,0:T(8,128)(2,1)} %get-tuple-element.10.refs_0_, bf16[128,256]{1,0:T(8,128)(2,1)} %copy-done.5, bf16[128,256]{1,0:T(8,128)(2,1)} %copy-done.6, bf16[128,256]{1,0:T(8,128)(2,1)} %copy-done.7), custom_call_target="tpu_custom_call" | custom-call | flops 134217728 | bytes 530432 | tf_op jit(solution)/shard_map/pallas_call | solution.py:159
  25.4 6.8 %all-to-all-start.1 = ((bf16[8,8,1072]{2,1,0:T(8,128)(2,1)}), bf16[8,8,1072]{2,1,0:T(8,128)(2,1)S(1)}, u32[]{:S(2)}, u32[]{:S(2)}) async-start(bf16[8,8,1072]{2,1,0:T(8,128)(2,1)} %bitcast.101), calls=%async_computation.1 | async-start | bytes 294912 | tf_op jit(solution)/shard_map/all_to_all | solution.py:243
  32.1 0.9 %fusion.53 = (f32[8,8]{0,1:T(8,128)S(1)}, f32[1,1,1,8,8,64]{5,3,4,0,2,1:T(8,128)S(1)}) fusion(bf16[8,8,128]{2,0,1:T(8,128)(2,1)S(1)} %bitcast.102, bf16[64,1280]{1,0:T(8,128)(2,1)} %bitcast.98, pred[8,64]{1,0:T(8,128)(4,1)S(1)} %fusion.39), kind=kOutput, calls=%fused_computation.106 | convolution fusion | flops 1060800 | bytes 49920 | tf_op jit(solution)/shard_map/rtkgh,rbpkh->brkgtp/dot_general | solution.py:35
  33.5 6.8 %all-to-all-done.1 = bf16[8,8,1072]{2,1,0:T(8,128)(2,1)S(1)} async-done(((bf16[8,8,1072]{2,1,0:T(8,128)(2,1)}), bf16[8,8,1072]{2,1,0:T(8,128)(2,1)S(1)}, u32[]{:S(2)}, u32[]{:S(2)}) %all-to-all-start.1) | async-done | bytes 137248 | tf_op jit(solution)/shard_map/all_to_all | solution.py:243
  40.9 0.8 %fusion.11 = bf16[8,1024]{1,0:T(8,128)(2,1)S(1)} fusion(f32[8,1024]{1,0:T(8,128)S(1)} %fusion.18, bf16[64,1280]{1,0:T(8,128)(2,1)} %bitcast.99, bf16[8,8,64]{2,0,1:T(8,128)(2,1)S(1)} %get-tuple-element.12, f32[8,8]{0,1:T(8,128)S(1)} %copy.29, f32[8,8]{0,1:T(8,128)S(1)} %copy.25), kind=kOutput, calls=%fused_computation.21 | convolution fusion | flops 1081344 | bytes 74240 | tf_op jit(solution)/shard_map/brkgtp,rbpkh->brtkgh/dot_general | solution.py:44
  41.7 0.9 %broadcast_in_dim.34 = bf16[32,8,1024]{2,1,0:T(8,128)(2,1)} broadcast(bf16[8,1024]{1,0:T(8,128)(2,1)S(1)} %fusion.11), dimensions={1,2} | broadcast | bytes 540672 | tf_op jit(solution)/shard_map/broadcast_in_dim | solution.py:180
  42.6 4.0 %all-to-all-start.2 = ((bf16[32,8,1024]{2,1,0:T(8,128)(2,1)}), bf16[32,8,1024]{2,1,0:T(8,128)(2,1)S(1)}, u32[]{:S(2)}, u32[]{:S(2)}) async-start(bf16[32,8,1024]{2,1,0:T(8,128)(2,1)} %broadcast_in_dim.34), calls=%async_computation.2 | async-start | bytes 1048576 | tf_op jit(solution)/shard_map/all_to_all | solution.py:181
  46.7 0.9 %convolution_convert_fusion.2 = bf16[8,256]{1,0:T(8,128)(2,1)S(1)} fusion(bf16[64,1280]{1,0:T(8,128)(2,1)} %bitcast.100, s32[8]{0:T(128)S(1)} %fusion.51), kind=kOutput, calls=%fused_computation.23 | convolution fusion | flops 264704 | bytes 36896 | tf_op jit(solution)/shard_map/dot_general | solution.py:218
  47.7 1.2 %collective-permute-start.3 = (bf16[8,256]{1,0:T(8,128)(2,1)S(1)}, bf16[8,256]{1,0:T(8,128)(2,1)S(1)}, u32[]{:S(2)}, u32[]{:S(2)}) collective-permute-start(bf16[8,256]{1,0:T(8,128)(2,1)S(1)} %convolution_convert_fusion.2), channel_id=1, source_target_pairs={{0,8},{8,16},{16,24},{24,0},{1,9},{9,17},{17,25},{25,1},{2,10},{10... | collective-permute-start | bytes 12296 | tf_op jit(solution)/shard_map/ppermute | solution.py:175
  48.8 2.5 %collective-permute-start.4 = (bf16[8,256]{1,0:T(8,128)(2,1)S(1)}, bf16[8,256]{1,0:T(8,128)(2,1)S(1)}, u32[]{:S(2)}, u32[]{:S(2)}) collective-permute-start(bf16[8,256]{1,0:T(8,128)(2,1)S(1)} %convolution_convert_fusion.2), channel_id=1, source_target_pairs={{0,16},{8,24},{16,0},{24,8},{1,17},{9,25},{17,1},{25,9},{2,18},{10... | collective-permute-start | bytes 12296 | tf_op jit(solution)/shard_map/ppermute | solution.py:175
  51.3 1.1 %collective-permute-start.5 = (bf16[8,256]{1,0:T(8,128)(2,1)S(1)}, bf16[8,256]{1,0:T(8,128)(2,1)S(1)}, u32[]{:S(2)}, u32[]{:S(2)}) collective-permute-start(bf16[8,256]{1,0:T(8,128)(2,1)S(1)} %convolution_convert_fusion.2), channel_id=1, source_target_pairs={{0,24},{8,0},{16,8},{24,16},{1,25},{9,1},{17,9},{25,17},{2,26},{10... | collective-permute-start | bytes 12296 | tf_op jit(solution)/shard_map/ppermute | solution.py:175
  52.5 0.6 collective-permute-done.4
  53.1 1.0 %collective-permute-done.5 = bf16[8,256]{1,0:T(8,128)(2,1)S(1)} collective-permute-done((bf16[8,256]{1,0:T(8,128)(2,1)S(1)}, bf16[8,256]{1,0:T(8,128)(2,1)S(1)}, u32[]{:S(2)}, u32[]{:S(2)}) %collective-permute-start.5) | collective-permute-done | bytes 4128 | tf_op jit(solution)/shard_map/ppermute | solution.py:175
  54.7 0.9 %fusion = bf16[4,128,128]{2,1,0:T(8,128)(2,1)} fusion(bf16[4,128,128]{2,1,0:T(8,128)(2,1)S(1)} %copy-done.2, pred[4,128]{1,0:T(4,128)(4,1)S(1)} %compare_and_fusion, bf16[4,8,256]{2,1,0:T(8,128)(2,1)S(1)} %fusion.26, s32[4,128]{1,0:T(4,128)S(1)} %broadcast_subtract_fusion), kind=kOutput, calls=%fused_computation.3 | convolution fusion | flops 1187840 | bytes 273408 | tf_op jit(solution)/shard_map/rps,rsc->rpc/dot_general | solution.py:91
  55.6 2.9 %all-to-all-done.2 = bf16[32,8,1024]{2,1,0:T(8,128)(2,1)S(1)} async-done(((bf16[32,8,1024]{2,1,0:T(8,128)(2,1)}), bf16[32,8,1024]{2,1,0:T(8,128)(2,1)S(1)}, u32[]{:S(2)}, u32[]{:S(2)}) %all-to-all-start.2) | async-done | bytes 524320 | tf_op jit(solution)/shard_map/all_to_all | solution.py:181
  58.5 1.0 %fusion.13 = f32[8,32,256]{2,1,0:T(8,128)} fusion(bf16[8,32,1024]{2,1,0:T(8,128)(2,1)S(1)} %bitcast.96, bf16[1024,256]{1,0:T(8,128)(2,1)S(1)} %copy-done), kind=kOutput, calls=%fused_computation.28 | convolution fusion | flops 134217728 | bytes 1310720 | tf_op jit(solution)/shard_map/dot_general | solution.py:260
  59.5 10.2 %all-to-all-start.3 = ((f32[8,32,256]{2,1,0:T(8,128)}), f32[8,32,256]{2,1,0:T(8,128)S(1)}, u32[]{:S(2)}, u32[]{:S(2)}) async-start(f32[8,32,256]{2,1,0:T(8,128)} %fusion.13), calls=%async_computation.3 | async-start | bytes 524288 | tf_op jit(solution)/shard_map/all_to_all | solution.py:262
  69.8 0.9 %fusion.1 = bf16[4,128,128]{2,1,0:T(8,128)(2,1)} fusion(bf16[4,128,128]{2,1,0:T(8,128)(2,1)S(1)} %copy-done.3, pred[4,128]{1,0:T(4,128)(4,1)S(1)} %compare_and_fusion, bf16[4,8,256]{2,1,0:T(8,128)(2,1)S(1)} %fusion.26, s32[4,128]{1,0:T(4,128)S(1)} %broadcast_subtract_fusion), kind=kOutput, calls=%fused_computation.4 | convolution fusion | flops 1187840 | bytes 273408 | tf_op jit(solution)/shard_map/rps,rsc->rpc/dot_general | solution.py:91
  70.7 5.5 %all-to-all-done.3 = f32[8,32,256]{2,1,0:T(8,128)S(1)} async-done(((f32[8,32,256]{2,1,0:T(8,128)}), f32[8,32,256]{2,1,0:T(8,128)S(1)}, u32[]{:S(2)}, u32[]{:S(2)}) %all-to-all-start.3) | async-done | bytes 262176 | tf_op jit(solution)/shard_map/all_to_all | solution.py:262
  76.3 0.6 reduce_sum.42
  (56 shorter events, 3.8 us)
Async XLA Ops:
  0.6 57.9 %copy-start = (bf16[1024,256]{1,0:T(8,128)(2,1)S(1)}, bf16[1024,256]{1,0:T(8,128)(2,1)}, u32[]{:S(2)}) copy-start(bf16[1024,256]{1,0:T(8,128)(2,1)} %param.15) | copy-start | bytes 1572868
  2.1 9.1 %copy-start.2 = (bf16[4,128,128]{2,1,0:T(8,128)(2,1)S(1)}, bf16[4,128,128]{2,1,0:T(8,128)(2,1)}, u32[]{:S(2)}) copy-start(bf16[4,128,128]{2,1,0:T(8,128)(2,1)} %param.13) | copy-start | bytes 393220
  2.1 9.1 %copy-start.3 = (bf16[4,128,128]{2,1,0:T(8,128)(2,1)S(1)}, bf16[4,128,128]{2,1,0:T(8,128)(2,1)}, u32[]{:S(2)}) copy-start(bf16[4,128,128]{2,1,0:T(8,128)(2,1)} %param.14) | copy-start | bytes 393220
  2.1 20.0 %all-to-all-start = ((bf16[8,8,1280]{2,1,0:T(8,128)(2,1)}), bf16[8,8,1280]{2,1,0:T(8,128)(2,1)S(1)}, u32[]{:S(2)}, u32[]{:S(2)}) async-start(bf16[8,8,1280]{2,1,0:T(8,128)(2,1)} %broadcast_in_dim.30), calls=%async_computation | async-start | bytes 327680 | tf_op jit(solution)/shard_map/all_to_all | solution.py:181
  12.1 10.0 %collective-permute-start = (bf16[128,256]{1,0:T(8,128)(2,1)S(1)}, bf16[128,256]{1,0:T(8,128)(2,1)S(1)}, u32[]{:S(2)}, u32[]{:S(2)}) collective-permute-start(bf16[128,256]{1,0:T(8,128)(2,1)S(1)} %get-tuple-element.9), channel_id=1, source_target_pairs={{0,8},{8,16},{16,24},{24,0},{1,9},{9,17},{17,25},{25,1},{2,10},{10... | collective-permute-start | bytes 196616 | tf_op jit(solution)/shard_map/ppermute | solution.py:175
  13.3 8.8 %collective-permute-start.1 = (bf16[128,256]{1,0:T(8,128)(2,1)S(1)}, bf16[128,256]{1,0:T(8,128)(2,1)S(1)}, u32[]{:S(2)}, u32[]{:S(2)}) collective-permute-start(bf16[128,256]{1,0:T(8,128)(2,1)S(1)} %get-tuple-element.8), channel_id=1, source_target_pairs={{0,16},{8,24},{16,0},{24,8},{1,17},{9,25},{17,1},{25,9},{2,18},{10... | collective-permute-start | bytes 196616 | tf_op jit(solution)/shard_map/ppermute | solution.py:175
  15.8 6.3 %collective-permute-start.2 = (bf16[128,256]{1,0:T(8,128)(2,1)S(1)}, bf16[128,256]{1,0:T(8,128)(2,1)S(1)}, u32[]{:S(2)}, u32[]{:S(2)}) collective-permute-start(bf16[128,256]{1,0:T(8,128)(2,1)S(1)} %get-tuple-element.7), channel_id=1, source_target_pairs={{0,24},{8,0},{16,8},{24,16},{1,25},{9,1},{17,9},{25,17},{2,26},{10... | collective-permute-start | bytes 196616 | tf_op jit(solution)/shard_map/ppermute | solution.py:175
  18.9 0.7 copy-start.8
  22.1 0.6 copy-start.5
  22.1 0.6 copy-start.6
  22.1 0.6 copy-start.7
  22.1 0.7 copy-start.1
  25.4 6.8 %copy-start.4 = (bf16[8,1024]{1,0:T(8,128)(2,1)S(1)}, bf16[8,1024]{1,0:T(8,128)(2,1)}, u32[]{:S(2)}) copy-start(bf16[8,1024]{1,0:T(8,128)(2,1)} %param.10) | copy-start | bytes 49156
  25.4 15.0 %all-to-all-start.1 = ((bf16[8,8,1072]{2,1,0:T(8,128)(2,1)}), bf16[8,8,1072]{2,1,0:T(8,128)(2,1)S(1)}, u32[]{:S(2)}, u32[]{:S(2)}) async-start(bf16[8,8,1072]{2,1,0:T(8,128)(2,1)} %bitcast.101), calls=%async_computation.1 | async-start | bytes 294912 | tf_op jit(solution)/shard_map/all_to_all | solution.py:243
  42.6 4.0 %copy-start.9 = (s32[4]{0:T(128)S(1)}, s32[4]{0:T(128)}, u32[]{:S(2)}) copy-start(s32[4]{0:T(128)} %param.19) | copy-start | bytes 52
  42.6 15.9 %all-to-all-start.2 = ((bf16[32,8,1024]{2,1,0:T(8,128)(2,1)}), bf16[32,8,1024]{2,1,0:T(8,128)(2,1)S(1)}, u32[]{:S(2)}, u32[]{:S(2)}) async-start(bf16[32,8,1024]{2,1,0:T(8,128)(2,1)} %broadcast_in_dim.34), calls=%async_computation.2 | async-start | bytes 1048576 | tf_op jit(solution)/shard_map/all_to_all | solution.py:181
  47.7 4.8 %collective-permute-start.3 = (bf16[8,256]{1,0:T(8,128)(2,1)S(1)}, bf16[8,256]{1,0:T(8,128)(2,1)S(1)}, u32[]{:S(2)}, u32[]{:S(2)}) collective-permute-start(bf16[8,256]{1,0:T(8,128)(2,1)S(1)} %convolution_convert_fusion.2), channel_id=1, source_target_pairs={{0,8},{8,16},{16,24},{24,0},{1,9},{9,17},{17,25},{25,1},{2,10},{10... | collective-permute-start | bytes 12296 | tf_op jit(solution)/shard_map/ppermute | solution.py:175
  48.8 4.3 %collective-permute-start.4 = (bf16[8,256]{1,0:T(8,128)(2,1)S(1)}, bf16[8,256]{1,0:T(8,128)(2,1)S(1)}, u32[]{:S(2)}, u32[]{:S(2)}) collective-permute-start(bf16[8,256]{1,0:T(8,128)(2,1)S(1)} %convolution_convert_fusion.2), channel_id=1, source_target_pairs={{0,16},{8,24},{16,0},{24,8},{1,17},{9,25},{17,1},{25,9},{2,18},{10... | collective-permute-start | bytes 12296 | tf_op jit(solution)/shard_map/ppermute | solution.py:175
  51.3 2.8 %collective-permute-start.5 = (bf16[8,256]{1,0:T(8,128)(2,1)S(1)}, bf16[8,256]{1,0:T(8,128)(2,1)S(1)}, u32[]{:S(2)}, u32[]{:S(2)}) collective-permute-start(bf16[8,256]{1,0:T(8,128)(2,1)S(1)} %convolution_convert_fusion.2), channel_id=1, source_target_pairs={{0,24},{8,0},{16,8},{24,16},{1,25},{9,1},{17,9},{25,17},{2,26},{10... | collective-permute-start | bytes 12296 | tf_op jit(solution)/shard_map/ppermute | solution.py:175
  59.5 16.7 %all-to-all-start.3 = ((f32[8,32,256]{2,1,0:T(8,128)}), f32[8,32,256]{2,1,0:T(8,128)S(1)}, u32[]{:S(2)}, u32[]{:S(2)}) async-start(f32[8,32,256]{2,1,0:T(8,128)} %fusion.13), calls=%async_computation.3 | async-start | bytes 524288 | tf_op jit(solution)/shard_map/all_to_all | solution.py:262

commit v14 on v13

--- a/solution.py
+++ b/solution.py
@@ -102,9 +102,13 @@
     return hi, mid, lo
 
 
-def block_attention_kernel(block_len, limit_ref, q_ref, *refs):
+def block_attention_kernel(block_len, ring, meta_ref, q_ref, *refs):
     kv_refs, (out_ref, stats_ref) = refs[:-2], refs[-2:]
     blocks = len(kv_refs)
+    requests = meta_ref.shape[0] - 2
+    my_x = meta_ref[requests]
+    my_z = meta_ref[requests + 1]
+    length = meta_ref[my_x]
     rows = out_ref.shape[0]
     heads = stats_ref.shape[1] // 2
     score_scale = 1.0 / math.sqrt(HEAD_SIZE)
@@ -123,7 +127,9 @@
             )
             * score_scale
         )
-        valid = lax.broadcasted_iota(jnp.int32, s.shape, 1) < limit_ref[b]
+        source_x = (my_x - b + blocks) % blocks
+        limit = length - (source_x * ring + my_z) * block_len
+        valid = lax.broadcasted_iota(jnp.int32, s.shape, 1) < limit
         scores.append(jnp.where(valid, s, NEG_FLOOR))
         valids.append(valid)
     peak = jnp.max(scores[0], axis=1, keepdims=True)
@@ -151,13 +157,13 @@
         out_ref[:, width + j * 2 * heads : width + (j + 1) * 2 * heads] = part
 
 
-def block_attention(limit, group_rows, blocks_kv, width, block_len):
+def block_attention(meta, group_rows, blocks_kv, width, block_len, ring):
     rows = group_rows.shape[0]
     heads = width // HEAD_SIZE
     blocks = len(blocks_kv)
     vmem = pl.BlockSpec(memory_space=pltpu.VMEM)
     return pl.pallas_call(
-        functools.partial(block_attention_kernel, block_len),
+        functools.partial(block_attention_kernel, block_len, ring),
         out_shape=jax.ShapeDtypeStruct((rows, width + 6 * heads), jnp.bfloat16),
         in_specs=[pl.BlockSpec(memory_space=pltpu.SMEM), vmem] + [vmem] * blocks,
         out_specs=vmem,
@@ -167,7 +173,7 @@
             transcendentals=rows * heads * blocks * block_len,
             bytes_accessed=2 * (rows * width + 2 * blocks * block_len * HEAD_SIZE + rows * (width + 6 * heads)),
         ),
-    )(limit, group_rows, *blocks_kv)
+    )(meta, group_rows, *blocks_kv)
 
 
 def shifted(block, axis_name, shift):
@@ -235,9 +241,8 @@
     own_reach = lax.dynamic_slice_in_dim(reachable, node_start, rows_dev, 1)
     draft_usable = (own_reach > 0.5)[None, :, None, None, :, :]
     draft_part = partial_softmax(local_queries, tree_keys, tree_values, draft_usable, score_scale)
-    source_blocks = source_x * ring + my_z
-    limit = lengths[my_request] - source_blocks * block_len
-    packed_out = block_attention(limit, group_rows, blocks_kv, width_q, block_len)
+    meta = jnp.concatenate([lengths, jnp.stack([my_x, my_z]).astype(jnp.int32)])
+    packed_out = block_attention(meta, group_rows, blocks_kv, width_q, block_len, ring)
     head_count = width_q // HEAD_SIZE
     width_out = width_q
     moved = lax.all_to_all(

time: 78 us -> 76.8 us (0.985)
    sub x1 -> x0, other arithmetic: 1.19 us -> none  [on_device_body(): limit = lengths[my_request] - source_blocks * block_len]
  transfers between devices with their start and end apart: 10 -> 10, of which waited for: 5 -> 5; matrix products, arithmetic and copies ran while one was open for 13% -> 12% of each run, Pallas kernels for 0% -> 0%
where the time goes in v14:
time: 76.8 us; the launch traced here: 75.7 us
  starting transfers between devices  39.8 us (52%)
  waiting for transfers between devices  16.9 us (22%)
  matrix products  6.55 us (9%)
  local copies, waits for them, and re-layouts  5.93 us (8%)
  other arithmetic  3.14 us (4%)
  Pallas kernels  2.58 us (3%)
  between operations  0.84 us (1%)
    all_to_all x2, starting transfers between devices, gather_rows(): lax.all_to_all(spread, axis_name, split_axis=0, concat_axis=0, tiled=True)  13.2 us
    all_to_all x1, starting transfers between devices, on_device_body(): lax.all_to_all(partial.reshape(kv_count, out_rows, partial.shape[1]), 'kv...  10.2 us
    ppermute x6, starting transfers between devices, shifted(): lax.ppermute(block, axis_name, [(i, (i + shift) % count) for i in range(c...  9.61 us
    all_to_all x1, waiting for transfers between devices, on_device_body(): lax.all_to_all(packed_out.reshape(ring, rows_dev, -1), 'bz', split_axis=0...  6.82 us
    all_to_all x1, starting transfers between devices, on_device_body(): lax.all_to_all(packed_out.reshape(ring, rows_dev, -1), 'bz', split_axis=0...  6.77 us
    all_to_all x1, waiting for transfers between devices, on_device_body(): lax.all_to_all(partial.reshape(kv_count, out_rows, partial.shape[1]), 'kv...  5.54 us
    all_to_all x2, waiting for transfers between devices, gather_rows(): lax.all_to_all(spread, axis_name, split_axis=0, concat_axis=0, tiled=True)  2.9 us
    pallas_call x1, Pallas kernels, block_attention(): pl.pallas_call(functools.partial(block_attention_kernel, block_len, ring)...  2.58 us
  transfers between devices with their start and end apart: 10, of which 5 were waited for; matrix products, arithmetic and copies ran while one was open for 12% of the time, Pallas kernels for 0%

profile of v14, /device:TPU:1, one launch (start us, length us, event | category | flops | bytes accessed | tf_op | source)
XLA Modules:
  0.0 75.7 jit_solution(16135234897194911262)
XLA Ops:
  0.6 0.8 %pad_maximum_fusion = bf16[8,1280]{1,0:T(8,128)(2,1)S(1)} fusion(bf16[8,128]{1,0:T(8,128)(2,1)} %param.12, bf16[8,128]{1,0:T(8,128)(2,1)} %param.11, bf16[8,1024]{1,0:T(8,128)(2,1)} %param.10), kind=kLoop, calls=%fused_computation.56 | loop fusion | flops 61440 | bytes 40960 | tf_op jit(solution)/shard_map/concatenate | solution.py:219
  1.5 0.7 broadcast_in_dim.30
  2.1 9.1 %all-to-all-start = ((bf16[8,8,1280]{2,1,0:T(8,128)(2,1)}), bf16[8,8,1280]{2,1,0:T(8,128)(2,1)S(1)}, u32[]{:S(2)}, u32[]{:S(2)}) async-start(bf16[8,8,1280]{2,1,0:T(8,128)(2,1)} %broadcast_in_dim.30), calls=%async_computation | async-start | bytes 327680 | tf_op jit(solution)/shard_map/all_to_all | solution.py:187
  11.4 0.6 slice_bitcast_fusion
  12.1 1.2 %collective-permute-start = (bf16[128,256]{1,0:T(8,128)(2,1)S(1)}, bf16[128,256]{1,0:T(8,128)(2,1)S(1)}, u32[]{:S(2)}, u32[]{:S(2)}) collective-permute-start(bf16[128,256]{1,0:T(8,128)(2,1)S(1)} %get-tuple-element.9), channel_id=1, source_target_pairs={{0,8},{8,16},{16,24},{24,0},{1,9},{9,17},{17,25},{25,1},{2,10},{10... | collective-permute-start | bytes 196616 | tf_op jit(solution)/shard_map/ppermute | solution.py:181
  13.3 2.5 %collective-permute-start.1 = (bf16[128,256]{1,0:T(8,128)(2,1)S(1)}, bf16[128,256]{1,0:T(8,128)(2,1)S(1)}, u32[]{:S(2)}, u32[]{:S(2)}) collective-permute-start(bf16[128,256]{1,0:T(8,128)(2,1)S(1)} %get-tuple-element.8), channel_id=1, source_target_pairs={{0,16},{8,24},{16,0},{24,8},{1,17},{9,25},{17,1},{25,9},{2,18},{10... | collective-permute-start | bytes 196616 | tf_op jit(solution)/shard_map/ppermute | solution.py:181
  15.8 1.2 %collective-permute-start.2 = (bf16[128,256]{1,0:T(8,128)(2,1)S(1)}, bf16[128,256]{1,0:T(8,128)(2,1)S(1)}, u32[]{:S(2)}, u32[]{:S(2)}) collective-permute-start(bf16[128,256]{1,0:T(8,128)(2,1)S(1)} %get-tuple-element.7), channel_id=1, source_target_pairs={{0,24},{8,0},{16,8},{24,16},{1,25},{9,1},{17,9},{25,17},{2,26},{10... | collective-permute-start | bytes 196616 | tf_op jit(solution)/shard_map/ppermute | solution.py:181
  16.9 0.7 fusion.45
  18.9 0.7 fusion.46
  19.6 0.6 copy-done.8
  20.3 0.6 pad_add_fusion.meta_ref
  20.9 0.6 copy-done.5
  21.6 2.6 %shard_map.121 = bf16[64,1072]{1,0:T(8,128)(2,1)} custom-call(s32[6]{0:T(128)} %pad_add_fusion.meta_ref, bf16[64,1280]{1,0:T(8,128)(2,1)} %bitcast.98, bf16[128,256]{1,0:T(8,128)(2,1)} %get-tuple-element.10.refs_0_, bf16[128,256]{1,0:T(8,128)(2,1)} %copy-done.5, bf16[128,256]{1,0:T(8,128)(2,1)} %copy-done.6, bf16[128,256]{1,0:T(8,128)(2,1)} %copy-done.7), custom_call_target="tpu_custom_call" | custom-call | flops 134217728 | bytes 530432 | tf_op jit(solution)/shard_map/pallas_call | solution.py:165
  24.2 6.8 %all-to-all-start.1 = ((bf16[8,8,1072]{2,1,0:T(8,128)(2,1)}), bf16[8,8,1072]{2,1,0:T(8,128)(2,1)S(1)}, u32[]{:S(2)}, u32[]{:S(2)}) async-start(bf16[8,8,1072]{2,1,0:T(8,128)(2,1)} %bitcast.102), calls=%async_computation.1 | async-start | bytes 294912 | tf_op jit(solution)/shard_map/all_to_all | solution.py:248
  31.0 0.9 %fusion.48 = (f32[8,8]{0,1:T(8,128)S(1)}, f32[1,1,1,8,8,64]{5,3,4,0,2,1:T(8,128)S(1)}) fusion(bf16[8,8,128]{2,0,1:T(8,128)(2,1)S(1)} %bitcast.103, bf16[64,1280]{1,0:T(8,128)(2,1)} %bitcast.99, pred[8,64]{1,0:T(8,128)(4,1)S(1)} %fusion.39), kind=kOutput, calls=%fused_computation.99 | convolution fusion | flops 1060800 | bytes 49920 | tf_op jit(solution)/shard_map/rtkgh,rbpkh->brkgtp/dot_general | solution.py:35
  32.3 6.8 %all-to-all-done.1 = bf16[8,8,1072]{2,1,0:T(8,128)(2,1)S(1)} async-done(((bf16[8,8,1072]{2,1,0:T(8,128)(2,1)}), bf16[8,8,1072]{2,1,0:T(8,128)(2,1)S(1)}, u32[]{:S(2)}, u32[]{:S(2)}) %all-to-all-start.1) | async-done | bytes 137248 | tf_op jit(solution)/shard_map/all_to_all | solution.py:248
  39.7 0.8 %fusion.11 = bf16[8,1024]{1,0:T(8,128)(2,1)S(1)} fusion(f32[8,1024]{1,0:T(8,128)S(1)} %fusion.18, bf16[64,1280]{1,0:T(8,128)(2,1)} %bitcast.100, bf16[8,8,64]{2,0,1:T(8,128)(2,1)S(1)} %get-tuple-element.12, f32[8,8]{0,1:T(8,128)S(1)} %copy.29, f32[8,8]{0,1:T(8,128)S(1)} %copy.25), kind=kOutput, calls=%fused_computation.21 | convolution fusion | flops 1081344 | bytes 74240 | tf_op jit(solution)/shard_map/brkgtp,rbpkh->brtkgh/dot_general | solution.py:44
  40.6 0.9 %broadcast_in_dim.34 = bf16[32,8,1024]{2,1,0:T(8,128)(2,1)} broadcast(bf16[8,1024]{1,0:T(8,128)(2,1)S(1)} %fusion.11), dimensions={1,2} | broadcast | bytes 540672 | tf_op jit(solution)/shard_map/broadcast_in_dim | solution.py:186
  41.4 4.0 %all-to-all-start.2 = ((bf16[32,8,1024]{2,1,0:T(8,128)(2,1)}), bf16[32,8,1024]{2,1,0:T(8,128)(2,1)S(1)}, u32[]{:S(2)}, u32[]{:S(2)}) async-start(bf16[32,8,1024]{2,1,0:T(8,128)(2,1)} %broadcast_in_dim.34), calls=%async_computation.2 | async-start | bytes 1048576 | tf_op jit(solution)/shard_map/all_to_all | solution.py:187
  45.5 0.9 %convolution_convert_fusion.2 = bf16[8,256]{1,0:T(8,128)(2,1)S(1)} fusion(bf16[64,1280]{1,0:T(8,128)(2,1)} %bitcast.101, s32[8]{0:T(128)S(1)} %fusion.46), kind=kOutput, calls=%fused_computation.23 | convolution fusion | flops 264704 | bytes 36896 | tf_op jit(solution)/shard_map/dot_general | solution.py:224
  46.5 1.2 %collective-permute-start.3 = (bf16[8,256]{1,0:T(8,128)(2,1)S(1)}, bf16[8,256]{1,0:T(8,128)(2,1)S(1)}, u32[]{:S(2)}, u32[]{:S(2)}) collective-permute-start(bf16[8,256]{1,0:T(8,128)(2,1)S(1)} %convolution_convert_fusion.2), channel_id=1, source_target_pairs={{0,8},{8,16},{16,24},{24,0},{1,9},{9,17},{17,25},{25,1},{2,10},{10... | collective-permute-start | bytes 12296 | tf_op jit(solution)/shard_map/ppermute | solution.py:181
  47.7 2.5 %collective-permute-start.4 = (bf16[8,256]{1,0:T(8,128)(2,1)S(1)}, bf16[8,256]{1,0:T(8,128)(2,1)S(1)}, u32[]{:S(2)}, u32[]{:S(2)}) collective-permute-start(bf16[8,256]{1,0:T(8,128)(2,1)S(1)} %convolution_convert_fusion.2), channel_id=1, source_target_pairs={{0,16},{8,24},{16,0},{24,8},{1,17},{9,25},{17,1},{25,9},{2,18},{10... | collective-permute-start | bytes 12296 | tf_op jit(solution)/shard_map/ppermute | solution.py:181
  50.2 1.1 %collective-permute-start.5 = (bf16[8,256]{1,0:T(8,128)(2,1)S(1)}, bf16[8,256]{1,0:T(8,128)(2,1)S(1)}, u32[]{:S(2)}, u32[]{:S(2)}) collective-permute-start(bf16[8,256]{1,0:T(8,128)(2,1)S(1)} %convolution_convert_fusion.2), channel_id=1, source_target_pairs={{0,24},{8,0},{16,8},{24,16},{1,25},{9,1},{17,9},{25,17},{2,26},{10... | collective-permute-start | bytes 12296 | tf_op jit(solution)/shard_map/ppermute | solution.py:181
  51.3 0.6 collective-permute-done.4
  51.9 1.0 %collective-permute-done.5 = bf16[8,256]{1,0:T(8,128)(2,1)S(1)} collective-permute-done((bf16[8,256]{1,0:T(8,128)(2,1)S(1)}, bf16[8,256]{1,0:T(8,128)(2,1)S(1)}, u32[]{:S(2)}, u32[]{:S(2)}) %collective-permute-start.5) | collective-permute-done | bytes 4128 | tf_op jit(solution)/shard_map/ppermute | solution.py:181
  53.5 0.9 %fusion = bf16[4,128,128]{2,1,0:T(8,128)(2,1)} fusion(bf16[4,128,128]{2,1,0:T(8,128)(2,1)S(1)} %copy-done.2, pred[4,128]{1,0:T(4,128)(4,1)S(1)} %compare_and_fusion, bf16[4,8,256]{2,1,0:T(8,128)(2,1)S(1)} %fusion.26, s32[4,128]{1,0:T(4,128)S(1)} %broadcast_subtract_fusion), kind=kOutput, calls=%fused_computation.3 | convolution fusion | flops 1187840 | bytes 273408 | tf_op jit(solution)/shard_map/rps,rsc->rpc/dot_general | solution.py:91
  54.5 2.9 %all-to-all-done.2 = bf16[32,8,1024]{2,1,0:T(8,128)(2,1)S(1)} async-done(((bf16[32,8,1024]{2,1,0:T(8,128)(2,1)}), bf16[32,8,1024]{2,1,0:T(8,128)(2,1)S(1)}, u32[]{:S(2)}, u32[]{:S(2)}) %all-to-all-start.2) | async-done | bytes 524320 | tf_op jit(solution)/shard_map/all_to_all | solution.py:187
  57.4 1.0 %fusion.13 = f32[8,32,256]{2,1,0:T(8,128)} fusion(bf16[8,32,1024]{2,1,0:T(8,128)(2,1)S(1)} %bitcast.97, bf16[1024,256]{1,0:T(8,128)(2,1)S(1)} %copy-done), kind=kOutput, calls=%fused_computation.28 | convolution fusion | flops 134217728 | bytes 1310720 | tf_op jit(solution)/shard_map/dot_general | solution.py:265
  58.4 10.2 %all-to-all-start.3 = ((f32[8,32,256]{2,1,0:T(8,128)}), f32[8,32,256]{2,1,0:T(8,128)S(1)}, u32[]{:S(2)}, u32[]{:S(2)}) async-start(f32[8,32,256]{2,1,0:T(8,128)} %fusion.13), calls=%async_computation.3 | async-start | bytes 524288 | tf_op jit(solution)/shard_map/all_to_all | solution.py:267
  68.6 0.9 %fusion.1 = bf16[4,128,128]{2,1,0:T(8,128)(2,1)} fusion(bf16[4,128,128]{2,1,0:T(8,128)(2,1)S(1)} %copy-done.3, pred[4,128]{1,0:T(4,128)(4,1)S(1)} %compare_and_fusion, bf16[4,8,256]{2,1,0:T(8,128)(2,1)S(1)} %fusion.26, s32[4,128]{1,0:T(4,128)S(1)} %broadcast_subtract_fusion), kind=kOutput, calls=%fused_computation.4 | convolution fusion | flops 1187840 | bytes 273408 | tf_op jit(solution)/shard_map/rps,rsc->rpc/dot_general | solution.py:91
  69.5 5.5 %all-to-all-done.3 = f32[8,32,256]{2,1,0:T(8,128)S(1)} async-done(((f32[8,32,256]{2,1,0:T(8,128)}), f32[8,32,256]{2,1,0:T(8,128)S(1)}, u32[]{:S(2)}, u32[]{:S(2)}) %all-to-all-start.3) | async-done | bytes 262176 | tf_op jit(solution)/shard_map/all_to_all | solution.py:267
  75.1 0.6 reduce_sum.42
  (55 shorter events, 3.2 us)
Async XLA Ops:
  0.6 56.7 %copy-start = (bf16[1024,256]{1,0:T(8,128)(2,1)S(1)}, bf16[1024,256]{1,0:T(8,128)(2,1)}, u32[]{:S(2)}) copy-start(bf16[1024,256]{1,0:T(8,128)(2,1)} %param.15) | copy-start | bytes 1572868
  2.1 9.1 %copy-start.2 = (bf16[4,128,128]{2,1,0:T(8,128)(2,1)S(1)}, bf16[4,128,128]{2,1,0:T(8,128)(2,1)}, u32[]{:S(2)}) copy-start(bf16[4,128,128]{2,1,0:T(8,128)(2,1)} %param.13) | copy-start | bytes 393220
  2.1 9.1 %copy-start.3 = (bf16[4,128,128]{2,1,0:T(8,128)(2,1)S(1)}, bf16[4,128,128]{2,1,0:T(8,128)(2,1)}, u32[]{:S(2)}) copy-start(bf16[4,128,128]{2,1,0:T(8,128)(2,1)} %param.14) | copy-start | bytes 393220
  2.1 18.8 %all-to-all-start = ((bf16[8,8,1280]{2,1,0:T(8,128)(2,1)}), bf16[8,8,1280]{2,1,0:T(8,128)(2,1)S(1)}, u32[]{:S(2)}, u32[]{:S(2)}) async-start(bf16[8,8,1280]{2,1,0:T(8,128)(2,1)} %broadcast_in_dim.30), calls=%async_computation | async-start | bytes 327680 | tf_op jit(solution)/shard_map/all_to_all | solution.py:187
  12.1 8.8 %collective-permute-start = (bf16[128,256]{1,0:T(8,128)(2,1)S(1)}, bf16[128,256]{1,0:T(8,128)(2,1)S(1)}, u32[]{:S(2)}, u32[]{:S(2)}) collective-permute-start(bf16[128,256]{1,0:T(8,128)(2,1)S(1)} %get-tuple-element.9), channel_id=1, source_target_pairs={{0,8},{8,16},{16,24},{24,0},{1,9},{9,17},{17,25},{25,1},{2,10},{10... | collective-permute-start | bytes 196616 | tf_op jit(solution)/shard_map/ppermute | solution.py:181
  13.3 7.6 %collective-permute-start.1 = (bf16[128,256]{1,0:T(8,128)(2,1)S(1)}, bf16[128,256]{1,0:T(8,128)(2,1)S(1)}, u32[]{:S(2)}, u32[]{:S(2)}) collective-permute-start(bf16[128,256]{1,0:T(8,128)(2,1)S(1)} %get-tuple-element.8), channel_id=1, source_target_pairs={{0,16},{8,24},{16,0},{24,8},{1,17},{9,25},{17,1},{25,9},{2,18},{10... | collective-permute-start | bytes 196616 | tf_op jit(solution)/shard_map/ppermute | solution.py:181
  15.8 5.2 %collective-permute-start.2 = (bf16[128,256]{1,0:T(8,128)(2,1)S(1)}, bf16[128,256]{1,0:T(8,128)(2,1)S(1)}, u32[]{:S(2)}, u32[]{:S(2)}) collective-permute-start(bf16[128,256]{1,0:T(8,128)(2,1)S(1)} %get-tuple-element.7), channel_id=1, source_target_pairs={{0,24},{8,0},{16,8},{24,16},{1,25},{9,1},{17,9},{25,17},{2,26},{10... | collective-permute-start | bytes 196616 | tf_op jit(solution)/shard_map/ppermute | solution.py:181
  19.5 0.7 copy-start.8
  20.9 0.6 copy-start.5
  20.9 0.6 copy-start.6
  20.9 0.6 copy-start.7
  20.9 0.7 copy-start.1
  24.2 6.8 %copy-start.4 = (bf16[8,1024]{1,0:T(8,128)(2,1)S(1)}, bf16[8,1024]{1,0:T(8,128)(2,1)}, u32[]{:S(2)}) copy-start(bf16[8,1024]{1,0:T(8,128)(2,1)} %param.10) | copy-start | bytes 49156
  24.2 15.0 %all-to-all-start.1 = ((bf16[8,8,1072]{2,1,0:T(8,128)(2,1)}), bf16[8,8,1072]{2,1,0:T(8,128)(2,1)S(1)}, u32[]{:S(2)}, u32[]{:S(2)}) async-start(bf16[8,8,1072]{2,1,0:T(8,128)(2,1)} %bitcast.102), calls=%async_computation.1 | async-start | bytes 294912 | tf_op jit(solution)/shard_map/all_to_all | solution.py:248
  41.4 4.0 %copy-start.9 = (s32[4]{0:T(128)S(1)}, s32[4]{0:T(128)}, u32[]{:S(2)}) copy-start(s32[4]{0:T(128)} %param.19) | copy-start | bytes 52
  41.4 15.9 %all-to-all-start.2 = ((bf16[32,8,1024]{2,1,0:T(8,128)(2,1)}), bf16[32,8,1024]{2,1,0:T(8,128)(2,1)S(1)}, u32[]{:S(2)}, u32[]{:S(2)}) async-start(bf16[32,8,1024]{2,1,0:T(8,128)(2,1)} %broadcast_in_dim.34), calls=%async_computation.2 | async-start | bytes 1048576 | tf_op jit(solution)/shard_map/all_to_all | solution.py:187
  46.5 4.8 %collective-permute-start.3 = (bf16[8,256]{1,0:T(8,128)(2,1)S(1)}, bf16[8,256]{1,0:T(8,128)(2,1)S(1)}, u32[]{:S(2)}, u32[]{:S(2)}) collective-permute-start(bf16[8,256]{1,0:T(8,128)(2,1)S(1)} %convolution_convert_fusion.2), channel_id=1, source_target_pairs={{0,8},{8,16},{16,24},{24,0},{1,9},{9,17},{17,25},{25,1},{2,10},{10... | collective-permute-start | bytes 12296 | tf_op jit(solution)/shard_map/ppermute | solution.py:181
  47.7 4.3 %collective-permute-start.4 = (bf16[8,256]{1,0:T(8,128)(2,1)S(1)}, bf16[8,256]{1,0:T(8,128)(2,1)S(1)}, u32[]{:S(2)}, u32[]{:S(2)}) collective-permute-start(bf16[8,256]{1,0:T(8,128)(2,1)S(1)} %convolution_convert_fusion.2), channel_id=1, source_target_pairs={{0,16},{8,24},{16,0},{24,8},{1,17},{9,25},{17,1},{25,9},{2,18},{10... | collective-permute-start | bytes 12296 | tf_op jit(solution)/shard_map/ppermute | solution.py:181
  50.2 2.8 %collective-permute-start.5 = (bf16[8,256]{1,0:T(8,128)(2,1)S(1)}, bf16[8,256]{1,0:T(8,128)(2,1)S(1)}, u32[]{:S(2)}, u32[]{:S(2)}) collective-permute-start(bf16[8,256]{1,0:T(8,128)(2,1)S(1)} %convolution_convert_fusion.2), channel_id=1, source_target_pairs={{0,24},{8,0},{16,8},{24,16},{1,25},{9,1},{17,9},{25,17},{2,26},{10... | collective-permute-start | bytes 12296 | tf_op jit(solution)/shard_map/ppermute | solution.py:181
  58.4 16.7 %all-to-all-start.3 = ((f32[8,32,256]{2,1,0:T(8,128)}), f32[8,32,256]{2,1,0:T(8,128)S(1)}, u32[]{:S(2)}, u32[]{:S(2)}) async-start(f32[8,32,256]{2,1,0:T(8,128)} %fusion.13), calls=%async_computation.3 | async-start | bytes 524288 | tf_op jit(solution)/shard_map/all_to_all | solution.py:267
